TPU v7x, 256 devices: a whole 4x4x8 slice. The times are simulated.
256 devices in a mesh: attn: 32 (over z, y), expert: 4 (over x), rep: 2 (over core).
Axes of the slice: x: 4, y: 4, z: 8, core: 2. Of those that a mesh axis runs over, the one named last changes fastest.
Arguments:
- queries: bfloat16 [256, 73728], P('attn', ('expert', 'rep')), may hold values from -120 to 120
- new_latent: bfloat16 [256, 576], P('attn'), may hold values from -6 to 6
- cache_pool: bfloat16 [16384, 576], P('attn'), may hold values from -6 to 6
- local_len: int32 [32, 4], P('attn'), may hold values from 1 to 384, 512 in all within a row
- spill_cache: bfloat16 [1024, 16, 576], P('attn'), may hold values from -6 to 6
- spill_owner: int32 [1024], replicated, may hold values from -1 to 127, as said below
- w_uv: bfloat16 [128, 512, 128], P(('expert', 'rep')), may hold values from -0.25 to 0.25
- w_o: bfloat16 [16384, 7168], P(('expert', 'rep'), 'attn'), may hold values from -0.046875 to 0.046875
- residual: bfloat16 [256, 7168], P(None, 'attn'), may hold values from -3 to 3
- norm_gain: float32 [7168], replicated, may hold values from 0.5 to 1.5
- route_ids: int32 [256, 4], replicated, may hold values from 0 to 15, all different within a row; in each aligned block of 128 rows (0 to 127, 128 to 255, ...) at most 40 rows name the same one
- route_scores: float32 [256, 4], replicated, may hold values from 0.05 to 1
- w_gate: bfloat16 [7168, 32768], P(None, ('attn', 'expert')), may hold values from -0.0625 to 0.0625
- w_up: bfloat16 [7168, 32768], P(None, ('attn', 'expert')), may hold values from -0.0625 to 0.0625
- w_down: bfloat16 [32768, 7168], P(('attn', 'expert')), may hold values from -0.125 to 0.125
Outputs:
- mixed: bfloat16 [256, 7168], P('rep', ('attn', 'expert'))
Inputs may be any that keep to these rules, and one draw needn't show every extreme that they name: Each row of local_len sums to 512. `spill_owner`: each entry is -1 or the number of a request that lives on another index of attn than the block's slot. The slots of one index of attn hold at most 2 blocks of the requests of any one other index, and some index holds exactly 2 for some other index in every draw. `route_ids`: the token rows fall into 2 aligned blocks of 128 rows in order (2 being the size of rep); in each block no expert is named by more than 40 rows, and in some block one is named by exactly 40.
All inputs are finite; a program needn't handle non-finite values.
Results may differ from a plain program's by a relative error of at most 0.025.
Values may be sent and summed in bfloat16 or wider, within the bound.
No kernel may reach another device: no remote copies, remote signals or barrier semaphores. Data moves between devices by JAX's collectives and lax.ppermute only.
A program may use at most 128 MiB of HBM per device.

v0:
```python
import jax
import jax.numpy as jnp
from jax import lax
from jax.sharding import PartitionSpec as P

ROPE = 64
VH = 128
EXPERTS = 16
TOP = 4
MAXLOC = 384
CAP = 2


floor_score = -1e30
scale_out = 2.5


def expert_tables(route_ids, part_index, part_count, capacity):
    row_count = route_ids.shape[0] // part_count
    route_part = lax.dynamic_slice_in_dim(route_ids, part_index * row_count, row_count, 0)
    member = jnp.any(
        route_part[:, :, None] == jnp.arange(EXPERTS, dtype=jnp.int32)[None, None, :], axis=1
    )
    order_rank = jnp.cumsum(member.astype(jnp.int32), axis=0) - 1
    slot_ids = jnp.arange(capacity, dtype=jnp.int32)
    slot_hit = member[None, :, :] & (order_rank[None, :, :] == slot_ids[:, None, None])
    place_ids = jnp.arange(row_count, dtype=jnp.int32)
    slot_token = jnp.sum(jnp.where(slot_hit, place_ids[None, :, None], 0), axis=1)
    filled = jnp.any(slot_hit, axis=1)
    return (slot_token.T, filled.T, route_part)


def per_device(
    queries,
    new_latent,
    cache_pool,
    local_len,
    spill_cache,
    spill_owner,
    w_uv,
    w_o,
    residual,
    norm_gain,
    route_ids,
    route_scores,
    w_gate,
    w_up,
    w_down,
):
    n_attn = lax.axis_size("attn")
    n_expert = lax.axis_size("expert")
    n_rep = lax.axis_size("rep")
    attn_here = lax.axis_index("attn")
    expert_here = lax.axis_index("expert")
    rep_here = lax.axis_index("rep")
    req_count = local_len.shape[1]
    head_count = w_uv.shape[0]
    row_width = new_latent.shape[1]
    lat_width = w_uv.shape[1]
    score_scale = float(VH + ROPE) ** (-0.5)
    query_rows = queries.reshape(req_count, 2, head_count, row_width)
    lengths = local_len[0]
    starts = jnp.cumsum(lengths) - lengths
    padded = jnp.concatenate([cache_pool, jnp.zeros((MAXLOC, row_width), cache_pool.dtype)], axis=0)
    windows = jax.vmap(lambda start_one: lax.dynamic_slice_in_dim(padded, start_one, MAXLOC, 0))(
        starts
    )
    local_scores = (
        jnp.einsum("rthc,rkc->rthk", query_rows, windows, preferred_element_type=jnp.float32)
        * score_scale
    )
    inside = jnp.arange(MAXLOC)[None, :] < lengths[:, None]
    local_scores = jnp.where(inside[:, None, None, :], local_scores, floor_score)
    fresh_keys = new_latent.reshape(req_count, 2, row_width)
    fresh_scores = (
        jnp.einsum("rthc,rkc->rthk", query_rows, fresh_keys, preferred_element_type=jnp.float32)
        * score_scale
    )
    causal = jnp.arange(2)[None, :] <= jnp.arange(2)[:, None]
    fresh_scores = jnp.where(causal[None, :, None, :], fresh_scores, floor_score)
    spill_count = spill_cache.shape[0]
    directory = spill_owner.reshape(n_attn, spill_count)
    owner_dev = jnp.where(directory >= 0, directory // req_count, -1)
    earlier = jnp.arange(spill_count)[:, None] > jnp.arange(spill_count)[None, :]
    same_owner = owner_dev[:, :, None] == owner_dev[:, None, :]
    order_rank = jnp.sum(same_owner & earlier[None, :, :], axis=2)
    slot_ids = jnp.arange(CAP)
    own_row = owner_dev[attn_here]
    own_rank = order_rank[attn_here]
    pick_slot = (own_row[None, None, :] == jnp.arange(n_attn)[:, None, None]) & (
        own_rank[None, None, :] == slot_ids[None, :, None]
    )
    outgoing = jnp.einsum(
        "dks,sbc->dkbc",
        pick_slot.astype(jnp.bfloat16),
        spill_cache,
        preferred_element_type=jnp.float32,
    ).astype(jnp.bfloat16)
    incoming = lax.all_to_all(outgoing, "attn", split_axis=0, concat_axis=0, tiled=True)
    mine_slot = (owner_dev[:, None, :] == attn_here) & (
        order_rank[:, None, :] == slot_ids[None, :, None]
    )
    present = jnp.any(mine_slot, axis=2).reshape(-1)
    request = jnp.sum(
        jnp.where(mine_slot, directory[:, None, :] - attn_here * req_count, 0), axis=2
    ).reshape(-1)
    blocks = incoming.reshape(n_attn * CAP, incoming.shape[2], row_width)
    slot_query = jnp.take(query_rows, request, axis=0)
    spill_scores = (
        jnp.einsum("nthc,nbc->nthb", slot_query, blocks, preferred_element_type=jnp.float32)
        * score_scale
    )
    spill_scores = jnp.where(present[:, None, None, None], spill_scores, floor_score)
    belong = (request[None, :] == jnp.arange(req_count)[:, None]) & present[None, :]
    spill_top = jnp.max(
        jnp.where(belong[:, :, None, None], jnp.max(spill_scores, axis=3)[None], floor_score),
        axis=1,
    )
    row_top = jnp.maximum(
        jnp.maximum(jnp.max(local_scores, axis=3), jnp.max(fresh_scores, axis=3)), spill_top
    )
    local_weight = jnp.exp(local_scores - row_top[..., None])
    fresh_weight = jnp.exp(fresh_scores - row_top[..., None])
    spill_weight = jnp.exp(spill_scores - jnp.take(row_top, request, axis=0)[..., None])
    spill_weight = jnp.where(present[:, None, None, None], spill_weight, 0.0)
    belong_f = belong.astype(jnp.float32)
    denominator = jnp.sum(local_weight, axis=3) + jnp.sum(fresh_weight, axis=3)
    denominator = denominator + jnp.einsum(
        "rn,nth->rth", belong_f, jnp.sum(spill_weight, axis=3), precision=lax.Precision.HIGHEST
    )
    numerator = jnp.einsum(
        "rthk,rkc->rthc",
        local_weight.astype(jnp.bfloat16),
        windows[:, :, :lat_width],
        preferred_element_type=jnp.float32,
    )
    numerator = numerator + jnp.einsum(
        "rthk,rkc->rthc",
        fresh_weight.astype(jnp.bfloat16),
        fresh_keys[:, :, :lat_width],
        preferred_element_type=jnp.float32,
    )
    spill_numer = jnp.einsum(
        "nthb,nbc->nthc",
        spill_weight.astype(jnp.bfloat16),
        blocks[:, :, :lat_width],
        preferred_element_type=jnp.float32,
    )
    numerator = numerator + jnp.einsum(
        "rn,nthc->rthc", belong_f, spill_numer, precision=lax.Precision.HIGHEST
    )
    attended = (numerator / denominator[..., None]).astype(jnp.bfloat16)
    values = jnp.einsum(
        "rthc,hcv->rthv", attended, w_uv, preferred_element_type=jnp.float32
    ).astype(jnp.bfloat16)
    values = values.reshape(2 * req_count, head_count * w_uv.shape[2])
    partial_cols = jnp.dot(
        lax.all_gather(values, "attn", axis=0, tiled=True), w_o, preferred_element_type=jnp.float32
    )
    attn_cols = lax.psum(partial_cols.astype(jnp.bfloat16), ("expert", "rep")).astype(jnp.float32)
    hidden_cols = (residual.astype(jnp.float32) + attn_cols).astype(jnp.bfloat16)
    rows_part = route_ids.shape[0] // n_rep
    capacity = rows_part * TOP // EXPERTS * 5 // 4
    shards = n_attn * n_expert // EXPERTS
    slot_token, filled, route_part = expert_tables(route_ids, rep_here, n_rep, capacity)
    part_cols = lax.dynamic_slice_in_dim(hidden_cols, rep_here * rows_part, rows_part, 0)
    dest_expert = (jnp.arange(n_attn) * n_expert + expert_here) // shards
    send_rows = jnp.take(slot_token, dest_expert, axis=0)
    send_ok = jnp.take(filled, dest_expert, axis=0)
    outgoing_rows = jnp.where(
        send_ok[:, :, None], jnp.take(part_cols, send_rows, axis=0), jnp.zeros((), jnp.bfloat16)
    )
    outgoing_rows = outgoing_rows[:, :, None, :]
    received = lax.all_to_all(outgoing_rows, "attn", split_axis=0, concat_axis=2, tiled=True)
    item_count = received.shape[1]
    full_rows = received.reshape(item_count, -1)
    widened = full_rows.astype(jnp.float32)
    normed = (
        widened * lax.rsqrt(jnp.mean(widened * widened, axis=1, keepdims=True) + 1e-06) * norm_gain
    ).astype(jnp.bfloat16)
    gate_proj = jnp.dot(normed, w_gate, preferred_element_type=jnp.float32)
    up_proj = jnp.dot(normed, w_up, preferred_element_type=jnp.float32)
    activated = (jax.nn.silu(gate_proj) * up_proj).astype(jnp.bfloat16)
    result = jnp.dot(activated, w_down, preferred_element_type=jnp.float32)
    returned_block = lax.all_to_all(
        result.reshape(1, item_count, n_attn * n_expert, -1).astype(jnp.bfloat16),
        ("attn", "expert"),
        split_axis=2,
        concat_axis=0,
        tiled=True,
    ).astype(jnp.float32)
    returned = returned_block.reshape(n_attn * n_expert, item_count, -1)
    share_part = lax.dynamic_slice_in_dim(route_scores, rep_here * rows_part, rows_part, 0)
    share_part = share_part / jnp.sum(share_part, axis=1, keepdims=True)
    share_table = jnp.sum(
        jnp.where(
            route_part[:, :, None] == jnp.arange(EXPERTS, dtype=jnp.int32)[None, None, :],
            share_part[:, :, None],
            0.0,
        ),
        axis=1,
    )
    source_expert = jnp.arange(n_attn * n_expert) // shards
    back_rows = jnp.take(slot_token, source_expert, axis=0)
    back_ok = jnp.take(filled, source_expert, axis=0)
    weight_coef = (
        jnp.where(back_ok, share_table[back_rows, source_expert[:, None]], 0.0) * scale_out
    )
    sub_cols = returned.shape[2]
    weighted = (weight_coef[:, :, None] * returned).reshape(-1, sub_cols)
    routed = jax.ops.segment_sum(weighted, back_rows.reshape(-1), num_segments=rows_part)
    own_cols = lax.dynamic_slice_in_dim(part_cols, expert_here * sub_cols, sub_cols, 1)
    return (own_cols.astype(jnp.float32) + routed).astype(jnp.bfloat16)


def solution(mesh):
    return jax.shard_map(
        per_device,
        mesh=mesh,
        in_specs=(
            P("attn", ("expert", "rep")),
            P("attn", None),
            P("attn", None),
            P("attn", None),
            P("attn", None, None),
            P(),
            P(("expert", "rep"), None, None),
            P(("expert", "rep"), "attn"),
            P(None, "attn"),
            P(),
            P(),
            P(),
            P(None, ("attn", "expert")),
            P(None, ("attn", "expert")),
            P(("attn", "expert"), None),
        ),
        out_specs=P("rep", ("attn", "expert")),
        check_vma=False,
    )
```

profile of v0, /device:TPU:2, one launch (start us, length us, event | category | flops | bytes accessed | tf_op | source)
XLA Modules:
  0.0 362.0 jit_solution(18145144369421537697)
XLA Ops:
  11.4 11.7 %all-to-all-start = ((bf16[32,2,16,576]{3,2,1,0:T(8,128)(2,1)}), bf16[32,2,16,576]{3,2,1,0:T(8,128)(2,1)}, u32[]{:S(2)}, u32[]{:S(2)}) async-start(bf16[32,2,16,576]{3,2,1,0:T(8,128)(2,1)} %copy.175), calls=%async_computation | async-start | bytes 2621440 | tf_op jit(solution)/shard_map/all_to_all | solution.py:99
  25.7 2.4 gather_fusion
  29.7 8.1 %while.1 = (s32[]{:T(128)}, bf16[896,576]{1,0:T(8,128)(2,1)S(1)}, s32[4,2]{0,1:T(2,128)S(1)}, bf16[4,384,576]{2,1,0:T(8,128)(2,1)}, s32[]{:T(128)}) while((s32[]{:T(128)}, bf16[896,576]{1,0:T(8,128)(2,1)S(1)}, s32[4,2]{0,1:T(2,128)S(1)}, bf16[4,384,576]{2,1,0:T(8,128)(2,1)}, s32[]{:T(128)}) %tuple.22), condition=%wide.while_cond, body=%wide.while_body.sunk | while | flops 2 | bytes 935001 | solution.py:65
  37.8 3.0 fusion.93
  40.8 16.0 %all-to-all-done = bf16[32,2,16,576]{3,2,1,0:T(8,128)(2,1)} async-done(((bf16[32,2,16,576]{3,2,1,0:T(8,128)(2,1)}), bf16[32,2,16,576]{3,2,1,0:T(8,128)(2,1)}, u32[]{:S(2)}, u32[]{:S(2)}) %all-to-all-start) | async-done | bytes 1179680 | tf_op jit(solution)/shard_map/all_to_all | solution.py:99
  56.7 6.0 %fusion.2 = f32[64,2,16,16]{2,3,1,0:T(8,128)S(1)} fusion(bf16[64,16,576,1]{2,1,3,0:T(8,128)(2,1)} %bitcast.13, bf16[64,2,16,576]{3,2,1,0:T(8,128)(2,1)} %gather_fusion, pred[64]{0:T(512)(128)(4,1)S(1)} %compare_and_fusion.3), kind=kOutput, calls=%fused_computation.14 | convolution fusion | flops 38928384 | bytes 3670080 | tf_op jit(solution)/shard_map/nthc,nbc->nthb/dot_general | solution.py:110
  68.6 3.8 %fusion = f32[4,2,16,512]{3,0,2,1:T(4,128)S(1)} fusion(f32[64,2,16,512]{3,2,1,0:T(8,128)S(1)} %fusion.43, pred[4,64]{1,0:T(4,128)(4,1)S(1)} %fusion.81), kind=kOutput, calls=%fused_computation.12 | convolution fusion | flops 50331648 | bytes 4456704 | tf_op jit(solution)/shard_map/rn,nthc->rthc/dot_general | solution.py:149
  78.1 69.6 %all-gather.2.cloned.1.call-done = bf16[256,2048]{1,0:T(8,128)(2,1)} async-done(((bf16[8,2048]{1,0:T(8,128)(2,1)}), bf16[256,2048]{1,0:T(8,128)(2,1)}) %all-gather.2.cloned.1.call-update) | async-done | bytes 1048592 | tf_op jit(solution)/shard_map/all_gather | solution.py:158
  147.7 2.4 convolution_convert_fusion.2
  150.1 58.1 %all-reduce.4.cloned.1.call-done = bf16[256,224]{0,1:T(8,128)(2,1)} async-done(((bf16[256,224]{0,1:T(8,128)(2,1)}), bf16[256,224]{0,1:T(8,128)(2,1)}) %all-reduce.4.cloned.1.call-update) | async-done | bytes 114704 | tf_op jit(solution)/shard_map/psum | solution.py:160
  209.3 4.1 %gather_fusion.7 = bf16[1280,224]{1,0:T(8,128)(2,1)S(1)} fusion(bf16[128,224]{1,0:T(8,128)(2,1)S(1)} %copy.194, s32[2048]{0:T(1024)S(1)} %pad_clamp_fusion), kind=kCustom, calls=%fused_computation.7 | custom fusion | bytes 1152000 | tf_op jit(solution)/shard_map/jit(_take)/gather | solution.py:171
  214.6 9.8 %all-to-all-start.1 = ((bf16[32,40,1,224]{3,1,2,0:T(8,128)(2,1)}), bf16[32,40,1,224]{3,1,2,0:T(8,128)(2,1)S(1)}, u32[]{:S(2)}, u32[]{:S(2)}) async-start(bf16[32,40,1,224]{3,1,2,0:T(8,128)(2,1)} %select_select_fusion), calls=%async_computation.1 | async-start | bytes 1310720 | tf_op jit(solution)/shard_map/all_to_all | solution.py:174
  224.6 19.9 %all-to-all-done.1 = bf16[32,40,1,224]{3,1,2,0:T(8,128)(2,1)S(1)} async-done(((bf16[32,40,1,224]{3,1,2,0:T(8,128)(2,1)}), bf16[32,40,1,224]{3,1,2,0:T(8,128)(2,1)S(1)}, u32[]{:S(2)}, u32[]{:S(2)}) %all-to-all-start.1) | async-done | bytes 573472 | tf_op jit(solution)/shard_map/all_to_all | solution.py:174
  246.8 2.1 reshape.672
  250.3 2.9 fusion.91
  253.1 6.1 %convolution_convert_fusion = bf16[40,7168]{1,0:T(8,128)(2,1)} fusion(bf16[256,7168]{1,0:T(8,128)(2,1)} %param.29, bf16[7168,256]{1,0:T(8,128)(2,1)} %param.28, f32[40,256]{1,0:T(8,128)S(1)} %fusion.91, f32[40,7168]{1,0:T(8,128)S(1)} %reshape.672, f32[7168]{0:T(1024)S(1)} %copy-done.8, f32[40]{0:T(128)S(1)} %add_rsqrt_fusion), kind=kOutput, calls=%fused_computation.11 | convolution fusion | flops 294809600 | bytes 9130144 | tf_op jit(solution)/shard_map/dot_general | solution.py:184
  259.3 3.7 %convert_element_type.126 = bf16[1,40,128,56]{3,2,1,0:T(8,128)(2,1)S(1)} reshape(bf16[40,7168]{1,0:T(8,128)(2,1)} %convolution_convert_fusion) | data formatting | bytes 1146880 | tf_op jit(solution)/shard_map/convert_element_type | solution.py:186
  264.9 3.7 %reshape.761 = bf16[128,2,1120]{2,1,0:T(2,128)(2,1)} reshape(bf16[128,1,40,56]{3,2,1,0:T(8,128)(2,1)} %bitcast.155) | data formatting | bytes 1146880
  268.6 9.8 %all-to-all-start.2 = ((bf16[128,2,1120]{2,1,0:T(2,128)(2,1)}), bf16[128,2,1120]{2,1,0:T(2,128)(2,1)}, u32[]{:S(2)}, u32[]{:S(2)}) async-start(bf16[128,2,1120]{2,1,0:T(2,128)(2,1)} %reshape.761), calls=%async_computation.2 | async-start | bytes 1179648 | tf_op jit(solution)/shard_map/all_to_all | solution.py:185
  280.0 33.0 %gather_fusion.4 = f32[5120]{0:T(1024)S(1)} fusion(f32[128,16]{0,1:T(8,128)S(1)} %select_reduce_fusion.2, s32[5120]{0:T(1024)S(1)} %reshape.708), kind=kCustom, calls=%fused_computation.4 | custom fusion | bytes 81920 | tf_op jit(solution)/shard_map/gather | solution.py:207
  315.0 3.4 reshape.762
  320.0 2.1 copy.217
  323.3 3.0 copy.200
  326.3 28.2 %scatter_fusion = f32[128,56]{1,0:T(8,128)S(1)} fusion(f32[128,56]{1,0:T(8,128)S(1)} %copy.199, s32[5120]{0:T(1024)S(1)} %copy-done.9, f32[5120,56]{1,0:T(8,128)} %copy.200), kind=kCustom, calls=%fused_computation.8 | custom fusion | flops 286720 | bytes 3461120 | tf_op jit(solution)/shard_map/scatter-add | solution.py:211
  (149 shorter events, 43.2 us)
Async XLA Ops:
  6.5 66.6 %copy-start = (bf16[16,512,128]{2,1,0:T(8,128)(2,1)S(1)}, bf16[16,512,128]{2,1,0:T(8,128)(2,1)}, u32[]{:S(2)}) copy-start(bf16[16,512,128]{2,1,0:T(8,128)(2,1)} %param.21) | copy-start | bytes 6291460
  11.4 12.5 %copy-start.14 = (s32[1,4]{1,0:T(1,128)S(1)}, s32[1,4]{1,0:T(1,128)}, u32[]{:S(2)}) copy-start(s32[1,4]{1,0:T(1,128)} %param.18) | copy-start | bytes 52
  11.4 12.8 %copy-start.10 = (bf16[8,576]{1,0:T(8,128)(2,1)S(1)}, bf16[8,576]{1,0:T(8,128)(2,1)}, u32[]{:S(2)}) copy-start(bf16[8,576]{1,0:T(8,128)(2,1)} %param.16) | copy-start | bytes 27652
  11.4 12.8 %copy-start.6 = (bf16[8,9216]{1,0:T(8,128)(2,1)S(1)}, bf16[8,9216]{1,0:T(8,128)(2,1)}, u32[]{:S(2)}) copy-start(bf16[8,9216]{1,0:T(8,128)(2,1)} %param.15) | copy-start | bytes 442372
  11.4 13.2 %copy-start.5 = (bf16[512,576]{0,1:T(8,128)(2,1)S(1)}, bf16[512,576]{0,1:T(8,128)(2,1)}, u32[]{:S(2)}) copy-start(bf16[512,576]{0,1:T(8,128)(2,1)} %param.17) | copy-start | bytes 1769476
  11.4 45.3 %all-to-all-start = ((bf16[32,2,16,576]{3,2,1,0:T(8,128)(2,1)}), bf16[32,2,16,576]{3,2,1,0:T(8,128)(2,1)}, u32[]{:S(2)}, u32[]{:S(2)}) async-start(bf16[32,2,16,576]{3,2,1,0:T(8,128)(2,1)} %copy.175), calls=%async_computation | async-start | bytes 2621440 | tf_op jit(solution)/shard_map/all_to_all | solution.py:99
  23.2 124.6 %all-gather.2.cloned.1.call-start = ((), (), s32[]{:S(2)}) async-start(), calls=%async_computation.3 | async-start | bytes 1081344 | tf_op jit(solution)/shard_map/all_gather | solution.py:158
  68.6 4.1 %copy-start.2 = (bf16[4,384,576]{2,1,0:T(8,128)(2,1)S(1)}, bf16[4,384,576]{2,1,0:T(8,128)(2,1)}, u32[]{:S(2)}) copy-start(bf16[4,384,576]{2,1,0:T(8,128)(2,1)} %get-tuple-element.12) | copy-start | bytes 5308420
  68.6 4.1 %copy-start.4 = (f32[4,2,16,384]{3,2,1,0:T(8,128)S(1)}, f32[4,2,16,384]{3,2,1,0:T(8,128)}, u32[]{:S(2)}) copy-start(f32[4,2,16,384]{3,2,1,0:T(8,128)} %get-tuple-element.28) | copy-start | bytes 589828
  73.2 1.4 copy-start.13
  73.2 74.6 %copy-start.3 = (bf16[2048,224]{0,1:T(8,128)(2,1)S(1)}, bf16[2048,224]{0,1:T(8,128)(2,1)}, u32[]{:S(2)}) copy-start(bf16[2048,224]{0,1:T(8,128)(2,1)} %param.22) | copy-start | bytes 2752516
  73.6 134.7 %copy-start.7 = (bf16[256,224]{0,1:T(8,128)(2,1)S(1)}, bf16[256,224]{0,1:T(8,128)(2,1)}, u32[]{:S(2)}) copy-start(bf16[256,224]{0,1:T(8,128)(2,1)} %param.23) | copy-start | bytes 344068
  74.3 134.0 %all-reduce.4.cloned.1.call-start = ((), (), s32[]{:S(2)}) async-start(), calls=%async_computation.4 | async-start | bytes 229376 | tf_op jit(solution)/shard_map/psum | solution.py:160
  214.6 29.8 %all-to-all-start.1 = ((bf16[32,40,1,224]{3,1,2,0:T(8,128)(2,1)}), bf16[32,40,1,224]{3,1,2,0:T(8,128)(2,1)S(1)}, u32[]{:S(2)}, u32[]{:S(2)}) async-start(bf16[32,40,1,224]{3,1,2,0:T(8,128)(2,1)} %select_select_fusion), calls=%async_computation.1 | async-start | bytes 1310720 | tf_op jit(solution)/shard_map/all_to_all | solution.py:174
  224.5 88.6 %copy-start.11 = (pred[128]{0:T(512)(128)(4,1)}, pred[128]{0:T(512)(128)(4,1)S(1)}, u32[]{:S(2)}) copy-start(pred[128]{0:T(512)(128)(4,1)S(1)} %compare_and_fusion.2) | copy-start | bytes 388
  244.4 0.9 copy-start.1
  246.8 3.5 copy-start.8
  264.9 14.9 %copy-start.12 = (f32[256,4]{0,1:T(4,128)S(1)}, f32[256,4]{0,1:T(4,128)}, u32[]{:S(2)}) copy-start(f32[256,4]{0,1:T(4,128)} %param.26) | copy-start | bytes 12292
  268.6 46.4 %all-to-all-start.2 = ((bf16[128,2,1120]{2,1,0:T(2,128)(2,1)}), bf16[128,2,1120]{2,1,0:T(2,128)(2,1)}, u32[]{:S(2)}, u32[]{:S(2)}) async-start(bf16[128,2,1120]{2,1,0:T(2,128)(2,1)} %reshape.761), calls=%async_computation.2 | async-start | bytes 1179648 | tf_op jit(solution)/shard_map/all_to_all | solution.py:185
  323.3 3.0 copy-start.9
Sparse Core Ops, SparseCore 0:
  74.4 73.3 all-gather.1
  150.2 57.9 all-reduce.3
where the time goes:
time: 365 us; the launch traced here: 362 us
  waiting for transfers between devices  164 us (45%)
  local copies, waits for them, and re-layouts  82.7 us (23%)
  other arithmetic  40.6 us (11%)
  starting transfers between devices  31.9 us (9%)
  matrix products  29.1 us (8%)
  between operations  14 us (4%)
    all_gather x1, waiting for transfers between devices, per_device(): lax.all_gather(values, 'attn', axis=0, tiled=True)  69.6 us
    psum x1, waiting for transfers between devices, per_device(): lax.psum(partial_cols.astype(jnp.bfloat16), ('expert', 'rep'))  58.1 us
    gather x2, local copies, waits for them, and re-layouts, per_device(): share_table[back_rows, source_expert[:, None]]  33.1 us
    scatter-add x1, other arithmetic, per_device(): jax.ops.segment_sum(weighted, back_rows.reshape(-1), num_segments=rows_part)  28.2 us
    all_to_all x1, waiting for transfers between devices, per_device(): lax.all_to_all(outgoing_rows, 'attn', split_axis=0, concat_axis=2, tiled=...  19.9 us
    all_to_all x1, waiting for transfers between devices, per_device(): lax.all_to_all(outgoing, 'attn', split_axis=0, concat_axis=0, tiled=True)  16 us
    all_to_all x1, starting transfers between devices, per_device(): lax.all_to_all(outgoing, 'attn', split_axis=0, concat_axis=0, tiled=True)  11.7 us
    all_to_all x1, starting transfers between devices, per_device(): lax.all_to_all(outgoing_rows, 'attn', split_axis=0, concat_axis=2, tiled=...  9.85 us
  transfers between devices with their start and end apart: 5, of which 4 were waited for; matrix products, arithmetic and copies ran while one was open for 16% of the time, Pallas kernels for 0%

commit v1 on v0

v1 whole, which is shorter than its diff:
```python
import jax
import jax.numpy as jnp
from jax import lax
from jax.sharding import PartitionSpec as P

ROPE = 64
VH = 128
EXPERTS = 16
TOP = 4
CAP = 2


floor_score = -1e30
scale_out = 2.5
HIGH = lax.Precision.HIGHEST


def expert_tables(route_ids, part_index, part_count, capacity):
    row_count = route_ids.shape[0] // part_count
    route_part = lax.dynamic_slice_in_dim(route_ids, part_index * row_count, row_count, 0)
    member = jnp.any(
        route_part[:, :, None] == jnp.arange(EXPERTS, dtype=jnp.int32)[None, None, :], axis=1
    )
    order_rank = jnp.cumsum(member.astype(jnp.int32), axis=0) - 1
    slot_ids = jnp.arange(capacity, dtype=jnp.int32)
    pick = (member.T[:, None, :]) & (order_rank.T[:, None, :] == slot_ids[None, :, None])
    return pick, route_part


def per_device(
    queries,
    new_latent,
    cache_pool,
    local_len,
    spill_cache,
    spill_owner,
    w_uv,
    w_o,
    residual,
    norm_gain,
    route_ids,
    route_scores,
    w_gate,
    w_up,
    w_down,
):
    n_attn = lax.axis_size("attn")
    n_expert = lax.axis_size("expert")
    n_rep = lax.axis_size("rep")
    attn_here = lax.axis_index("attn")
    expert_here = lax.axis_index("expert")
    rep_here = lax.axis_index("rep")
    req_count = local_len.shape[1]
    head_count = w_uv.shape[0]
    row_width = new_latent.shape[1]
    lat_width = w_uv.shape[1]
    pool_rows = cache_pool.shape[0]
    score_scale = float(VH + ROPE) ** (-0.5)

    spill_count = spill_cache.shape[0]
    blk = spill_cache.shape[1]
    directory = spill_owner.reshape(n_attn, spill_count)
    owner_dev = jnp.where(directory >= 0, directory // req_count, -1)
    earlier = jnp.arange(spill_count)[:, None] > jnp.arange(spill_count)[None, :]
    same_owner = owner_dev[:, :, None] == owner_dev[:, None, :]
    order_rank = jnp.sum(same_owner & earlier[None, :, :], axis=2)
    slot_ids = jnp.arange(CAP)
    own_row = owner_dev[attn_here]
    own_rank = order_rank[attn_here]
    pick_slot = (own_row[None, None, :] == jnp.arange(n_attn)[:, None, None]) & (
        own_rank[None, None, :] == slot_ids[None, :, None]
    )
    outgoing = jnp.einsum(
        "dks,sbc->dkbc",
        pick_slot.astype(jnp.bfloat16),
        spill_cache,
        preferred_element_type=jnp.float32,
    ).astype(jnp.bfloat16)
    incoming = lax.all_to_all(outgoing, "attn", split_axis=0, concat_axis=0, tiled=True)
    mine_slot = (owner_dev[:, None, :] == attn_here) & (
        order_rank[:, None, :] == slot_ids[None, :, None]
    )
    present = jnp.any(mine_slot, axis=2).reshape(-1)
    request = jnp.sum(
        jnp.where(mine_slot, directory[:, None, :] - attn_here * req_count, 0), axis=2
    ).reshape(-1)
    spill_rows = incoming.reshape(n_attn * CAP * blk, row_width)

    query_rows = queries.reshape(req_count, 2, head_count, row_width)
    lengths = local_len[0]
    starts = jnp.cumsum(lengths) - lengths
    pos = jnp.arange(pool_rows)
    pool_ok = (pos[None, :] >= starts[:, None]) & (pos[None, :] < (starts + lengths)[:, None])
    pool_scores = (
        jnp.einsum("rthc,kc->rthk", query_rows, cache_pool, preferred_element_type=jnp.float32)
        * score_scale
    )
    pool_scores = jnp.where(pool_ok[:, None, None, :], pool_scores, floor_score)
    fresh_scores = (
        jnp.einsum("rthc,kc->rthk", query_rows, new_latent, preferred_element_type=jnp.float32)
        * score_scale
    )
    fresh_pos = jnp.arange(2 * req_count)
    fresh_ok = (fresh_pos[None, None, :] // 2 == jnp.arange(req_count)[:, None, None]) & (
        fresh_pos[None, None, :] % 2 <= jnp.arange(2)[None, :, None]
    )
    fresh_scores = jnp.where(fresh_ok[:, :, None, :], fresh_scores, floor_score)
    block_ok = (request[None, :] == jnp.arange(req_count)[:, None]) & present[None, :]
    spill_ok = jnp.broadcast_to(block_ok[:, :, None], block_ok.shape + (blk,)).reshape(
        req_count, -1
    )
    spill_scores = (
        jnp.einsum("rthc,kc->rthk", query_rows, spill_rows, preferred_element_type=jnp.float32)
        * score_scale
    )
    spill_scores = jnp.where(spill_ok[:, None, None, :], spill_scores, floor_score)
    row_top = jnp.maximum(
        jnp.maximum(jnp.max(pool_scores, axis=3), jnp.max(fresh_scores, axis=3)),
        jnp.max(spill_scores, axis=3),
    )
    pool_weight = jnp.exp(pool_scores - row_top[..., None])
    fresh_weight = jnp.exp(fresh_scores - row_top[..., None])
    spill_weight = jnp.exp(spill_scores - row_top[..., None])
    denominator = (
        jnp.sum(pool_weight, axis=3) + jnp.sum(fresh_weight, axis=3) + jnp.sum(spill_weight, axis=3)
    )
    numerator = jnp.einsum(
        "rthk,kc->rthc",
        pool_weight.astype(jnp.bfloat16),
        cache_pool[:, :lat_width],
        preferred_element_type=jnp.float32,
    )
    numerator = numerator + jnp.einsum(
        "rthk,kc->rthc",
        fresh_weight.astype(jnp.bfloat16),
        new_latent[:, :lat_width],
        preferred_element_type=jnp.float32,
    )
    numerator = numerator + jnp.einsum(
        "rthk,kc->rthc",
        spill_weight.astype(jnp.bfloat16),
        spill_rows[:, :lat_width],
        preferred_element_type=jnp.float32,
    )
    attended = (numerator / denominator[..., None]).astype(jnp.bfloat16)
    values = jnp.einsum(
        "rthc,hcv->rthv", attended, w_uv, preferred_element_type=jnp.float32
    ).astype(jnp.bfloat16)
    tok_here = 2 * req_count
    values = values.reshape(tok_here, head_count * w_uv.shape[2])

    spread = jnp.broadcast_to(values[None], (n_attn,) + values.shape)
    all_values = lax.all_to_all(spread, "attn", split_axis=0, concat_axis=0, tiled=True)
    all_values = all_values.reshape(n_attn * tok_here, -1)
    partial_cols = jnp.dot(all_values, w_o, preferred_element_type=jnp.float32)

    tokens = partial_cols.shape[0]
    rows_part = tokens // n_rep
    sub_cols = partial_cols.shape[1] // n_expert
    pieces = (
        partial_cols.astype(jnp.bfloat16)
        .reshape(n_rep, rows_part, n_expert, sub_cols)
        .transpose(2, 0, 1, 3)
        .reshape(n_expert * n_rep, rows_part, sub_cols)
    )
    got = lax.all_to_all(pieces, ("expert", "rep"), split_axis=0, concat_axis=0, tiled=True)
    attn_own = jnp.sum(got.astype(jnp.float32), axis=0)
    res_own = lax.dynamic_slice(
        residual, (rep_here * rows_part, expert_here * sub_cols), (rows_part, sub_cols)
    )
    hidden_own = (res_own.astype(jnp.float32) + attn_own).astype(jnp.bfloat16)

    capacity = rows_part * TOP // EXPERTS * 5 // 4
    shards = n_attn * n_expert // EXPERTS
    pick, route_part = expert_tables(route_ids, rep_here, n_rep, capacity)
    pick_f = pick.astype(jnp.float32)
    rows_e = jnp.einsum(
        "jsr,rc->jsc", pick.astype(jnp.bfloat16), hidden_own, preferred_element_type=jnp.float32
    ).astype(jnp.bfloat16)
    send_rows = jnp.repeat(rows_e, shards, axis=0)
    recv_rows = lax.all_to_all(send_rows, ("attn", "expert"), split_axis=0, concat_axis=0, tiled=True)
    full_rows = recv_rows.transpose(1, 0, 2).reshape(capacity, -1)
    widened = full_rows.astype(jnp.float32)
    normed = (
        widened * lax.rsqrt(jnp.mean(widened * widened, axis=1, keepdims=True) + 1e-06) * norm_gain
    ).astype(jnp.bfloat16)
    gate_proj = jnp.dot(normed, w_gate, preferred_element_type=jnp.float32)
    up_proj = jnp.dot(normed, w_up, preferred_element_type=jnp.float32)
    activated = (jax.nn.silu(gate_proj) * up_proj).astype(jnp.bfloat16)
    result = jnp.dot(activated, w_down, preferred_element_type=jnp.float32)

    n_dev = n_attn * n_expert
    back = result.astype(jnp.bfloat16).reshape(capacity, n_dev, sub_cols).transpose(1, 0, 2)
    returned = lax.all_to_all(back, ("attn", "expert"), split_axis=0, concat_axis=0, tiled=True)
    summed = jnp.sum(
        returned.astype(jnp.float32).reshape(EXPERTS, shards, capacity, sub_cols), axis=1
    )
    share_part = lax.dynamic_slice_in_dim(route_scores, rep_here * rows_part, rows_part, 0)
    share_part = share_part / jnp.sum(share_part, axis=1, keepdims=True)
    share_table = jnp.sum(
        jnp.where(
            route_part[:, :, None] == jnp.arange(EXPERTS, dtype=jnp.int32)[None, None, :],
            share_part[:, :, None],
            0.0,
        ),
        axis=1,
    )
    coef = jnp.sum(jnp.where(pick, share_table.T[:, None, :], 0.0), axis=2) * scale_out
    weighted = coef[:, :, None] * summed
    routed = jnp.einsum("jsr,jsc->rc", pick_f, weighted, precision=HIGH)
    return (hidden_own.astype(jnp.float32) + routed).astype(jnp.bfloat16)


def solution(mesh):
    return jax.shard_map(
        per_device,
        mesh=mesh,
        in_specs=(
            P("attn", ("expert", "rep")),
            P("attn", None),
            P("attn", None),
            P("attn", None),
            P("attn", None, None),
            P(),
            P(("expert", "rep"), None, None),
            P(("expert", "rep"), "attn"),
            P(None, "attn"),
            P(),
            P(),
            P(),
            P(None, ("attn", "expert")),
            P(None, ("attn", "expert")),
            P(("attn", "expert"), None),
        ),
        out_specs=P("rep", ("attn", "expert")),
        check_vma=False,
    )
```

time: 365 us -> 193 us (0.53)
  waiting for transfers between devices: 164 us -> 77.1 us
  local copies, waits for them, and re-layouts: 82.7 us -> 31.3 us
  other arithmetic: 40.6 us -> 4.04 us
  blocking collectives: 0 us -> 30.1 us
  between operations: 14 us -> 0.42 us
  matrix products: 29.1 us -> 19.8 us
    all_gather x1 -> x0, waiting for transfers between devices: 69.6 us -> none  [per_device(): lax.all_gather(values, 'attn', axis=0, tiled=True)]
    psum x1 -> x0, waiting for transfers between devices: 58.1 us -> none  [per_device(): lax.psum(partial_cols.astype(jnp.bfloat16), ('expert', 'rep'))]
    gather x21 -> x0, local copies, waits for them, and re-layouts: 50.8 us -> none  [the longest x2 33.1 us: per_device(): share_table[back_rows, source_expert[:, None]]]
    all_to_all x0 -> x1, blocking collectives: none -> 30.1 us  [per_device(): lax.all_to_all(send_rows, ('attn', 'expert'), split_axis=0, concat_axis=0...]
    all_to_all x2 -> x3, waiting for transfers between devices: 19.9 us -> 49.9 us  [the longest x1 26.6 us: per_device(): lax.all_to_all(spread, 'attn', split_axis=0, concat_axis=0, tiled=True)]
    scatter-add x1 -> x0, other arithmetic: 28.2 us -> none  [per_device(): jax.ops.segment_sum(weighted, back_rows.reshape(-1), num_segments=rows_part)]
    all_to_all x1, waiting for transfers between devices: 16 us -> 27.2 us  [per_device(): lax.all_to_all(outgoing, 'attn', split_axis=0, concat_axis=0, tiled=True)]
    dot_general x9, matrix products: 18.1 us -> 8.81 us  [the longest x1 2.15 us: per_device(): jnp.einsum('rthc,kc->rthk', query_rows, cache_pool, preferred_element_typ...]
  transfers between devices with their start and end apart: 5 -> 4, of which waited for: 4 -> 4; matrix products, arithmetic and copies ran while one was open for 16% -> 4% of each run, Pallas kernels for 0% -> 0%
where the time goes in v1:
time: 193 us
  waiting for transfers between devices  77.1 us (40%)
  local copies, waits for them, and re-layouts  31.3 us (16%)
  blocking collectives  30.1 us (16%)
  starting transfers between devices  29.9 us (15%)
  matrix products  19.8 us (10%)
  other arithmetic  4.04 us (2%)
    all_to_all x1, blocking collectives, per_device(): lax.all_to_all(send_rows, ('attn', 'expert'), split_axis=0, concat_axis=0...  30.1 us
    all_to_all x1, waiting for transfers between devices, per_device(): lax.all_to_all(outgoing, 'attn', split_axis=0, concat_axis=0, tiled=True)  27.2 us
    all_to_all x1, waiting for transfers between devices, per_device(): lax.all_to_all(spread, 'attn', split_axis=0, concat_axis=0, tiled=True)  26.6 us
    all_to_all x1, waiting for transfers between devices, per_device(): lax.all_to_all(back, ('attn', 'expert'), split_axis=0, concat_axis=0, til...  18.9 us
    unnamed x21, local copies, waits for them, and re-layouts  13.8 us
    all_to_all x1, starting transfers between devices, per_device(): lax.all_to_all(outgoing, 'attn', split_axis=0, concat_axis=0, tiled=True)  11.6 us
    all_to_all x1, starting transfers between devices, per_device(): lax.all_to_all(back, ('attn', 'expert'), split_axis=0, concat_axis=0, til...  7.63 us
    dot_general x1, matrix products, per_device(): result = jnp.dot(activated, w_down, preferred_element_type=jnp.float32)  6.12 us
  transfers between devices with their start and end apart: 4, of which 4 were waited for; matrix products, arithmetic and copies ran while one was open for 4% of the time, Pallas kernels for 0%

profile of v1, /device:TPU:2, one launch (start us, length us, event | category | flops | bytes accessed | tf_op | source)
XLA Modules:
  0.0 192.5 jit_solution(7931383255645465847)
XLA Ops:
  1.8 1.6 convolution_convert_fusion.1
  4.9 11.6 %all-to-all-start = ((bf16[32,2,16,576]{3,2,1,0:T(8,128)(2,1)}), bf16[32,2,16,576]{3,2,1,0:T(8,128)(2,1)S(1)}, u32[]{:S(2)}, u32[]{:S(2)}) async-start(bf16[32,2,16,576]{3,2,1,0:T(8,128)(2,1)} %copy.65), calls=%async_computation | async-start | bytes 2621440 | tf_op jit(solution)/shard_map/all_to_all | solution.py:79
  17.6 1.7 reshape.419
  20.7 2.1 %fusion.76 = (f32[4,2,16]{2,1,0:T(2,128)S(1)}, f32[4,2,16,512]{3,2,1,0:T(8,128)}) fusion(bf16[4,2,16,576]{3,2,1,0:T(8,128)(2,1)} %reshape.419, bf16[512,576]{0,1:T(8,128)(2,1)} %param.17, pred[4,512]{1,0:T(4,128)(4,1)S(1)} %fusion.68), kind=kOutput, calls=%fused_computation.127 | convolution fusion | flops 75693952 | bytes 1001984 | tf_op jit(solution)/shard_map/rthc,kc->rthk/dot_general | solution.py:95
  22.9 27.2 %all-to-all-done = bf16[32,2,16,576]{3,2,1,0:T(8,128)(2,1)S(1)} async-done(((bf16[32,2,16,576]{3,2,1,0:T(8,128)(2,1)}), bf16[32,2,16,576]{3,2,1,0:T(8,128)(2,1)S(1)}, u32[]{:S(2)}, u32[]{:S(2)}) %all-to-all-start) | async-done | bytes 1179680 | tf_op jit(solution)/shard_map/all_to_all | solution.py:79
  50.1 1.5 fusion.75
  54.9 5.8 %all-to-all-start.1 = ((bf16[32,8,2048]{2,1,0:T(8,128)(2,1)}), bf16[32,8,2048]{2,1,0:T(8,128)(2,1)S(1)}, u32[]{:S(2)}, u32[]{:S(2)}) async-start(bf16[32,8,2048]{2,1,0:T(8,128)(2,1)} %broadcast_in_dim.95), calls=%async_computation.1 | async-start | bytes 2097152 | tf_op jit(solution)/shard_map/all_to_all | solution.py:153
  61.1 26.6 %all-to-all-done.1 = bf16[32,8,2048]{2,1,0:T(8,128)(2,1)S(1)} async-done(((bf16[32,8,2048]{2,1,0:T(8,128)(2,1)}), bf16[32,8,2048]{2,1,0:T(8,128)(2,1)S(1)}, u32[]{:S(2)}, u32[]{:S(2)}) %all-to-all-start.1) | async-done | bytes 1048608 | tf_op jit(solution)/shard_map/all_to_all | solution.py:153
  87.7 1.7 convolution_convert_fusion.3
  90.0 4.8 %all-to-all-start.2 = ((bf16[8,128,56]{1,2,0:T(8,128)(2,1)}), bf16[8,128,56]{1,2,0:T(8,128)(2,1)S(1)}, u32[]{:S(2)}, u32[]{:S(2)}) async-start(bf16[8,128,56]{1,2,0:T(8,128)(2,1)} %bitcast.26), calls=%async_computation.2 | async-start | bytes 229376 | tf_op jit(solution)/shard_map/all_to_all | solution.py:166
  94.9 4.4 %all-to-all-done.2 = bf16[8,128,56]{1,2,0:T(8,128)(2,1)S(1)} async-done(((bf16[8,128,56]{1,2,0:T(8,128)(2,1)}), bf16[8,128,56]{1,2,0:T(8,128)(2,1)S(1)}, u32[]{:S(2)}, u32[]{:S(2)}) %all-to-all-start.2) | async-done | bytes 114720 | tf_op jit(solution)/shard_map/all_to_all | solution.py:166
  100.5 3.0 %reshape.443 = bf16[128,2,1120]{2,1,0:T(2,128)(2,1)} reshape(bf16[128,40,56]{2,1,0:T(8,128)(2,1)S(1)} %bitcast.114) | data formatting | bytes 1146880
  103.5 30.1 %all_to_all.25 = bf16[128,2,1120]{2,1,0:T(2,128)(2,1)} all-to-all(bf16[128,2,1120]{2,1,0:T(2,128)(2,1)} %reshape.443), channel_id=1, replica_groups=mesh['attn'=32,'expert'=4,'rep'=2] {'attn','expert'}, dimensions={0} | all-to-all | bytes 1146880 | tf_op jit(solution)/shard_map/all_to_all | solution.py:181
  133.6 3.3 %reshape.444 = bf16[128,40,56]{2,1,0:T(8,128)(2,1)S(1)} reshape(bf16[128,2,1120]{2,1,0:T(2,128)(2,1)} %all_to_all.25) | data formatting | bytes 1146880
  137.6 2.0 %copy.74 = f32[40,128,56]{2,1,0:T(8,128)} copy(f32[40,128,56]{2,0,1:T(8,128)S(1)} %convert_bitcast_fusion) | data formatting | bytes 2293760 | tf_op jit(solution)/shard_map/convert_element_type | solution.py:183
  139.6 2.9 %reshape.429 = f32[40,7168]{1,0:T(8,128)S(1)} reshape(f32[40,128,56]{2,1,0:T(8,128)} %copy.74) | data formatting | bytes 2293760 | tf_op jit(solution)/shard_map/convert_element_type | solution.py:183
  142.5 2.8 %fusion.73 = f32[40,256]{1,0:T(8,128)S(1)} fusion(bf16[7168,256]{1,0:T(8,128)(2,1)} %param.27, f32[40,7168]{1,0:T(8,128)S(1)} %reshape.429, f32[7168]{0:T(1024)S(1)} %copy-done.3, f32[40]{0:T(128)S(1)} %add_rsqrt_fusion), kind=kOutput, calls=%fused_computation.125 | convolution fusion | flops 147660800 | bytes 4886688 | tf_op jit(solution)/shard_map/dot_general | solution.py:187
  145.4 6.1 %convolution_convert_fusion = bf16[40,7168]{1,0:T(8,128)(2,1)} fusion(bf16[256,7168]{1,0:T(8,128)(2,1)} %param.29, bf16[7168,256]{1,0:T(8,128)(2,1)} %param.28, f32[40,256]{1,0:T(8,128)S(1)} %fusion.73, f32[40,7168]{1,0:T(8,128)S(1)} %reshape.429, f32[7168]{0:T(1024)S(1)} %copy-done.3, f32[40]{0:T(128)S(1)} %add_rsqrt_fusion), kind=kOutput, calls=%fused_computation | convolution fusion | flops 294809600 | bytes 9130144 | tf_op jit(solution)/shard_map/dot_general | solution.py:190
  151.5 3.7 %reshape.426 = bf16[40,128,56]{2,1,0:T(8,128)(2,1)S(1)} reshape(bf16[40,7168]{1,0:T(8,128)(2,1)} %convolution_convert_fusion) | data formatting | bytes 1146880 | tf_op jit(solution)/shard_map/reshape | solution.py:193
  155.2 1.9 copy.75
  157.1 3.7 %reshape.445 = bf16[128,2,1120]{2,1,0:T(2,128)(2,1)} reshape(bf16[128,40,56]{2,1,0:T(8,128)(2,1)} %copy.75) | data formatting | bytes 1146880
  160.8 7.6 %all-to-all-start.4 = ((bf16[128,2,1120]{2,1,0:T(2,128)(2,1)}), bf16[128,2,1120]{2,1,0:T(2,128)(2,1)}, u32[]{:S(2)}, u32[]{:S(2)}) async-start(bf16[128,2,1120]{2,1,0:T(2,128)(2,1)} %reshape.445), calls=%async_computation.4 | async-start | bytes 1179648 | tf_op jit(solution)/shard_map/all_to_all | solution.py:194
  168.8 18.9 %all-to-all-done.4 = bf16[128,2,1120]{2,1,0:T(2,128)(2,1)} async-done(((bf16[128,2,1120]{2,1,0:T(2,128)(2,1)}), bf16[128,2,1120]{2,1,0:T(2,128)(2,1)}, u32[]{:S(2)}, u32[]{:S(2)}) %all-to-all-start.4) | async-done | bytes 573472 | tf_op jit(solution)/shard_map/all_to_all | solution.py:194
  187.7 3.3 %reshape.446 = bf16[128,40,56]{2,1,0:T(8,128)(2,1)S(1)} reshape(bf16[128,2,1120]{2,1,0:T(2,128)(2,1)} %all-to-all-done.4) | data formatting | bytes 1146880
  (79 shorter events, 13.5 us)
Async XLA Ops:
  0.0 53.3 %copy-start = (bf16[16,512,128]{2,1,0:T(8,128)(2,1)S(1)}, bf16[16,512,128]{2,1,0:T(8,128)(2,1)}, u32[]{:S(2)}) copy-start(bf16[16,512,128]{2,1,0:T(8,128)(2,1)} %param.21) | copy-start | bytes 6291460
  4.9 11.7 %copy-start.7 = (s32[1,4]{1,0:T(1,128)S(1)}, s32[1,4]{1,0:T(1,128)}, u32[]{:S(2)}) copy-start(s32[1,4]{1,0:T(1,128)} %param.18) | copy-start | bytes 52
  4.9 14.6 %copy-start.4 = (bf16[8,576]{1,0:T(8,128)(2,1)S(1)}, bf16[8,576]{1,0:T(8,128)(2,1)}, u32[]{:S(2)}) copy-start(bf16[8,576]{1,0:T(8,128)(2,1)} %param.16) | copy-start | bytes 27652
  4.9 45.2 %all-to-all-start = ((bf16[32,2,16,576]{3,2,1,0:T(8,128)(2,1)}), bf16[32,2,16,576]{3,2,1,0:T(8,128)(2,1)S(1)}, u32[]{:S(2)}, u32[]{:S(2)}) async-start(bf16[32,2,16,576]{3,2,1,0:T(8,128)(2,1)} %copy.65), calls=%async_computation | async-start | bytes 2621440 | tf_op jit(solution)/shard_map/all_to_all | solution.py:79
  51.7 1.0 copy-start.1
  51.9 1.1 copy-start.2
  54.9 5.8 %copy-start.6 = (s32[256,4]{0,1:T(4,128)S(1)}, s32[256,4]{0,1:T(4,128)}, u32[]{:S(2)}) copy-start(s32[256,4]{0,1:T(4,128)} %param.25) | copy-start | bytes 12292
  54.9 32.7 %all-to-all-start.1 = ((bf16[32,8,2048]{2,1,0:T(8,128)(2,1)}), bf16[32,8,2048]{2,1,0:T(8,128)(2,1)S(1)}, u32[]{:S(2)}, u32[]{:S(2)}) async-start(bf16[32,8,2048]{2,1,0:T(8,128)(2,1)} %broadcast_in_dim.95), calls=%async_computation.1 | async-start | bytes 2097152 | tf_op jit(solution)/shard_map/all_to_all | solution.py:153
  90.0 9.3 %all-to-all-start.2 = ((bf16[8,128,56]{1,2,0:T(8,128)(2,1)}), bf16[8,128,56]{1,2,0:T(8,128)(2,1)S(1)}, u32[]{:S(2)}, u32[]{:S(2)}) async-start(bf16[8,128,56]{1,2,0:T(8,128)(2,1)} %bitcast.26), calls=%async_computation.2 | async-start | bytes 229376 | tf_op jit(solution)/shard_map/all_to_all | solution.py:166
  139.6 2.9 %copy-start.3 = (f32[7168]{0:T(1024)S(1)}, f32[7168]{0:T(1024)}, u32[]{:S(2)}) copy-start(f32[7168]{0:T(1024)} %param.24) | copy-start | bytes 86020
  157.1 11.4 %copy-start.5 = (f32[256,4]{0,1:T(4,128)S(1)}, f32[256,4]{0,1:T(4,128)}, u32[]{:S(2)}) copy-start(f32[256,4]{0,1:T(4,128)} %param.26) | copy-start | bytes 12292
  160.8 26.8 %all-to-all-start.4 = ((bf16[128,2,1120]{2,1,0:T(2,128)(2,1)}), bf16[128,2,1120]{2,1,0:T(2,128)(2,1)}, u32[]{:S(2)}, u32[]{:S(2)}) async-start(bf16[128,2,1120]{2,1,0:T(2,128)(2,1)} %reshape.445), calls=%async_computation.4 | async-start | bytes 1179648 | tf_op jit(solution)/shard_map/all_to_all | solution.py:194

commit v2 on v1

--- a/solution.py
+++ b/solution.py
@@ -70,13 +70,18 @@
     pick_slot = (own_row[None, None, :] == jnp.arange(n_attn)[:, None, None]) & (
         own_rank[None, None, :] == slot_ids[None, :, None]
     )
+    my_slot = lax.dynamic_slice_in_dim(pick_slot, rep_here, 1, 1)
     outgoing = jnp.einsum(
         "dks,sbc->dkbc",
-        pick_slot.astype(jnp.bfloat16),
+        my_slot.astype(jnp.bfloat16),
         spill_cache,
         preferred_element_type=jnp.float32,
     ).astype(jnp.bfloat16)
-    incoming = lax.all_to_all(outgoing, "attn", split_axis=0, concat_axis=0, tiled=True)
+    half = lax.all_to_all(outgoing, "attn", split_axis=0, concat_axis=0, tiled=True)
+    other = lax.ppermute(half, "rep", [(i, (i + 1) % n_rep) for i in range(n_rep)])
+    first = jnp.where(rep_here == 0, half, other)
+    second = jnp.where(rep_here == 0, other, half)
+    incoming = jnp.concatenate([first, second], axis=1)
     mine_slot = (owner_dev[:, None, :] == attn_here) & (
         order_rank[:, None, :] == slot_ids[None, :, None]
     )

time: 193 us -> 183 us (0.948)
  waiting for transfers between devices: 77.1 us -> 70.9 us
  matrix products: 19.8 us -> 16 us
    all_to_all x1, waiting for transfers between devices: 27.2 us -> 19.2 us  [per_device(): lax.all_to_all(outgoing, 'attn', split_axis=0, concat_axis=0, tiled=True)]
    unnamed x21 -> x19, local copies, waits for them, and re-layouts: 13.8 us -> 13.5 us
  transfers between devices with their start and end apart: 4 -> 5, of which waited for: 4 -> 5; matrix products, arithmetic and copies ran while one was open for 4% -> 2% of each run, Pallas kernels for 0% -> 0%
where the time goes in v2:
time: 183 us; the launch traced here: 182 us
  waiting for transfers between devices  70.9 us (39%)
  blocking collectives  30.1 us (16%)
  local copies, waits for them, and re-layouts  29.9 us (16%)
  starting transfers between devices  29.2 us (16%)
  matrix products  16 us (9%)
  other arithmetic  5.43 us (3%)
    all_to_all x1, blocking collectives, per_device(): lax.all_to_all(send_rows, ('attn', 'expert'), split_axis=0, concat_axis=0...  30.1 us
    all_to_all x1, waiting for transfers between devices, per_device(): lax.all_to_all(spread, 'attn', split_axis=0, concat_axis=0, tiled=True)  28.2 us
    all_to_all x1, waiting for transfers between devices, per_device(): lax.all_to_all(outgoing, 'attn', split_axis=0, concat_axis=0, tiled=True)  19.2 us
    all_to_all x1, waiting for transfers between devices, per_device(): lax.all_to_all(back, ('attn', 'expert'), split_axis=0, concat_axis=0, til...  18.9 us
    unnamed x19, local copies, waits for them, and re-layouts  13.5 us
    all_to_all x1, starting transfers between devices, per_device(): lax.all_to_all(outgoing, 'attn', split_axis=0, concat_axis=0, tiled=True)  11.6 us
    all_to_all x1, starting transfers between devices, per_device(): lax.all_to_all(back, ('attn', 'expert'), split_axis=0, concat_axis=0, til...  7.63 us
    dot_general x1, matrix products, per_device(): result = jnp.dot(activated, w_down, preferred_element_type=jnp.float32)  6.12 us
  transfers between devices with their start and end apart: 5, of which 5 were waited for; matrix products, arithmetic and copies ran while one was open for 2% of the time, Pallas kernels for 0%

profile of v2, /device:TPU:2, one launch (start us, length us, event | category | flops | bytes accessed | tf_op | source)
XLA Modules:
  0.0 182.0 jit_solution(1378319463999789971)
XLA Ops:
  1.8 1.4 fusion.3
  4.3 11.6 %all-to-all-start = ((bf16[32,1,16,576]{3,2,1,0:T(8,128)(2,1)}), bf16[32,1,16,576]{3,2,1,0:T(8,128)(2,1)S(1)}, u32[]{:S(2)}, u32[]{:S(2)}) async-start(bf16[32,1,16,576]{3,2,1,0:T(8,128)(2,1)} %copy.65), calls=%async_computation | async-start | bytes 1310720 | tf_op jit(solution)/shard_map/all_to_all | solution.py:80
  16.9 19.2 %all-to-all-done = bf16[32,1,16,576]{3,2,1,0:T(8,128)(2,1)S(1)} async-done(((bf16[32,1,16,576]{3,2,1,0:T(8,128)(2,1)}), bf16[32,1,16,576]{3,2,1,0:T(8,128)(2,1)S(1)}, u32[]{:S(2)}, u32[]{:S(2)}) %all-to-all-start) | async-done | bytes 589856 | tf_op jit(solution)/shard_map/all_to_all | solution.py:80
  36.4 1.1 reshape.424
  38.4 1.2 broadcast_select_fusion.1
  42.3 1.1 broadcast_in_dim.95
  43.4 5.1 %all-to-all-start.1 = ((bf16[32,8,2048]{2,1,0:T(8,128)(2,1)}), bf16[32,8,2048]{2,1,0:T(8,128)(2,1)S(1)}, u32[]{:S(2)}, u32[]{:S(2)}) async-start(bf16[32,8,2048]{2,1,0:T(8,128)(2,1)} %broadcast_in_dim.95), calls=%async_computation.1 | async-start | bytes 2097152 | tf_op jit(solution)/shard_map/all_to_all | solution.py:158
  48.9 28.2 %all-to-all-done.1 = bf16[32,8,2048]{2,1,0:T(8,128)(2,1)S(1)} async-done(((bf16[32,8,2048]{2,1,0:T(8,128)(2,1)}), bf16[32,8,2048]{2,1,0:T(8,128)(2,1)S(1)}, u32[]{:S(2)}, u32[]{:S(2)}) %all-to-all-start.1) | async-done | bytes 1048608 | tf_op jit(solution)/shard_map/all_to_all | solution.py:158
  77.1 1.7 convolution_convert_fusion.3
  79.5 4.8 %all-to-all-start.2 = ((bf16[8,128,56]{1,2,0:T(8,128)(2,1)}), bf16[8,128,56]{1,2,0:T(8,128)(2,1)S(1)}, u32[]{:S(2)}, u32[]{:S(2)}) async-start(bf16[8,128,56]{1,2,0:T(8,128)(2,1)} %bitcast.26), calls=%async_computation.2 | async-start | bytes 229376 | tf_op jit(solution)/shard_map/all_to_all | solution.py:171
  84.4 4.4 %all-to-all-done.2 = bf16[8,128,56]{1,2,0:T(8,128)(2,1)S(1)} async-done(((bf16[8,128,56]{1,2,0:T(8,128)(2,1)}), bf16[8,128,56]{1,2,0:T(8,128)(2,1)S(1)}, u32[]{:S(2)}, u32[]{:S(2)}) %all-to-all-start.2) | async-done | bytes 114720 | tf_op jit(solution)/shard_map/all_to_all | solution.py:171
  90.0 3.0 %reshape.448 = bf16[128,2,1120]{2,1,0:T(2,128)(2,1)} reshape(bf16[128,40,56]{2,1,0:T(8,128)(2,1)S(1)} %bitcast.112) | data formatting | bytes 1146880
  93.0 30.1 %all_to_all.25 = bf16[128,2,1120]{2,1,0:T(2,128)(2,1)} all-to-all(bf16[128,2,1120]{2,1,0:T(2,128)(2,1)} %reshape.448), channel_id=1, replica_groups=mesh['attn'=32,'expert'=4,'rep'=2] {'attn','expert'}, dimensions={0} | all-to-all | bytes 1146880 | tf_op jit(solution)/shard_map/all_to_all | solution.py:186
  123.1 3.3 %reshape.449 = bf16[128,40,56]{2,1,0:T(8,128)(2,1)S(1)} reshape(bf16[128,2,1120]{2,1,0:T(2,128)(2,1)} %all_to_all.25) | data formatting | bytes 1146880
  127.1 2.0 %copy.74 = f32[40,128,56]{2,1,0:T(8,128)} copy(f32[40,128,56]{2,0,1:T(8,128)S(1)} %convert_bitcast_fusion) | data formatting | bytes 2293760 | tf_op jit(solution)/shard_map/convert_element_type | solution.py:188
  129.1 2.9 %reshape.435 = f32[40,7168]{1,0:T(8,128)S(1)} reshape(f32[40,128,56]{2,1,0:T(8,128)} %copy.74) | data formatting | bytes 2293760 | tf_op jit(solution)/shard_map/convert_element_type | solution.py:188
  132.0 2.8 %fusion.73 = f32[40,256]{1,0:T(8,128)S(1)} fusion(bf16[7168,256]{1,0:T(8,128)(2,1)} %param.27, f32[40,7168]{1,0:T(8,128)S(1)} %reshape.435, f32[7168]{0:T(1024)S(1)} %copy-done.2, f32[40]{0:T(128)S(1)} %add_rsqrt_fusion), kind=kOutput, calls=%fused_computation.129 | convolution fusion | flops 147660800 | bytes 4886688 | tf_op jit(solution)/shard_map/dot_general | solution.py:192
  134.9 6.1 %convolution_convert_fusion = bf16[40,7168]{1,0:T(8,128)(2,1)} fusion(bf16[256,7168]{1,0:T(8,128)(2,1)} %param.29, bf16[7168,256]{1,0:T(8,128)(2,1)} %param.28, f32[40,256]{1,0:T(8,128)S(1)} %fusion.73, f32[40,7168]{1,0:T(8,128)S(1)} %reshape.435, f32[7168]{0:T(1024)S(1)} %copy-done.2, f32[40]{0:T(128)S(1)} %add_rsqrt_fusion), kind=kOutput, calls=%fused_computation | convolution fusion | flops 294809600 | bytes 9130144 | tf_op jit(solution)/shard_map/dot_general | solution.py:195
  141.0 3.7 %reshape.432 = bf16[40,128,56]{2,1,0:T(8,128)(2,1)S(1)} reshape(bf16[40,7168]{1,0:T(8,128)(2,1)} %convolution_convert_fusion) | data formatting | bytes 1146880 | tf_op jit(solution)/shard_map/reshape | solution.py:198
  144.7 1.9 %copy.75 = bf16[128,40,56]{2,1,0:T(8,128)(2,1)} copy(bf16[128,40,56]{2,0,1:T(8,128)(2,1)S(1)} %bitcast.113) | data formatting | bytes 1146880 | tf_op jit(solution)/shard_map/transpose | solution.py:198
  146.6 3.7 %reshape.450 = bf16[128,2,1120]{2,1,0:T(2,128)(2,1)} reshape(bf16[128,40,56]{2,1,0:T(8,128)(2,1)} %copy.75) | data formatting | bytes 1146880
  150.3 7.6 %all-to-all-start.4 = ((bf16[128,2,1120]{2,1,0:T(2,128)(2,1)}), bf16[128,2,1120]{2,1,0:T(2,128)(2,1)}, u32[]{:S(2)}, u32[]{:S(2)}) async-start(bf16[128,2,1120]{2,1,0:T(2,128)(2,1)} %reshape.450), calls=%async_computation.4 | async-start | bytes 1179648 | tf_op jit(solution)/shard_map/all_to_all | solution.py:199
  158.3 18.9 %all-to-all-done.4 = bf16[128,2,1120]{2,1,0:T(2,128)(2,1)} async-done(((bf16[128,2,1120]{2,1,0:T(2,128)(2,1)}), bf16[128,2,1120]{2,1,0:T(2,128)(2,1)}, u32[]{:S(2)}, u32[]{:S(2)}) %all-to-all-start.4) | async-done | bytes 573472 | tf_op jit(solution)/shard_map/all_to_all | solution.py:199
  177.1 3.3 %reshape.451 = bf16[128,40,56]{2,1,0:T(8,128)(2,1)S(1)} reshape(bf16[128,2,1120]{2,1,0:T(2,128)(2,1)} %all-to-all-done.4) | data formatting | bytes 1146880
  (82 shorter events, 12.1 us)
Async XLA Ops:
  0.0 41.8 %copy-start = (bf16[16,512,128]{2,1,0:T(8,128)(2,1)S(1)}, bf16[16,512,128]{2,1,0:T(8,128)(2,1)}, u32[]{:S(2)}) copy-start(bf16[16,512,128]{2,1,0:T(8,128)(2,1)} %param.21) | copy-start | bytes 6291460
  3.2 13.0 %copy-start.6 = (s32[1,4]{1,0:T(1,128)S(1)}, s32[1,4]{1,0:T(1,128)}, u32[]{:S(2)}) copy-start(s32[1,4]{1,0:T(1,128)} %param.18) | copy-start | bytes 52
  3.2 34.2 %copy-start.3 = (bf16[8,576]{1,0:T(8,128)(2,1)S(1)}, bf16[8,576]{1,0:T(8,128)(2,1)}, u32[]{:S(2)}) copy-start(bf16[8,576]{1,0:T(8,128)(2,1)} %param.16) | copy-start | bytes 27652
  4.3 33.5 %copy-start.1 = (bf16[512,576]{0,1:T(8,128)(2,1)S(1)}, bf16[512,576]{0,1:T(8,128)(2,1)}, u32[]{:S(2)}) copy-start(bf16[512,576]{0,1:T(8,128)(2,1)} %param.17) | copy-start | bytes 1769476
  4.3 31.8 %all-to-all-start = ((bf16[32,1,16,576]{3,2,1,0:T(8,128)(2,1)}), bf16[32,1,16,576]{3,2,1,0:T(8,128)(2,1)S(1)}, u32[]{:S(2)}, u32[]{:S(2)}) async-start(bf16[32,1,16,576]{3,2,1,0:T(8,128)(2,1)} %copy.65), calls=%async_computation | async-start | bytes 1310720 | tf_op jit(solution)/shard_map/all_to_all | solution.py:80
  36.1 2.2 %collective-permute-start = (bf16[32,1,16,576]{3,2,1,0:T(8,128)(2,1)S(1)}, bf16[32,1,16,576]{3,2,1,0:T(8,128)(2,1)}, u32[]{:S(2)}, u32[]{:S(2)}) collective-permute-start(bf16[32,1,16,576]{3,2,1,0:T(8,128)(2,1)S(1)} %all-to-all-done), channel_id=1, source_target_pairs={{0,1},{1,0},{2,3},{3,2},{4,5},{5,4},{6,7},{7,6},{8,9},{9,8},{10,11... | collective-permute-start | bytes 1769480 | tf_op jit(solution)/shard_map/ppermute | solution.py:81
  43.4 5.2 %copy-start.5 = (s32[256,4]{0,1:T(4,128)S(1)}, s32[256,4]{0,1:T(4,128)}, u32[]{:S(2)}) copy-start(s32[256,4]{0,1:T(4,128)} %param.25) | copy-start | bytes 12292
  43.4 33.7 %all-to-all-start.1 = ((bf16[32,8,2048]{2,1,0:T(8,128)(2,1)}), bf16[32,8,2048]{2,1,0:T(8,128)(2,1)S(1)}, u32[]{:S(2)}, u32[]{:S(2)}) async-start(bf16[32,8,2048]{2,1,0:T(8,128)(2,1)} %broadcast_in_dim.95), calls=%async_computation.1 | async-start | bytes 2097152 | tf_op jit(solution)/shard_map/all_to_all | solution.py:158
  79.5 9.3 %all-to-all-start.2 = ((bf16[8,128,56]{1,2,0:T(8,128)(2,1)}), bf16[8,128,56]{1,2,0:T(8,128)(2,1)S(1)}, u32[]{:S(2)}, u32[]{:S(2)}) async-start(bf16[8,128,56]{1,2,0:T(8,128)(2,1)} %bitcast.26), calls=%async_computation.2 | async-start | bytes 229376 | tf_op jit(solution)/shard_map/all_to_all | solution.py:171
  129.1 2.9 %copy-start.2 = (f32[7168]{0:T(1024)S(1)}, f32[7168]{0:T(1024)}, u32[]{:S(2)}) copy-start(f32[7168]{0:T(1024)} %param.24) | copy-start | bytes 86020
  146.6 11.4 %copy-start.4 = (f32[256,4]{0,1:T(4,128)S(1)}, f32[256,4]{0,1:T(4,128)}, u32[]{:S(2)}) copy-start(f32[256,4]{0,1:T(4,128)} %param.26) | copy-start | bytes 12292
  150.3 26.8 %all-to-all-start.4 = ((bf16[128,2,1120]{2,1,0:T(2,128)(2,1)}), bf16[128,2,1120]{2,1,0:T(2,128)(2,1)}, u32[]{:S(2)}, u32[]{:S(2)}) async-start(bf16[128,2,1120]{2,1,0:T(2,128)(2,1)} %reshape.450), calls=%async_computation.4 | async-start | bytes 1179648 | tf_op jit(solution)/shard_map/all_to_all | solution.py:199

commit v3 on v2

--- a/solution.py
+++ b/solution.py
@@ -192,10 +192,11 @@
     gate_proj = jnp.dot(normed, w_gate, preferred_element_type=jnp.float32)
     up_proj = jnp.dot(normed, w_up, preferred_element_type=jnp.float32)
     activated = (jax.nn.silu(gate_proj) * up_proj).astype(jnp.bfloat16)
-    result = jnp.dot(activated, w_down, preferred_element_type=jnp.float32)
-
     n_dev = n_attn * n_expert
-    back = result.astype(jnp.bfloat16).reshape(capacity, n_dev, sub_cols).transpose(1, 0, 2)
+    down_blocks = w_down.reshape(w_down.shape[0], n_dev, sub_cols).transpose(1, 0, 2)
+    back = jnp.einsum(
+        "ku,duc->dkc", activated, down_blocks, preferred_element_type=jnp.float32
+    ).astype(jnp.bfloat16)
     returned = lax.all_to_all(back, ("attn", "expert"), split_axis=0, concat_axis=0, tiled=True)
     summed = jnp.sum(
         returned.astype(jnp.float32).reshape(EXPERTS, shards, capacity, sub_cols), axis=1

time: 183 us -> 180 us (0.984)
  blocking collectives: 30.1 us -> 0 us
  waiting for transfers between devices: 70.9 us -> 85.9 us
  starting transfers between devices: 29.2 us -> 38.5 us
  local copies, waits for them, and re-layouts: 29.9 us -> 31.8 us
    all_to_all x1 -> x0, blocking collectives: 30.1 us -> none  [per_device(): lax.all_to_all(send_rows, ('attn', 'expert'), split_axis=0, concat_axis=0...]
    all_to_all x0 -> x1, waiting for transfers between devices: none -> 15.1 us  [per_device(): lax.all_to_all(send_rows, ('attn', 'expert'), split_axis=0, concat_axis=0...]
    all_to_all x0 -> x1, starting transfers between devices: none -> 9.02 us  [per_device(): lax.all_to_all(send_rows, ('attn', 'expert'), split_axis=0, concat_axis=0...]
    unnamed x19 -> x20, local copies, waits for them, and re-layouts: 13.5 us -> 18.7 us
    reshape x1 -> x0, local copies, waits for them, and re-layouts: 3.7 us -> none  [per_device(): result.astype(jnp.bfloat16).reshape(capacity, n_dev, sub_cols)]
    convert_element_type x0 -> x1, local copies, waits for them, and re-layouts: none -> 2.34 us  [per_device(): back = jnp.einsum('ku,duc->dkc', activated, down_blocks, preferred_elemen...]
    transpose x1 -> x0, local copies, waits for them, and re-layouts: 1.91 us -> none  [per_device(): result.astype(jnp.bfloat16).reshape(capacity, n_dev, sub_cols)]
  transfers between devices with their start and end apart: 5 -> 6, of which waited for: 5 -> 6; matrix products, arithmetic and copies ran while one was open for 2% -> 5% of each run, Pallas kernels for 0% -> 0%
where the time goes in v3:
time: 180 us; the launch traced here: 179 us
  waiting for transfers between devices  85.9 us (48%)
  starting transfers between devices  38.5 us (21%)
  local copies, waits for them, and re-layouts  31.8 us (18%)
  matrix products  16.6 us (9%)
  other arithmetic  5.28 us (3%)
    all_to_all x1, waiting for transfers between devices, per_device(): lax.all_to_all(spread, 'attn', split_axis=0, concat_axis=0, tiled=True)  28.2 us
    all_to_all x1, waiting for transfers between devices, per_device(): lax.all_to_all(outgoing, 'attn', split_axis=0, concat_axis=0, tiled=True)  19.2 us
    unnamed x20, local copies, waits for them, and re-layouts  18.7 us
    all_to_all x1, waiting for transfers between devices, per_device(): lax.all_to_all(back, ('attn', 'expert'), split_axis=0, concat_axis=0, til...  18.7 us
    all_to_all x1, waiting for transfers between devices, per_device(): lax.all_to_all(send_rows, ('attn', 'expert'), split_axis=0, concat_axis=0...  15.1 us
    all_to_all x1, starting transfers between devices, per_device(): lax.all_to_all(outgoing, 'attn', split_axis=0, concat_axis=0, tiled=True)  11.6 us
    all_to_all x1, starting transfers between devices, per_device(): lax.all_to_all(send_rows, ('attn', 'expert'), split_axis=0, concat_axis=0...  9.02 us
    all_to_all x1, starting transfers between devices, per_device(): lax.all_to_all(back, ('attn', 'expert'), split_axis=0, concat_axis=0, til...  7.84 us
  transfers between devices with their start and end apart: 6, of which 6 were waited for; matrix products, arithmetic and copies ran while one was open for 5% of the time, Pallas kernels for 0%

profile of v3, /device:TPU:2, one launch (start us, length us, event | category | flops | bytes accessed | tf_op | source)
XLA Modules:
  0.0 178.5 jit_solution(10811265917862493970)
XLA Ops:
  1.8 1.4 fusion.8
  4.3 11.6 %all-to-all-start = ((bf16[32,1,16,576]{3,2,1,0:T(8,128)(2,1)}), bf16[32,1,16,576]{3,2,1,0:T(8,128)(2,1)S(1)}, u32[]{:S(2)}, u32[]{:S(2)}) async-start(bf16[32,1,16,576]{3,2,1,0:T(8,128)(2,1)} %copy.69), calls=%async_computation | async-start | bytes 1310720 | tf_op jit(solution)/shard_map/all_to_all | solution.py:80
  16.9 19.2 %all-to-all-done = bf16[32,1,16,576]{3,2,1,0:T(8,128)(2,1)S(1)} async-done(((bf16[32,1,16,576]{3,2,1,0:T(8,128)(2,1)}), bf16[32,1,16,576]{3,2,1,0:T(8,128)(2,1)S(1)}, u32[]{:S(2)}, u32[]{:S(2)}) %all-to-all-start) | async-done | bytes 589856 | tf_op jit(solution)/shard_map/all_to_all | solution.py:80
  38.4 1.2 broadcast_select_fusion.1
  43.4 5.1 %all-to-all-start.1 = ((bf16[32,8,2048]{2,1,0:T(8,128)(2,1)}), bf16[32,8,2048]{2,1,0:T(8,128)(2,1)S(1)}, u32[]{:S(2)}, u32[]{:S(2)}) async-start(bf16[32,8,2048]{2,1,0:T(8,128)(2,1)} %broadcast_in_dim.95), calls=%async_computation.1 | async-start | bytes 2097152 | tf_op jit(solution)/shard_map/all_to_all | solution.py:158
  48.9 28.2 %all-to-all-done.1 = bf16[32,8,2048]{2,1,0:T(8,128)(2,1)S(1)} async-done(((bf16[32,8,2048]{2,1,0:T(8,128)(2,1)}), bf16[32,8,2048]{2,1,0:T(8,128)(2,1)S(1)}, u32[]{:S(2)}, u32[]{:S(2)}) %all-to-all-start.1) | async-done | bytes 1048608 | tf_op jit(solution)/shard_map/all_to_all | solution.py:158
  77.1 1.7 convolution_convert_fusion.2
  79.5 4.8 %all-to-all-start.2 = ((bf16[8,128,56]{1,2,0:T(8,128)(2,1)}), bf16[8,128,56]{1,2,0:T(8,128)(2,1)S(1)}, u32[]{:S(2)}, u32[]{:S(2)}) async-start(bf16[8,128,56]{1,2,0:T(8,128)(2,1)} %bitcast.26), calls=%async_computation.2 | async-start | bytes 229376 | tf_op jit(solution)/shard_map/all_to_all | solution.py:171
  84.4 4.4 %all-to-all-done.2 = bf16[8,128,56]{1,2,0:T(8,128)(2,1)S(1)} async-done(((bf16[8,128,56]{1,2,0:T(8,128)(2,1)}), bf16[8,128,56]{1,2,0:T(8,128)(2,1)S(1)}, u32[]{:S(2)}, u32[]{:S(2)}) %all-to-all-start.2) | async-done | bytes 114720 | tf_op jit(solution)/shard_map/all_to_all | solution.py:171
  90.0 3.1 %reshape.449 = bf16[128,2,1120]{2,1,0:T(2,128)(2,1)} reshape(bf16[128,40,56]{2,1,0:T(8,128)(2,1)S(1)} %bitcast.120) | data formatting | bytes 1146880
  93.0 9.0 %all-to-all-start.3 = ((bf16[128,2,1120]{2,1,0:T(2,128)(2,1)}), bf16[128,2,1120]{2,1,0:T(2,128)(2,1)}, u32[]{:S(2)}, u32[]{:S(2)}) async-start(bf16[128,2,1120]{2,1,0:T(2,128)(2,1)} %reshape.449), calls=%async_computation.3 | async-start | bytes 1179648 | tf_op jit(solution)/shard_map/all_to_all | solution.py:186
  102.0 5.9 %copy.78 = bf16[256,7168]{0,1:T(8,128)(2,1)} copy(bf16[256,7168]{1,0:T(8,128)(2,1)} %param.29) | data formatting | bytes 7340032 | tf_op args[14]
  108.0 15.1 %all-to-all-done.3 = bf16[128,2,1120]{2,1,0:T(2,128)(2,1)} async-done(((bf16[128,2,1120]{2,1,0:T(2,128)(2,1)}), bf16[128,2,1120]{2,1,0:T(2,128)(2,1)}, u32[]{:S(2)}, u32[]{:S(2)}) %all-to-all-start.3) | async-done | bytes 573472 | tf_op jit(solution)/shard_map/all_to_all | solution.py:186
  123.1 3.3 %reshape.450 = bf16[128,40,56]{2,1,0:T(8,128)(2,1)S(1)} reshape(bf16[128,2,1120]{2,1,0:T(2,128)(2,1)} %all-to-all-done.3) | data formatting | bytes 1146880
  127.1 2.0 %copy.77 = f32[40,128,56]{2,1,0:T(8,128)} copy(f32[40,128,56]{2,0,1:T(8,128)S(1)} %convert_bitcast_fusion) | data formatting | bytes 2293760 | tf_op jit(solution)/shard_map/convert_element_type | solution.py:188
  129.1 2.9 %reshape.435 = f32[40,7168]{1,0:T(8,128)S(1)} reshape(f32[40,128,56]{2,1,0:T(8,128)} %copy.77) | data formatting | bytes 2293760 | tf_op jit(solution)/shard_map/convert_element_type | solution.py:188
  132.0 2.8 %fusion.83 = f32[40,256]{1,0:T(8,128)S(1)} fusion(bf16[7168,256]{1,0:T(8,128)(2,1)} %param.27, f32[40,7168]{1,0:T(8,128)S(1)} %reshape.435, f32[7168]{0:T(1024)S(1)} %copy-done.2, f32[40]{0:T(128)S(1)} %add_rsqrt_fusion), kind=kOutput, calls=%fused_computation.133 | convolution fusion | flops 147660800 | bytes 4886688 | tf_op jit(solution)/shard_map/dot_general | solution.py:192
  134.9 6.7 %fusion.9 = bf16[128,40,56]{0,1,2:T(8,128)(2,1)} fusion(bf16[128,256,56]{1,2,0:T(8,128)(2,1)} %bitcast.119, bf16[7168,256]{1,0:T(8,128)(2,1)} %param.28, f32[40,256]{1,0:T(8,128)S(1)} %fusion.83, f32[40,7168]{1,0:T(8,128)S(1)} %reshape.435, f32[7168]{0:T(1024)S(1)} %copy-done.2, f32[40]{0:T(128)S(1)} %add_rsqrt_fusion), kind=kOutput, calls=%fused_computation.12 | convolution fusion | flops 294809600 | bytes 9130144 | tf_op jit(solution)/shard_map/ku,duc->dkc/dot_general | solution.py:197
  141.5 2.3 %copy.80 = bf16[128,40,56]{2,1,0:T(8,128)(2,1)S(1)} copy(bf16[128,40,56]{0,1,2:T(8,128)(2,1)} %fusion.9) | data formatting | bytes 1146880 | tf_op jit(solution)/shard_map/convert_element_type | solution.py:199
  143.9 3.0 %reshape.451 = bf16[128,2,1120]{2,1,0:T(2,128)(2,1)} reshape(bf16[128,40,56]{2,1,0:T(8,128)(2,1)S(1)} %copy.80) | data formatting | bytes 1146880
  146.9 7.8 %all-to-all-start.4 = ((bf16[128,2,1120]{2,1,0:T(2,128)(2,1)}), bf16[128,2,1120]{2,1,0:T(2,128)(2,1)}, u32[]{:S(2)}, u32[]{:S(2)}) async-start(bf16[128,2,1120]{2,1,0:T(2,128)(2,1)} %reshape.451), calls=%async_computation.4 | async-start | bytes 1179648 | tf_op jit(solution)/shard_map/all_to_all | solution.py:200
  155.0 18.7 %all-to-all-done.4 = bf16[128,2,1120]{2,1,0:T(2,128)(2,1)} async-done(((bf16[128,2,1120]{2,1,0:T(2,128)(2,1)}), bf16[128,2,1120]{2,1,0:T(2,128)(2,1)}, u32[]{:S(2)}, u32[]{:S(2)}) %all-to-all-start.4) | async-done | bytes 573472 | tf_op jit(solution)/shard_map/all_to_all | solution.py:200
  173.8 3.3 %reshape.452 = bf16[128,40,56]{2,1,0:T(8,128)(2,1)S(1)} reshape(bf16[128,2,1120]{2,1,0:T(2,128)(2,1)} %all-to-all-done.4) | data formatting | bytes 1146880
  177.4 1.2 fusion.27
  (81 shorter events, 13.0 us)
Async XLA Ops:
  0.0 41.8 %copy-start = (bf16[16,512,128]{2,1,0:T(8,128)(2,1)S(1)}, bf16[16,512,128]{2,1,0:T(8,128)(2,1)}, u32[]{:S(2)}) copy-start(bf16[16,512,128]{2,1,0:T(8,128)(2,1)} %param.21) | copy-start | bytes 6291460
  3.2 13.0 %copy-start.6 = (s32[1,4]{1,0:T(1,128)S(1)}, s32[1,4]{1,0:T(1,128)}, u32[]{:S(2)}) copy-start(s32[1,4]{1,0:T(1,128)} %param.18) | copy-start | bytes 52
  3.2 34.2 %copy-start.3 = (bf16[8,576]{1,0:T(8,128)(2,1)S(1)}, bf16[8,576]{1,0:T(8,128)(2,1)}, u32[]{:S(2)}) copy-start(bf16[8,576]{1,0:T(8,128)(2,1)} %param.16) | copy-start | bytes 27652
  4.3 33.5 %copy-start.1 = (bf16[512,576]{0,1:T(8,128)(2,1)S(1)}, bf16[512,576]{0,1:T(8,128)(2,1)}, u32[]{:S(2)}) copy-start(bf16[512,576]{0,1:T(8,128)(2,1)} %param.17) | copy-start | bytes 1769476
  4.3 31.8 %all-to-all-start = ((bf16[32,1,16,576]{3,2,1,0:T(8,128)(2,1)}), bf16[32,1,16,576]{3,2,1,0:T(8,128)(2,1)S(1)}, u32[]{:S(2)}, u32[]{:S(2)}) async-start(bf16[32,1,16,576]{3,2,1,0:T(8,128)(2,1)} %copy.69), calls=%async_computation | async-start | bytes 1310720 | tf_op jit(solution)/shard_map/all_to_all | solution.py:80
  36.1 2.2 %collective-permute-start = (bf16[32,1,16,576]{3,2,1,0:T(8,128)(2,1)S(1)}, bf16[32,1,16,576]{3,2,1,0:T(8,128)(2,1)}, u32[]{:S(2)}, u32[]{:S(2)}) collective-permute-start(bf16[32,1,16,576]{3,2,1,0:T(8,128)(2,1)S(1)} %all-to-all-done), channel_id=1, source_target_pairs={{0,1},{1,0},{2,3},{3,2},{4,5},{5,4},{6,7},{7,6},{8,9},{9,8},{10,11... | collective-permute-start | bytes 1769480 | tf_op jit(solution)/shard_map/ppermute | solution.py:81
  43.4 5.2 %copy-start.5 = (s32[256,4]{0,1:T(4,128)S(1)}, s32[256,4]{0,1:T(4,128)}, u32[]{:S(2)}) copy-start(s32[256,4]{0,1:T(4,128)} %param.25) | copy-start | bytes 12292
  43.4 33.7 %all-to-all-start.1 = ((bf16[32,8,2048]{2,1,0:T(8,128)(2,1)}), bf16[32,8,2048]{2,1,0:T(8,128)(2,1)S(1)}, u32[]{:S(2)}, u32[]{:S(2)}) async-start(bf16[32,8,2048]{2,1,0:T(8,128)(2,1)} %broadcast_in_dim.95), calls=%async_computation.1 | async-start | bytes 2097152 | tf_op jit(solution)/shard_map/all_to_all | solution.py:158
  79.5 9.3 %all-to-all-start.2 = ((bf16[8,128,56]{1,2,0:T(8,128)(2,1)}), bf16[8,128,56]{1,2,0:T(8,128)(2,1)S(1)}, u32[]{:S(2)}, u32[]{:S(2)}) async-start(bf16[8,128,56]{1,2,0:T(8,128)(2,1)} %bitcast.26), calls=%async_computation.2 | async-start | bytes 229376 | tf_op jit(solution)/shard_map/all_to_all | solution.py:171
  93.0 30.1 %all-to-all-start.3 = ((bf16[128,2,1120]{2,1,0:T(2,128)(2,1)}), bf16[128,2,1120]{2,1,0:T(2,128)(2,1)}, u32[]{:S(2)}, u32[]{:S(2)}) async-start(bf16[128,2,1120]{2,1,0:T(2,128)(2,1)} %reshape.449), calls=%async_computation.3 | async-start | bytes 1179648 | tf_op jit(solution)/shard_map/all_to_all | solution.py:186
  129.1 2.9 %copy-start.2 = (f32[7168]{0:T(1024)S(1)}, f32[7168]{0:T(1024)}, u32[]{:S(2)}) copy-start(f32[7168]{0:T(1024)} %param.24) | copy-start | bytes 86020
  143.9 10.9 %copy-start.4 = (f32[256,4]{0,1:T(4,128)S(1)}, f32[256,4]{0,1:T(4,128)}, u32[]{:S(2)}) copy-start(f32[256,4]{0,1:T(4,128)} %param.26) | copy-start | bytes 12292
  146.9 26.8 %all-to-all-start.4 = ((bf16[128,2,1120]{2,1,0:T(2,128)(2,1)}), bf16[128,2,1120]{2,1,0:T(2,128)(2,1)}, u32[]{:S(2)}, u32[]{:S(2)}) async-start(bf16[128,2,1120]{2,1,0:T(2,128)(2,1)} %reshape.451), calls=%async_computation.4 | async-start | bytes 1179648 | tf_op jit(solution)/shard_map/all_to_all | solution.py:200

commit v4 on v3

--- a/solution.py
+++ b/solution.py
@@ -184,13 +184,17 @@
     ).astype(jnp.bfloat16)
     send_rows = jnp.repeat(rows_e, shards, axis=0)
     recv_rows = lax.all_to_all(send_rows, ("attn", "expert"), split_axis=0, concat_axis=0, tiled=True)
-    full_rows = recv_rows.transpose(1, 0, 2).reshape(capacity, -1)
-    widened = full_rows.astype(jnp.float32)
+    n_src = recv_rows.shape[0]
+    widened = recv_rows.astype(jnp.float32)
+    mean_sq = jnp.sum(widened * widened, axis=(0, 2)) / (n_src * sub_cols)
+    inv = lax.rsqrt(mean_sq + 1e-06)
     normed = (
-        widened * lax.rsqrt(jnp.mean(widened * widened, axis=1, keepdims=True) + 1e-06) * norm_gain
-    ).astype(jnp.bfloat16)
-    gate_proj = jnp.dot(normed, w_gate, preferred_element_type=jnp.float32)
-    up_proj = jnp.dot(normed, w_up, preferred_element_type=jnp.float32)
+        widened * inv[None, :, None] * norm_gain.reshape(n_src, 1, sub_cols)
+    ).astype(jnp.bfloat16)
+    gate_blocks = w_gate.reshape(n_src, sub_cols, w_gate.shape[1])
+    up_blocks = w_up.reshape(n_src, sub_cols, w_up.shape[1])
+    gate_proj = jnp.einsum("skc,scu->ku", normed, gate_blocks, preferred_element_type=jnp.float32)
+    up_proj = jnp.einsum("skc,scu->ku", normed, up_blocks, preferred_element_type=jnp.float32)
     activated = (jax.nn.silu(gate_proj) * up_proj).astype(jnp.bfloat16)
     n_dev = n_attn * n_expert
     down_blocks = w_down.reshape(w_down.shape[0], n_dev, sub_cols).transpose(1, 0, 2)

time: 180 us -> 175 us (0.972)
  local copies, waits for them, and re-layouts: 31.8 us -> 27 us
    convert_element_type x2 -> x0, local copies, waits for them, and re-layouts: 4.88 us -> none  [per_device(): widened = full_rows.astype(jnp.float32)]
where the time goes in v4:
time: 175 us; the launch traced here: 174 us
  waiting for transfers between devices  86 us (49%)
  starting transfers between devices  38 us (22%)
  local copies, waits for them, and re-layouts  27 us (15%)
  matrix products  17.1 us (10%)
  other arithmetic  5.11 us (3%)
    all_to_all x1, waiting for transfers between devices, per_device(): lax.all_to_all(spread, 'attn', split_axis=0, concat_axis=0, tiled=True)  28.2 us
    all_to_all x1, waiting for transfers between devices, per_device(): lax.all_to_all(outgoing, 'attn', split_axis=0, concat_axis=0, tiled=True)  19.2 us
    all_to_all x1, waiting for transfers between devices, per_device(): lax.all_to_all(back, ('attn', 'expert'), split_axis=0, concat_axis=0, til...  18.9 us
    unnamed x20, local copies, waits for them, and re-layouts  18.8 us
    all_to_all x1, waiting for transfers between devices, per_device(): lax.all_to_all(send_rows, ('attn', 'expert'), split_axis=0, concat_axis=0...  15 us
    all_to_all x1, starting transfers between devices, per_device(): lax.all_to_all(outgoing, 'attn', split_axis=0, concat_axis=0, tiled=True)  11.5 us
    all_to_all x1, starting transfers between devices, per_device(): lax.all_to_all(send_rows, ('attn', 'expert'), split_axis=0, concat_axis=0...  9.02 us
    all_to_all x1, starting transfers between devices, per_device(): lax.all_to_all(back, ('attn', 'expert'), split_axis=0, concat_axis=0, til...  7.64 us
  transfers between devices with their start and end apart: 6, of which 6 were waited for; matrix products, arithmetic and copies ran while one was open for 5% of the time, Pallas kernels for 0%

profile of v4, /device:TPU:2, one launch (start us, length us, event | category | flops | bytes accessed | tf_op | source)
XLA Modules:
  0.0 173.7 jit_solution(9007405130427952987)
XLA Ops:
  1.8 1.5 fusion.10
  4.4 11.5 %all-to-all-start = ((bf16[32,1,16,576]{3,2,1,0:T(8,128)(2,1)}), bf16[32,1,16,576]{3,2,1,0:T(8,128)(2,1)S(1)}, u32[]{:S(2)}, u32[]{:S(2)}) async-start(bf16[32,1,16,576]{3,2,1,0:T(8,128)(2,1)} %copy.70), calls=%async_computation | async-start | bytes 1310720 | tf_op jit(solution)/shard_map/all_to_all | solution.py:80
  16.8 19.2 %all-to-all-done = bf16[32,1,16,576]{3,2,1,0:T(8,128)(2,1)S(1)} async-done(((bf16[32,1,16,576]{3,2,1,0:T(8,128)(2,1)}), bf16[32,1,16,576]{3,2,1,0:T(8,128)(2,1)S(1)}, u32[]{:S(2)}, u32[]{:S(2)}) %all-to-all-start) | async-done | bytes 589856 | tf_op jit(solution)/shard_map/all_to_all | solution.py:80
  36.3 1.1 reshape.425
  38.3 1.2 broadcast_select_fusion.1
  42.3 1.1 broadcast_in_dim.140
  43.4 5.0 %all-to-all-start.1 = ((bf16[32,8,2048]{2,1,0:T(8,128)(2,1)}), bf16[32,8,2048]{2,1,0:T(8,128)(2,1)S(1)}, u32[]{:S(2)}, u32[]{:S(2)}) async-start(bf16[32,8,2048]{2,1,0:T(8,128)(2,1)} %broadcast_in_dim.140), calls=%async_computation.1 | async-start | bytes 2097152 | tf_op jit(solution)/shard_map/all_to_all | solution.py:158
  48.7 28.2 %all-to-all-done.1 = bf16[32,8,2048]{2,1,0:T(8,128)(2,1)S(1)} async-done(((bf16[32,8,2048]{2,1,0:T(8,128)(2,1)}), bf16[32,8,2048]{2,1,0:T(8,128)(2,1)S(1)}, u32[]{:S(2)}, u32[]{:S(2)}) %all-to-all-start.1) | async-done | bytes 1048608 | tf_op jit(solution)/shard_map/all_to_all | solution.py:158
  76.9 1.7 convolution_convert_fusion.2
  79.3 4.8 %all-to-all-start.2 = ((bf16[8,128,56]{1,2,0:T(8,128)(2,1)}), bf16[8,128,56]{1,2,0:T(8,128)(2,1)S(1)}, u32[]{:S(2)}, u32[]{:S(2)}) async-start(bf16[8,128,56]{1,2,0:T(8,128)(2,1)} %bitcast.26), calls=%async_computation.2 | async-start | bytes 229376 | tf_op jit(solution)/shard_map/all_to_all | solution.py:171
  84.2 4.4 %all-to-all-done.2 = bf16[8,128,56]{1,2,0:T(8,128)(2,1)S(1)} async-done(((bf16[8,128,56]{1,2,0:T(8,128)(2,1)}), bf16[8,128,56]{1,2,0:T(8,128)(2,1)S(1)}, u32[]{:S(2)}, u32[]{:S(2)}) %all-to-all-start.2) | async-done | bytes 114720 | tf_op jit(solution)/shard_map/all_to_all | solution.py:171
  89.8 3.1 %reshape.453 = bf16[128,2,1120]{2,1,0:T(2,128)(2,1)} reshape(bf16[128,40,56]{2,1,0:T(8,128)(2,1)S(1)} %bitcast.132) | data formatting | bytes 1146880
  92.8 9.0 %all-to-all-start.3 = ((bf16[128,2,1120]{2,1,0:T(2,128)(2,1)}), bf16[128,2,1120]{2,1,0:T(2,128)(2,1)}, u32[]{:S(2)}, u32[]{:S(2)}) async-start(bf16[128,2,1120]{2,1,0:T(2,128)(2,1)} %reshape.453), calls=%async_computation.3 | async-start | bytes 1179648 | tf_op jit(solution)/shard_map/all_to_all | solution.py:186
  102.0 5.9 %copy.78 = bf16[256,7168]{0,1:T(8,128)(2,1)} copy(bf16[256,7168]{1,0:T(8,128)(2,1)} %param.29) | data formatting | bytes 7340032 | tf_op args[14]
  107.9 15.0 %all-to-all-done.3 = bf16[128,2,1120]{2,1,0:T(2,128)(2,1)} async-done(((bf16[128,2,1120]{2,1,0:T(2,128)(2,1)}), bf16[128,2,1120]{2,1,0:T(2,128)(2,1)}, u32[]{:S(2)}, u32[]{:S(2)}) %all-to-all-start.3) | async-done | bytes 573472 | tf_op jit(solution)/shard_map/all_to_all | solution.py:186
  122.9 3.3 %reshape.454 = bf16[128,40,56]{2,1,0:T(8,128)(2,1)S(1)} reshape(bf16[128,2,1120]{2,1,0:T(2,128)(2,1)} %all-to-all-done.3) | data formatting | bytes 1146880
  126.7 3.0 %convolution_bitcast_fusion.1 = f32[40,256]{1,0:T(8,128)S(1)} fusion(bf16[128,56,256]{2,1,0:T(8,128)(2,1)} %bitcast.156, bf16[128,40,56]{2,1,0:T(8,128)(2,1)S(1)} %reshape.454, f32[128,56]{1,0:T(8,128)S(1)} %mul.94, f32[40]{0:T(128)S(1)} %add_rsqrt_fusion), kind=kOutput, calls=%fused_computation.29 | convolution fusion | flops 147947520 | bytes 4313248 | tf_op jit(solution)/shard_map/skc,scu->ku/dot_general | solution.py:196
  129.7 7.0 %fusion.11 = bf16[128,40,56]{0,1,2:T(8,128)(2,1)} fusion(bf16[128,256,56]{1,2,0:T(8,128)(2,1)} %bitcast.131, bf16[128,56,256]{2,1,0:T(8,128)(2,1)} %bitcast.135, bf16[128,40,56]{2,1,0:T(8,128)(2,1)S(1)} %reshape.454, f32[128,56]{1,0:T(8,128)S(1)} %mul.94, f32[40]{0:T(128)S(1)} %add_rsqrt_fusion, f32[40,256]{1,0:T(8,128)S(1)} %convolution_bitcast_fusion.1), kind=kOutput, calls=%fused_computation.14 | convolution fusion | flops 295096320 | bytes 8556704 | tf_op jit(solution)/shard_map/ku,duc->dkc/dot_general | solution.py:201
  136.7 2.4 %copy.80 = bf16[128,40,56]{2,1,0:T(8,128)(2,1)S(1)} copy(bf16[128,40,56]{0,1,2:T(8,128)(2,1)} %fusion.11) | data formatting | bytes 1146880 | tf_op jit(solution)/shard_map/convert_element_type | solution.py:203
  139.0 3.0 %reshape.455 = bf16[128,2,1120]{2,1,0:T(2,128)(2,1)} reshape(bf16[128,40,56]{2,1,0:T(8,128)(2,1)S(1)} %copy.80) | data formatting | bytes 1146880
  142.1 7.6 %all-to-all-start.4 = ((bf16[128,2,1120]{2,1,0:T(2,128)(2,1)}), bf16[128,2,1120]{2,1,0:T(2,128)(2,1)}, u32[]{:S(2)}, u32[]{:S(2)}) async-start(bf16[128,2,1120]{2,1,0:T(2,128)(2,1)} %reshape.455), calls=%async_computation.4 | async-start | bytes 1179648 | tf_op jit(solution)/shard_map/all_to_all | solution.py:204
  150.0 18.9 %all-to-all-done.4 = bf16[128,2,1120]{2,1,0:T(2,128)(2,1)} async-done(((bf16[128,2,1120]{2,1,0:T(2,128)(2,1)}), bf16[128,2,1120]{2,1,0:T(2,128)(2,1)}, u32[]{:S(2)}, u32[]{:S(2)}) %all-to-all-start.4) | async-done | bytes 573472 | tf_op jit(solution)/shard_map/all_to_all | solution.py:204
  168.9 3.3 %reshape.456 = bf16[128,40,56]{2,1,0:T(8,128)(2,1)S(1)} reshape(bf16[128,2,1120]{2,1,0:T(2,128)(2,1)} %all-to-all-done.4) | data formatting | bytes 1146880
  172.5 1.2 fusion.30
  (79 shorter events, 10.7 us)
Async XLA Ops:
  0.0 41.8 %copy-start = (bf16[16,512,128]{2,1,0:T(8,128)(2,1)S(1)}, bf16[16,512,128]{2,1,0:T(8,128)(2,1)}, u32[]{:S(2)}) copy-start(bf16[16,512,128]{2,1,0:T(8,128)(2,1)} %param.21) | copy-start | bytes 6291460
  0.9 15.6 %copy-start.6 = (s32[1,4]{1,0:T(1,128)S(1)}, s32[1,4]{1,0:T(1,128)}, u32[]{:S(2)}) copy-start(s32[1,4]{1,0:T(1,128)} %param.18) | copy-start | bytes 52
  1.8 35.6 %copy-start.3 = (bf16[8,576]{1,0:T(8,128)(2,1)S(1)}, bf16[8,576]{1,0:T(8,128)(2,1)}, u32[]{:S(2)}) copy-start(bf16[8,576]{1,0:T(8,128)(2,1)} %param.16) | copy-start | bytes 27652
  1.8 35.9 %copy-start.1 = (bf16[512,576]{0,1:T(8,128)(2,1)S(1)}, bf16[512,576]{0,1:T(8,128)(2,1)}, u32[]{:S(2)}) copy-start(bf16[512,576]{0,1:T(8,128)(2,1)} %param.17) | copy-start | bytes 1769476
  4.4 31.7 %all-to-all-start = ((bf16[32,1,16,576]{3,2,1,0:T(8,128)(2,1)}), bf16[32,1,16,576]{3,2,1,0:T(8,128)(2,1)S(1)}, u32[]{:S(2)}, u32[]{:S(2)}) async-start(bf16[32,1,16,576]{3,2,1,0:T(8,128)(2,1)} %copy.70), calls=%async_computation | async-start | bytes 1310720 | tf_op jit(solution)/shard_map/all_to_all | solution.py:80
  36.1 2.2 %collective-permute-start = (bf16[32,1,16,576]{3,2,1,0:T(8,128)(2,1)S(1)}, bf16[32,1,16,576]{3,2,1,0:T(8,128)(2,1)}, u32[]{:S(2)}, u32[]{:S(2)}) collective-permute-start(bf16[32,1,16,576]{3,2,1,0:T(8,128)(2,1)S(1)} %all-to-all-done), channel_id=1, source_target_pairs={{0,1},{1,0},{2,3},{3,2},{4,5},{5,4},{6,7},{7,6},{8,9},{9,8},{10,11... | collective-permute-start | bytes 1769480 | tf_op jit(solution)/shard_map/ppermute | solution.py:81
  42.2 6.2 %copy-start.5 = (s32[256,4]{0,1:T(4,128)S(1)}, s32[256,4]{0,1:T(4,128)}, u32[]{:S(2)}) copy-start(s32[256,4]{0,1:T(4,128)} %param.25) | copy-start | bytes 12292
  43.4 33.6 %all-to-all-start.1 = ((bf16[32,8,2048]{2,1,0:T(8,128)(2,1)}), bf16[32,8,2048]{2,1,0:T(8,128)(2,1)S(1)}, u32[]{:S(2)}, u32[]{:S(2)}) async-start(bf16[32,8,2048]{2,1,0:T(8,128)(2,1)} %broadcast_in_dim.140), calls=%async_computation.1 | async-start | bytes 2097152 | tf_op jit(solution)/shard_map/all_to_all | solution.py:158
  79.3 9.3 %all-to-all-start.2 = ((bf16[8,128,56]{1,2,0:T(8,128)(2,1)}), bf16[8,128,56]{1,2,0:T(8,128)(2,1)S(1)}, u32[]{:S(2)}, u32[]{:S(2)}) async-start(bf16[8,128,56]{1,2,0:T(8,128)(2,1)} %bitcast.26), calls=%async_computation.2 | async-start | bytes 229376 | tf_op jit(solution)/shard_map/all_to_all | solution.py:171
  89.6 12.3 %copy-start.2 = (f32[7168]{0:T(1024)S(1)}, f32[7168]{0:T(1024)}, u32[]{:S(2)}) copy-start(f32[7168]{0:T(1024)} %param.24) | copy-start | bytes 86020
  92.8 30.1 %all-to-all-start.3 = ((bf16[128,2,1120]{2,1,0:T(2,128)(2,1)}), bf16[128,2,1120]{2,1,0:T(2,128)(2,1)}, u32[]{:S(2)}, u32[]{:S(2)}) async-start(bf16[128,2,1120]{2,1,0:T(2,128)(2,1)} %reshape.453), calls=%async_computation.3 | async-start | bytes 1179648 | tf_op jit(solution)/shard_map/all_to_all | solution.py:186
  136.7 13.1 %copy-start.4 = (f32[256,4]{0,1:T(4,128)S(1)}, f32[256,4]{0,1:T(4,128)}, u32[]{:S(2)}) copy-start(f32[256,4]{0,1:T(4,128)} %param.26) | copy-start | bytes 12292
  142.1 26.8 %all-to-all-start.4 = ((bf16[128,2,1120]{2,1,0:T(2,128)(2,1)}), bf16[128,2,1120]{2,1,0:T(2,128)(2,1)}, u32[]{:S(2)}, u32[]{:S(2)}) async-start(bf16[128,2,1120]{2,1,0:T(2,128)(2,1)} %reshape.455), calls=%async_computation.4 | async-start | bytes 1179648 | tf_op jit(solution)/shard_map/all_to_all | solution.py:204

commit v5 on v4

--- a/solution.py
+++ b/solution.py
@@ -59,37 +59,32 @@
 
     spill_count = spill_cache.shape[0]
     blk = spill_cache.shape[1]
-    directory = spill_owner.reshape(n_attn, spill_count)
-    owner_dev = jnp.where(directory >= 0, directory // req_count, -1)
     earlier = jnp.arange(spill_count)[:, None] > jnp.arange(spill_count)[None, :]
-    same_owner = owner_dev[:, :, None] == owner_dev[:, None, :]
-    order_rank = jnp.sum(same_owner & earlier[None, :, :], axis=2)
-    slot_ids = jnp.arange(CAP)
-    own_row = owner_dev[attn_here]
-    own_rank = order_rank[attn_here]
-    pick_slot = (own_row[None, None, :] == jnp.arange(n_attn)[:, None, None]) & (
-        own_rank[None, None, :] == slot_ids[None, :, None]
-    )
-    my_slot = lax.dynamic_slice_in_dim(pick_slot, rep_here, 1, 1)
+    own_ids = lax.dynamic_slice_in_dim(spill_owner, attn_here * spill_count, spill_count, 0)
+    own_row = jnp.where(own_ids >= 0, own_ids // req_count, -1)
+    own_rank = jnp.sum((own_row[:, None] == own_row[None, :]) & earlier, axis=1)
+    my_slot = (own_row[None, :] == jnp.arange(n_attn)[:, None]) & (own_rank == rep_here)[None, :]
     outgoing = jnp.einsum(
-        "dks,sbc->dkbc",
+        "ds,sbc->dbc",
         my_slot.astype(jnp.bfloat16),
         spill_cache,
         preferred_element_type=jnp.float32,
-    ).astype(jnp.bfloat16)
+    ).astype(jnp.bfloat16)[:, None]
     half = lax.all_to_all(outgoing, "attn", split_axis=0, concat_axis=0, tiled=True)
+    directory = spill_owner.reshape(n_attn, spill_count)
+    owner_dev = jnp.where(directory >= 0, directory // req_count, -1)
+    same_owner = owner_dev[:, :, None] == owner_dev[:, None, :]
+    order_rank = jnp.sum(same_owner & earlier[None, :, :], axis=2)
     other = lax.ppermute(half, "rep", [(i, (i + 1) % n_rep) for i in range(n_rep)])
-    first = jnp.where(rep_here == 0, half, other)
-    second = jnp.where(rep_here == 0, other, half)
-    incoming = jnp.concatenate([first, second], axis=1)
+    part_slots = jnp.stack([rep_here, n_rep - 1 - rep_here])
     mine_slot = (owner_dev[:, None, :] == attn_here) & (
-        order_rank[:, None, :] == slot_ids[None, :, None]
-    )
-    present = jnp.any(mine_slot, axis=2).reshape(-1)
+        order_rank[:, None, :] == part_slots[None, :, None]
+    )
+    present = jnp.any(mine_slot, axis=2)
     request = jnp.sum(
         jnp.where(mine_slot, directory[:, None, :] - attn_here * req_count, 0), axis=2
-    ).reshape(-1)
-    spill_rows = incoming.reshape(n_attn * CAP * blk, row_width)
+    )
+    spill_parts = [part.reshape(n_attn * blk, row_width) for part in (half, other)]
 
     query_rows = queries.reshape(req_count, 2, head_count, row_width)
     lengths = local_len[0]
@@ -110,25 +105,28 @@
         fresh_pos[None, None, :] % 2 <= jnp.arange(2)[None, :, None]
     )
     fresh_scores = jnp.where(fresh_ok[:, :, None, :], fresh_scores, floor_score)
-    block_ok = (request[None, :] == jnp.arange(req_count)[:, None]) & present[None, :]
-    spill_ok = jnp.broadcast_to(block_ok[:, :, None], block_ok.shape + (blk,)).reshape(
-        req_count, -1
-    )
-    spill_scores = (
-        jnp.einsum("rthc,kc->rthk", query_rows, spill_rows, preferred_element_type=jnp.float32)
-        * score_scale
-    )
-    spill_scores = jnp.where(spill_ok[:, None, None, :], spill_scores, floor_score)
-    row_top = jnp.maximum(
-        jnp.maximum(jnp.max(pool_scores, axis=3), jnp.max(fresh_scores, axis=3)),
-        jnp.max(spill_scores, axis=3),
-    )
+    row_top = jnp.maximum(jnp.max(pool_scores, axis=3), jnp.max(fresh_scores, axis=3))
+    spill_scores = []
+    for part_index, part_rows in enumerate(spill_parts):
+        block_ok = (request[None, :, part_index] == jnp.arange(req_count)[:, None]) & present[
+            None, :, part_index
+        ]
+        spill_ok = jnp.broadcast_to(block_ok[:, :, None], block_ok.shape + (blk,)).reshape(
+            req_count, -1
+        )
+        part_scores = (
+            jnp.einsum("rthc,kc->rthk", query_rows, part_rows, preferred_element_type=jnp.float32)
+            * score_scale
+        )
+        part_scores = jnp.where(spill_ok[:, None, None, :], part_scores, floor_score)
+        row_top = jnp.maximum(row_top, jnp.max(part_scores, axis=3))
+        spill_scores.append(part_scores)
     pool_weight = jnp.exp(pool_scores - row_top[..., None])
     fresh_weight = jnp.exp(fresh_scores - row_top[..., None])
-    spill_weight = jnp.exp(spill_scores - row_top[..., None])
-    denominator = (
-        jnp.sum(pool_weight, axis=3) + jnp.sum(fresh_weight, axis=3) + jnp.sum(spill_weight, axis=3)
-    )
+    spill_weight = [jnp.exp(part - row_top[..., None]) for part in spill_scores]
+    denominator = jnp.sum(pool_weight, axis=3) + jnp.sum(fresh_weight, axis=3)
+    for part in spill_weight:
+        denominator = denominator + jnp.sum(part, axis=3)
     numerator = jnp.einsum(
         "rthk,kc->rthc",
         pool_weight.astype(jnp.bfloat16),
@@ -141,12 +139,13 @@
         new_latent[:, :lat_width],
         preferred_element_type=jnp.float32,
     )
-    numerator = numerator + jnp.einsum(
-        "rthk,kc->rthc",
-        spill_weight.astype(jnp.bfloat16),
-        spill_rows[:, :lat_width],
-        preferred_element_type=jnp.float32,
-    )
+    for part, part_rows in zip(spill_weight, spill_parts):
+        numerator = numerator + jnp.einsum(
+            "rthk,kc->rthc",
+            part.astype(jnp.bfloat16),
+            part_rows[:, :lat_width],
+            preferred_element_type=jnp.float32,
+        )
     attended = (numerator / denominator[..., None]).astype(jnp.bfloat16)
     values = jnp.einsum(
         "rthc,hcv->rthv", attended, w_uv, preferred_element_type=jnp.float32

time: 175 us -> 179 us (1.023)
  waiting for transfers between devices: 86 us -> 81.6 us
  matrix products: 17.1 us -> 21.5 us
  other arithmetic: 5.11 us -> 7.14 us
  local copies, waits for them, and re-layouts: 27 us -> 28.9 us
    all_to_all x1, waiting for transfers between devices: 19.2 us -> 14.8 us  [per_device(): lax.all_to_all(outgoing, 'attn', split_axis=0, concat_axis=0, tiled=True)]
    dot_general x3 -> x5, matrix products: 2.49 us -> 5.66 us  [the longest x2 2.61 us: per_device(): jnp.einsum('rthc,kc->rthk', query_rows, part_rows, preferred_element_type...]
    broadcast_in_dim x1 -> x3, local copies, waits for them, and re-layouts: 0.13 us -> 2.4 us  [the longest x2 1.36 us: per_device(): jnp.where(spill_ok[:, None, None, :], part_scores, floor_score)]
    unnamed x20 -> x26, local copies, waits for them, and re-layouts: 18.8 us -> 18.8 us
  transfers between devices with their start and end apart: 6 -> 6, of which waited for: 6 -> 5; matrix products, arithmetic and copies ran while one was open for 5% -> 10% of each run, Pallas kernels for 0% -> 0%
where the time goes in v5:
time: 179 us; the launch traced here: 177 us
  waiting for transfers between devices  81.6 us (46%)
  starting transfers between devices  38 us (21%)
  local copies, waits for them, and re-layouts  28.9 us (16%)
  matrix products  21.5 us (12%)
  other arithmetic  7.14 us (4%)
    all_to_all x1, waiting for transfers between devices, per_device(): lax.all_to_all(spread, 'attn', split_axis=0, concat_axis=0, tiled=True)  28.4 us
    all_to_all x1, waiting for transfers between devices, per_device(): lax.all_to_all(back, ('attn', 'expert'), split_axis=0, concat_axis=0, til...  18.9 us
    unnamed x26, local copies, waits for them, and re-layouts  18.8 us
    all_to_all x1, waiting for transfers between devices, per_device(): lax.all_to_all(send_rows, ('attn', 'expert'), split_axis=0, concat_axis=0...  15 us
    all_to_all x1, waiting for transfers between devices, per_device(): lax.all_to_all(outgoing, 'attn', split_axis=0, concat_axis=0, tiled=True)  14.8 us
    all_to_all x1, starting transfers between devices, per_device(): lax.all_to_all(outgoing, 'attn', split_axis=0, concat_axis=0, tiled=True)  11.5 us
    all_to_all x1, starting transfers between devices, per_device(): lax.all_to_all(send_rows, ('attn', 'expert'), split_axis=0, concat_axis=0...  9.01 us
    all_to_all x1, starting transfers between devices, per_device(): lax.all_to_all(back, ('attn', 'expert'), split_axis=0, concat_axis=0, til...  7.64 us
  transfers between devices with their start and end apart: 6, of which 5 were waited for; matrix products, arithmetic and copies ran while one was open for 10% of the time, Pallas kernels for 0%

profile of v5, /device:TPU:2, one launch (start us, length us, event | category | flops | bytes accessed | tf_op | source)
XLA Modules:
  0.0 177.5 jit_solution(2480066118913990972)
XLA Ops:
  1.2 1.4 fusion.10
  3.6 11.5 %all-to-all-start = ((bf16[32,1,16,576]{3,2,1,0:T(8,128)(2,1)}), bf16[32,1,16,576]{3,2,1,0:T(8,128)(2,1)S(1)}, u32[]{:S(2)}, u32[]{:S(2)}) async-start(bf16[32,1,16,576]{3,2,1,0:T(8,128)(2,1)} %copy.72), calls=%async_computation | async-start | bytes 1310720 | tf_op jit(solution)/shard_map/all_to_all | solution.py:73
  20.5 14.8 %all-to-all-done = bf16[32,1,16,576]{3,2,1,0:T(8,128)(2,1)S(1)} async-done(((bf16[32,1,16,576]{3,2,1,0:T(8,128)(2,1)}), bf16[32,1,16,576]{3,2,1,0:T(8,128)(2,1)S(1)}, u32[]{:S(2)}, u32[]{:S(2)}) %all-to-all-start) | async-done | bytes 589856 | tf_op jit(solution)/shard_map/all_to_all | solution.py:73
  35.3 1.2 fusion.89
  41.4 1.5 fusion.93
  44.1 1.3 fusion.20
  47.1 5.0 %all-to-all-start.1 = ((bf16[32,8,2048]{2,1,0:T(8,128)(2,1)}), bf16[32,8,2048]{2,1,0:T(8,128)(2,1)S(1)}, u32[]{:S(2)}, u32[]{:S(2)}) async-start(bf16[32,8,2048]{2,1,0:T(8,128)(2,1)} %broadcast_in_dim.161), calls=%async_computation.1 | async-start | bytes 2097152 | tf_op jit(solution)/shard_map/all_to_all | solution.py:157
  52.4 28.4 %all-to-all-done.1 = bf16[32,8,2048]{2,1,0:T(8,128)(2,1)S(1)} async-done(((bf16[32,8,2048]{2,1,0:T(8,128)(2,1)}), bf16[32,8,2048]{2,1,0:T(8,128)(2,1)S(1)}, u32[]{:S(2)}, u32[]{:S(2)}) %all-to-all-start.1) | async-done | bytes 1048608 | tf_op jit(solution)/shard_map/all_to_all | solution.py:157
  80.8 1.7 convolution_convert_fusion.2
  83.1 4.8 %all-to-all-start.2 = ((bf16[8,128,56]{1,2,0:T(8,128)(2,1)}), bf16[8,128,56]{1,2,0:T(8,128)(2,1)S(1)}, u32[]{:S(2)}, u32[]{:S(2)}) async-start(bf16[8,128,56]{1,2,0:T(8,128)(2,1)} %bitcast.34), calls=%async_computation.2 | async-start | bytes 229376 | tf_op jit(solution)/shard_map/all_to_all | solution.py:170
  88.0 4.4 %all-to-all-done.2 = bf16[8,128,56]{1,2,0:T(8,128)(2,1)S(1)} async-done(((bf16[8,128,56]{1,2,0:T(8,128)(2,1)}), bf16[8,128,56]{1,2,0:T(8,128)(2,1)S(1)}, u32[]{:S(2)}, u32[]{:S(2)}) %all-to-all-start.2) | async-done | bytes 114720 | tf_op jit(solution)/shard_map/all_to_all | solution.py:170
  93.6 3.1 %reshape.448 = bf16[128,2,1120]{2,1,0:T(2,128)(2,1)} reshape(bf16[128,40,56]{2,1,0:T(8,128)(2,1)S(1)} %bitcast.153) | data formatting | bytes 1146880
  96.7 9.0 %all-to-all-start.3 = ((bf16[128,2,1120]{2,1,0:T(2,128)(2,1)}), bf16[128,2,1120]{2,1,0:T(2,128)(2,1)}, u32[]{:S(2)}, u32[]{:S(2)}) async-start(bf16[128,2,1120]{2,1,0:T(2,128)(2,1)} %reshape.448), calls=%async_computation.3 | async-start | bytes 1179648 | tf_op jit(solution)/shard_map/all_to_all | solution.py:185
  105.8 5.9 %copy.81 = bf16[256,7168]{0,1:T(8,128)(2,1)} copy(bf16[256,7168]{1,0:T(8,128)(2,1)} %param.29) | data formatting | bytes 7340032 | tf_op args[14]
  111.7 15.0 %all-to-all-done.3 = bf16[128,2,1120]{2,1,0:T(2,128)(2,1)} async-done(((bf16[128,2,1120]{2,1,0:T(2,128)(2,1)}), bf16[128,2,1120]{2,1,0:T(2,128)(2,1)}, u32[]{:S(2)}, u32[]{:S(2)}) %all-to-all-start.3) | async-done | bytes 573472 | tf_op jit(solution)/shard_map/all_to_all | solution.py:185
  126.7 3.3 %reshape.449 = bf16[128,40,56]{2,1,0:T(8,128)(2,1)S(1)} reshape(bf16[128,2,1120]{2,1,0:T(2,128)(2,1)} %all-to-all-done.3) | data formatting | bytes 1146880
  130.6 3.0 %convolution_bitcast_fusion.1 = f32[40,256]{1,0:T(8,128)S(1)} fusion(bf16[128,56,256]{2,1,0:T(8,128)(2,1)} %bitcast.179, bf16[128,40,56]{2,1,0:T(8,128)(2,1)S(1)} %reshape.449, f32[128,56]{1,0:T(8,128)S(1)} %mul.98, f32[40]{0:T(128)S(1)} %add_rsqrt_fusion), kind=kOutput, calls=%fused_computation.32 | convolution fusion | flops 147947520 | bytes 4313248 | tf_op jit(solution)/shard_map/skc,scu->ku/dot_general | solution.py:195
  133.5 7.0 %fusion.11 = bf16[128,40,56]{0,1,2:T(8,128)(2,1)} fusion(bf16[128,256,56]{1,2,0:T(8,128)(2,1)} %bitcast.152, bf16[128,56,256]{2,1,0:T(8,128)(2,1)} %bitcast.154, bf16[128,40,56]{2,1,0:T(8,128)(2,1)S(1)} %reshape.449, f32[128,56]{1,0:T(8,128)S(1)} %mul.98, f32[40]{0:T(128)S(1)} %add_rsqrt_fusion, f32[40,256]{1,0:T(8,128)S(1)} %convolution_bitcast_fusion.1), kind=kOutput, calls=%fused_computation.13 | convolution fusion | flops 295096320 | bytes 8556704 | tf_op jit(solution)/shard_map/ku,duc->dkc/dot_general | solution.py:200
  140.5 2.4 %copy.83 = bf16[128,40,56]{2,1,0:T(8,128)(2,1)S(1)} copy(bf16[128,40,56]{0,1,2:T(8,128)(2,1)} %fusion.11) | data formatting | bytes 1146880 | tf_op jit(solution)/shard_map/convert_element_type | solution.py:202
  142.9 3.0 %reshape.450 = bf16[128,2,1120]{2,1,0:T(2,128)(2,1)} reshape(bf16[128,40,56]{2,1,0:T(8,128)(2,1)S(1)} %copy.83) | data formatting | bytes 1146880
  145.9 7.6 %all-to-all-start.4 = ((bf16[128,2,1120]{2,1,0:T(2,128)(2,1)}), bf16[128,2,1120]{2,1,0:T(2,128)(2,1)}, u32[]{:S(2)}, u32[]{:S(2)}) async-start(bf16[128,2,1120]{2,1,0:T(2,128)(2,1)} %reshape.450), calls=%async_computation.4 | async-start | bytes 1179648 | tf_op jit(solution)/shard_map/all_to_all | solution.py:203
  153.8 18.9 %all-to-all-done.4 = bf16[128,2,1120]{2,1,0:T(2,128)(2,1)} async-done(((bf16[128,2,1120]{2,1,0:T(2,128)(2,1)}), bf16[128,2,1120]{2,1,0:T(2,128)(2,1)}, u32[]{:S(2)}, u32[]{:S(2)}) %all-to-all-start.4) | async-done | bytes 573472 | tf_op jit(solution)/shard_map/all_to_all | solution.py:203
  172.7 3.3 %reshape.451 = bf16[128,40,56]{2,1,0:T(8,128)(2,1)S(1)} reshape(bf16[128,2,1120]{2,1,0:T(2,128)(2,1)} %all-to-all-done.4) | data formatting | bytes 1146880
  176.3 1.2 fusion.31
  (84 shorter events, 18.3 us)
Async XLA Ops:
  0.0 45.5 %copy-start = (bf16[16,512,128]{2,1,0:T(8,128)(2,1)S(1)}, bf16[16,512,128]{2,1,0:T(8,128)(2,1)}, u32[]{:S(2)}) copy-start(bf16[16,512,128]{2,1,0:T(8,128)(2,1)} %param.21) | copy-start | bytes 6291460
  0.0 15.1 %copy-start.5 = (s32[1024]{0:T(1024)S(1)}, s32[1024]{0:T(1024)}, u32[]{:S(2)}) copy-start(s32[1024]{0:T(1024)} %param.20) | copy-start | bytes 12292
  0.0 16.3 %copy-start.9 = (s32[1,4]{1,0:T(1,128)S(1)}, s32[1,4]{1,0:T(1,128)}, u32[]{:S(2)}) copy-start(s32[1,4]{1,0:T(1,128)} %param.18) | copy-start | bytes 52
  0.0 19.5 %copy-start.3 = (bf16[8,576]{1,0:T(8,128)(2,1)S(1)}, bf16[8,576]{1,0:T(8,128)(2,1)}, u32[]{:S(2)}) copy-start(bf16[8,576]{1,0:T(8,128)(2,1)} %param.16) | copy-start | bytes 27652
  0.0 39.2 %copy-start.1 = (bf16[512,576]{0,1:T(8,128)(2,1)S(1)}, bf16[512,576]{0,1:T(8,128)(2,1)}, u32[]{:S(2)}) copy-start(bf16[512,576]{0,1:T(8,128)(2,1)} %param.17) | copy-start | bytes 1769476
  3.6 31.7 %all-to-all-start = ((bf16[32,1,16,576]{3,2,1,0:T(8,128)(2,1)}), bf16[32,1,16,576]{3,2,1,0:T(8,128)(2,1)S(1)}, u32[]{:S(2)}, u32[]{:S(2)}) async-start(bf16[32,1,16,576]{3,2,1,0:T(8,128)(2,1)} %copy.72), calls=%async_computation | async-start | bytes 1310720 | tf_op jit(solution)/shard_map/all_to_all | solution.py:73
  35.3 6.1 %collective-permute-start = (bf16[32,1,16,576]{3,2,1,0:T(8,128)(2,1)S(1)}, bf16[32,1,16,576]{3,2,1,0:T(8,128)(2,1)}, u32[]{:S(2)}, u32[]{:S(2)}) collective-permute-start(bf16[32,1,16,576]{3,2,1,0:T(8,128)(2,1)S(1)} %all-to-all-done), channel_id=1, source_target_pairs={{0,1},{1,0},{2,3},{3,2},{4,5},{5,4},{6,7},{7,6},{8,9},{9,8},{10,11... | collective-permute-start | bytes 1769480 | tf_op jit(solution)/shard_map/ppermute | solution.py:78
  39.3 3.6 %copy-start.6 = (f32[4,2,16]{2,1,0:T(2,128)S(1)}, f32[4,2,16]{2,1,0:T(2,128)}, u32[]{:S(2)}) copy-start(f32[4,2,16]{2,1,0:T(2,128)} %get-tuple-element.20) | copy-start | bytes 1540
  39.3 3.7 %copy-start.4 = (bf16[8,576]{1,0:T(8,128)(2,1)S(1)}, bf16[8,576]{1,0:T(8,128)(2,1)}, u32[]{:S(2)}) copy-start(bf16[8,576]{1,0:T(8,128)(2,1)} %param.16) | copy-start | bytes 27652
  45.5 6.6 %copy-start.8 = (s32[256,4]{0,1:T(4,128)S(1)}, s32[256,4]{0,1:T(4,128)}, u32[]{:S(2)}) copy-start(s32[256,4]{0,1:T(4,128)} %param.25) | copy-start | bytes 12292
  47.1 33.7 %all-to-all-start.1 = ((bf16[32,8,2048]{2,1,0:T(8,128)(2,1)}), bf16[32,8,2048]{2,1,0:T(8,128)(2,1)S(1)}, u32[]{:S(2)}, u32[]{:S(2)}) async-start(bf16[32,8,2048]{2,1,0:T(8,128)(2,1)} %broadcast_in_dim.161), calls=%async_computation.1 | async-start | bytes 2097152 | tf_op jit(solution)/shard_map/all_to_all | solution.py:157
  83.1 9.3 %all-to-all-start.2 = ((bf16[8,128,56]{1,2,0:T(8,128)(2,1)}), bf16[8,128,56]{1,2,0:T(8,128)(2,1)S(1)}, u32[]{:S(2)}, u32[]{:S(2)}) async-start(bf16[8,128,56]{1,2,0:T(8,128)(2,1)} %bitcast.34), calls=%async_computation.2 | async-start | bytes 229376 | tf_op jit(solution)/shard_map/all_to_all | solution.py:170
  88.0 17.7 %copy-start.2 = (f32[7168]{0:T(1024)S(1)}, f32[7168]{0:T(1024)}, u32[]{:S(2)}) copy-start(f32[7168]{0:T(1024)} %param.24) | copy-start | bytes 86020
  96.7 30.1 %all-to-all-start.3 = ((bf16[128,2,1120]{2,1,0:T(2,128)(2,1)}), bf16[128,2,1120]{2,1,0:T(2,128)(2,1)}, u32[]{:S(2)}, u32[]{:S(2)}) async-start(bf16[128,2,1120]{2,1,0:T(2,128)(2,1)} %reshape.448), calls=%async_computation.3 | async-start | bytes 1179648 | tf_op jit(solution)/shard_map/all_to_all | solution.py:185
  140.5 13.1 %copy-start.7 = (f32[256,4]{0,1:T(4,128)S(1)}, f32[256,4]{0,1:T(4,128)}, u32[]{:S(2)}) copy-start(f32[256,4]{0,1:T(4,128)} %param.26) | copy-start | bytes 12292
  145.9 26.8 %all-to-all-start.4 = ((bf16[128,2,1120]{2,1,0:T(2,128)(2,1)}), bf16[128,2,1120]{2,1,0:T(2,128)(2,1)}, u32[]{:S(2)}, u32[]{:S(2)}) async-start(bf16[128,2,1120]{2,1,0:T(2,128)(2,1)} %reshape.450), calls=%async_computation.4 | async-start | bytes 1179648 | tf_op jit(solution)/shard_map/all_to_all | solution.py:203

commit v6 on v4

--- a/solution.py
+++ b/solution.py
@@ -201,10 +201,12 @@
     back = jnp.einsum(
         "ku,duc->dkc", activated, down_blocks, preferred_element_type=jnp.float32
     ).astype(jnp.bfloat16)
-    returned = lax.all_to_all(back, ("attn", "expert"), split_axis=0, concat_axis=0, tiled=True)
-    summed = jnp.sum(
-        returned.astype(jnp.float32).reshape(EXPERTS, shards, capacity, sub_cols), axis=1
-    )
+    pack = (2, capacity * sub_cols // 2)
+    returned = lax.all_to_all(
+        back.reshape((n_dev,) + pack), ("attn", "expert"), split_axis=0, concat_axis=0, tiled=True
+    )
+    summed = jnp.sum(returned.astype(jnp.float32).reshape((EXPERTS, shards) + pack), axis=1)
+    summed = summed.reshape(EXPERTS, capacity, sub_cols)
     share_part = lax.dynamic_slice_in_dim(route_scores, rep_here * rows_part, rows_part, 0)
     share_part = share_part / jnp.sum(share_part, axis=1, keepdims=True)
     share_table = jnp.sum(

time: 175 us -> 169 us (0.966)
  local copies, waits for them, and re-layouts: 27 us -> 21.8 us
    unnamed x20 -> x18, local copies, waits for them, and re-layouts: 18.8 us -> 12.4 us
    reshape x0 -> x2, local copies, waits for them, and re-layouts: none -> 2.26 us  [the longest x1 1.97 us: per_device(): back.reshape((n_dev,) + pack)]
  transfers between devices with their start and end apart: 6 -> 6, of which waited for: 6 -> 6; matrix products, arithmetic and copies ran while one was open for 5% -> 6% of each run, Pallas kernels for 0% -> 0%
where the time goes in v6:
time: 169 us; the launch traced here: 168 us
  waiting for transfers between devices  86.9 us (51%)
  starting transfers between devices  37 us (22%)
  local copies, waits for them, and re-layouts  21.8 us (13%)
  matrix products  17.1 us (10%)
  other arithmetic  5.27 us (3%)
    all_to_all x1, waiting for transfers between devices, per_device(): lax.all_to_all(spread, 'attn', split_axis=0, concat_axis=0, tiled=True)  28.2 us
    all_to_all x1, waiting for transfers between devices, per_device(): lax.all_to_all(back.reshape((n_dev,) + pack), ('attn', 'expert'), split_a...  19.8 us
    all_to_all x1, waiting for transfers between devices, per_device(): lax.all_to_all(outgoing, 'attn', split_axis=0, concat_axis=0, tiled=True)  19.2 us
    all_to_all x1, waiting for transfers between devices, per_device(): lax.all_to_all(send_rows, ('attn', 'expert'), split_axis=0, concat_axis=0...  15 us
    unnamed x18, local copies, waits for them, and re-layouts  12.4 us
    all_to_all x1, starting transfers between devices, per_device(): lax.all_to_all(outgoing, 'attn', split_axis=0, concat_axis=0, tiled=True)  11.5 us
    all_to_all x1, starting transfers between devices, per_device(): lax.all_to_all(send_rows, ('attn', 'expert'), split_axis=0, concat_axis=0...  9.02 us
    dot_general x1, matrix products, per_device(): jnp.einsum('ku,duc->dkc', activated, down_blocks, preferred_element_type=...  6.95 us
  transfers between devices with their start and end apart: 6, of which 6 were waited for; matrix products, arithmetic and copies ran while one was open for 6% of the time, Pallas kernels for 0%

profile of v6, /device:TPU:2, one launch (start us, length us, event | category | flops | bytes accessed | tf_op | source)
XLA Modules:
  0.0 168.5 jit_solution(9040425213412304616)
XLA Ops:
  1.8 1.5 fusion.10
  3.3 1.0 copy.89
  4.4 11.5 %all-to-all-start = ((bf16[32,1,16,576]{3,2,1,0:T(8,128)(2,1)}), bf16[32,1,16,576]{3,2,1,0:T(8,128)(2,1)S(1)}, u32[]{:S(2)}, u32[]{:S(2)}) async-start(bf16[32,1,16,576]{3,2,1,0:T(8,128)(2,1)} %copy.89), calls=%async_computation | async-start | bytes 1310720 | tf_op jit(solution)/shard_map/all_to_all | solution.py:80
  16.8 19.2 %all-to-all-done = bf16[32,1,16,576]{3,2,1,0:T(8,128)(2,1)S(1)} async-done(((bf16[32,1,16,576]{3,2,1,0:T(8,128)(2,1)}), bf16[32,1,16,576]{3,2,1,0:T(8,128)(2,1)S(1)}, u32[]{:S(2)}, u32[]{:S(2)}) %all-to-all-start) | async-done | bytes 589856 | tf_op jit(solution)/shard_map/all_to_all | solution.py:80
  36.3 1.1 reshape.431
  38.3 1.2 broadcast_select_fusion.1
  42.3 1.1 broadcast_in_dim.140
  43.4 5.0 %all-to-all-start.1 = ((bf16[32,8,2048]{2,1,0:T(8,128)(2,1)}), bf16[32,8,2048]{2,1,0:T(8,128)(2,1)S(1)}, u32[]{:S(2)}, u32[]{:S(2)}) async-start(bf16[32,8,2048]{2,1,0:T(8,128)(2,1)} %broadcast_in_dim.140), calls=%async_computation.1 | async-start | bytes 2097152 | tf_op jit(solution)/shard_map/all_to_all | solution.py:158
  48.7 28.2 %all-to-all-done.1 = bf16[32,8,2048]{2,1,0:T(8,128)(2,1)S(1)} async-done(((bf16[32,8,2048]{2,1,0:T(8,128)(2,1)}), bf16[32,8,2048]{2,1,0:T(8,128)(2,1)S(1)}, u32[]{:S(2)}, u32[]{:S(2)}) %all-to-all-start.1) | async-done | bytes 1048608 | tf_op jit(solution)/shard_map/all_to_all | solution.py:158
  76.9 1.7 convolution_convert_fusion.2
  79.3 4.8 %all-to-all-start.2 = ((bf16[8,128,56]{1,2,0:T(8,128)(2,1)}), bf16[8,128,56]{1,2,0:T(8,128)(2,1)S(1)}, u32[]{:S(2)}, u32[]{:S(2)}) async-start(bf16[8,128,56]{1,2,0:T(8,128)(2,1)} %bitcast.26), calls=%async_computation.2 | async-start | bytes 229376 | tf_op jit(solution)/shard_map/all_to_all | solution.py:171
  84.2 4.4 %all-to-all-done.2 = bf16[8,128,56]{1,2,0:T(8,128)(2,1)S(1)} async-done(((bf16[8,128,56]{1,2,0:T(8,128)(2,1)}), bf16[8,128,56]{1,2,0:T(8,128)(2,1)S(1)}, u32[]{:S(2)}, u32[]{:S(2)}) %all-to-all-start.2) | async-done | bytes 114720 | tf_op jit(solution)/shard_map/all_to_all | solution.py:171
  89.8 3.1 %reshape.461 = bf16[128,2,1120]{2,1,0:T(2,128)(2,1)} reshape(bf16[128,40,56]{2,1,0:T(8,128)(2,1)S(1)} %bitcast.133) | data formatting | bytes 1146880
  92.8 9.0 %all-to-all-start.3 = ((bf16[128,2,1120]{2,1,0:T(2,128)(2,1)}), bf16[128,2,1120]{2,1,0:T(2,128)(2,1)}, u32[]{:S(2)}, u32[]{:S(2)}) async-start(bf16[128,2,1120]{2,1,0:T(2,128)(2,1)} %reshape.461), calls=%async_computation.3 | async-start | bytes 1179648 | tf_op jit(solution)/shard_map/all_to_all | solution.py:186
  102.0 5.9 %copy.97 = bf16[256,7168]{0,1:T(8,128)(2,1)} copy(bf16[256,7168]{1,0:T(8,128)(2,1)} %param.29) | data formatting | bytes 7340032 | tf_op args[14]
  107.9 15.0 %all-to-all-done.3 = bf16[128,2,1120]{2,1,0:T(2,128)(2,1)} async-done(((bf16[128,2,1120]{2,1,0:T(2,128)(2,1)}), bf16[128,2,1120]{2,1,0:T(2,128)(2,1)}, u32[]{:S(2)}, u32[]{:S(2)}) %all-to-all-start.3) | async-done | bytes 573472 | tf_op jit(solution)/shard_map/all_to_all | solution.py:186
  122.9 3.3 %reshape.462 = bf16[128,40,56]{2,1,0:T(8,128)(2,1)S(1)} reshape(bf16[128,2,1120]{2,1,0:T(2,128)(2,1)} %all-to-all-done.3) | data formatting | bytes 1146880
  126.7 3.0 %convolution_bitcast_fusion.1 = f32[40,256]{1,0:T(8,128)S(1)} fusion(bf16[128,56,256]{2,1,0:T(8,128)(2,1)} %bitcast.158, bf16[128,40,56]{2,1,0:T(8,128)(2,1)S(1)} %reshape.462, f32[128,56]{1,0:T(8,128)S(1)} %mul.94, f32[40]{0:T(128)S(1)} %add_rsqrt_fusion), kind=kOutput, calls=%fused_computation.29 | convolution fusion | flops 147947520 | bytes 4313248 | tf_op jit(solution)/shard_map/skc,scu->ku/dot_general | solution.py:196
  129.7 7.0 %fusion.11 = bf16[128,40,56]{0,1,2:T(8,128)(2,1)} fusion(bf16[128,256,56]{1,2,0:T(8,128)(2,1)} %bitcast.132, bf16[128,56,256]{2,1,0:T(8,128)(2,1)} %bitcast.136, bf16[128,40,56]{2,1,0:T(8,128)(2,1)S(1)} %reshape.462, f32[128,56]{1,0:T(8,128)S(1)} %mul.94, f32[40]{0:T(128)S(1)} %add_rsqrt_fusion, f32[40,256]{1,0:T(8,128)S(1)} %convolution_bitcast_fusion.1), kind=kOutput, calls=%fused_computation.13 | convolution fusion | flops 295096320 | bytes 8556704 | tf_op jit(solution)/shard_map/ku,duc->dkc/dot_general | solution.py:201
  136.7 1.1 copy.99
  137.8 2.0 %copy.100 = bf16[128,2,1120]{2,1,0:T(2,128)(2,1)} copy(bf16[128,2,1120]{0,2,1:T(8,128)(2,1)S(1)} %bitcast.137) | data formatting | bytes 1146880 | tf_op jit(solution)/shard_map/reshape | solution.py:206
  139.8 6.6 %all-to-all-start.4 = ((bf16[128,2,1120]{2,1,0:T(2,128)(2,1)}), bf16[128,2,1120]{2,1,0:T(2,128)(2,1)S(1)}, u32[]{:S(2)}, u32[]{:S(2)}) async-start(bf16[128,2,1120]{2,1,0:T(2,128)(2,1)} %copy.100), calls=%async_computation.4 | async-start | bytes 1179648 | tf_op jit(solution)/shard_map/all_to_all | solution.py:205
  146.7 19.8 %all-to-all-done.4 = bf16[128,2,1120]{2,1,0:T(2,128)(2,1)S(1)} async-done(((bf16[128,2,1120]{2,1,0:T(2,128)(2,1)}), bf16[128,2,1120]{2,1,0:T(2,128)(2,1)S(1)}, u32[]{:S(2)}, u32[]{:S(2)}) %all-to-all-start.4) | async-done | bytes 573472 | tf_op jit(solution)/shard_map/all_to_all | solution.py:205
  167.3 1.2 fusion.30
  (80 shorter events, 10.2 us)
Async XLA Ops:
  0.0 41.8 %copy-start = (bf16[16,512,128]{2,1,0:T(8,128)(2,1)S(1)}, bf16[16,512,128]{2,1,0:T(8,128)(2,1)}, u32[]{:S(2)}) copy-start(bf16[16,512,128]{2,1,0:T(8,128)(2,1)} %param.21) | copy-start | bytes 6291460
  0.9 15.6 %copy-start.6 = (s32[1,4]{1,0:T(1,128)S(1)}, s32[1,4]{1,0:T(1,128)}, u32[]{:S(2)}) copy-start(s32[1,4]{1,0:T(1,128)} %param.18) | copy-start | bytes 52
  1.8 35.6 %copy-start.3 = (bf16[8,576]{1,0:T(8,128)(2,1)S(1)}, bf16[8,576]{1,0:T(8,128)(2,1)}, u32[]{:S(2)}) copy-start(bf16[8,576]{1,0:T(8,128)(2,1)} %param.16) | copy-start | bytes 27652
  1.8 35.9 %copy-start.1 = (bf16[512,576]{0,1:T(8,128)(2,1)S(1)}, bf16[512,576]{0,1:T(8,128)(2,1)}, u32[]{:S(2)}) copy-start(bf16[512,576]{0,1:T(8,128)(2,1)} %param.17) | copy-start | bytes 1769476
  4.4 31.7 %all-to-all-start = ((bf16[32,1,16,576]{3,2,1,0:T(8,128)(2,1)}), bf16[32,1,16,576]{3,2,1,0:T(8,128)(2,1)S(1)}, u32[]{:S(2)}, u32[]{:S(2)}) async-start(bf16[32,1,16,576]{3,2,1,0:T(8,128)(2,1)} %copy.89), calls=%async_computation | async-start | bytes 1310720 | tf_op jit(solution)/shard_map/all_to_all | solution.py:80
  36.1 2.2 %collective-permute-start = (bf16[32,1,16,576]{3,2,1,0:T(8,128)(2,1)S(1)}, bf16[32,1,16,576]{3,2,1,0:T(8,128)(2,1)}, u32[]{:S(2)}, u32[]{:S(2)}) collective-permute-start(bf16[32,1,16,576]{3,2,1,0:T(8,128)(2,1)S(1)} %all-to-all-done), channel_id=1, source_target_pairs={{0,1},{1,0},{2,3},{3,2},{4,5},{5,4},{6,7},{7,6},{8,9},{9,8},{10,11... | collective-permute-start | bytes 1769480 | tf_op jit(solution)/shard_map/ppermute | solution.py:81
  42.2 6.2 %copy-start.5 = (s32[256,4]{0,1:T(4,128)S(1)}, s32[256,4]{0,1:T(4,128)}, u32[]{:S(2)}) copy-start(s32[256,4]{0,1:T(4,128)} %param.25) | copy-start | bytes 12292
  43.4 33.6 %all-to-all-start.1 = ((bf16[32,8,2048]{2,1,0:T(8,128)(2,1)}), bf16[32,8,2048]{2,1,0:T(8,128)(2,1)S(1)}, u32[]{:S(2)}, u32[]{:S(2)}) async-start(bf16[32,8,2048]{2,1,0:T(8,128)(2,1)} %broadcast_in_dim.140), calls=%async_computation.1 | async-start | bytes 2097152 | tf_op jit(solution)/shard_map/all_to_all | solution.py:158
  79.3 9.3 %all-to-all-start.2 = ((bf16[8,128,56]{1,2,0:T(8,128)(2,1)}), bf16[8,128,56]{1,2,0:T(8,128)(2,1)S(1)}, u32[]{:S(2)}, u32[]{:S(2)}) async-start(bf16[8,128,56]{1,2,0:T(8,128)(2,1)} %bitcast.26), calls=%async_computation.2 | async-start | bytes 229376 | tf_op jit(solution)/shard_map/all_to_all | solution.py:171
  89.6 12.3 %copy-start.2 = (f32[7168]{0:T(1024)S(1)}, f32[7168]{0:T(1024)}, u32[]{:S(2)}) copy-start(f32[7168]{0:T(1024)} %param.24) | copy-start | bytes 86020
  92.8 30.1 %all-to-all-start.3 = ((bf16[128,2,1120]{2,1,0:T(2,128)(2,1)}), bf16[128,2,1120]{2,1,0:T(2,128)(2,1)}, u32[]{:S(2)}, u32[]{:S(2)}) async-start(bf16[128,2,1120]{2,1,0:T(2,128)(2,1)} %reshape.461), calls=%async_computation.3 | async-start | bytes 1179648 | tf_op jit(solution)/shard_map/all_to_all | solution.py:186
  136.7 9.8 %copy-start.4 = (f32[256,4]{0,1:T(4,128)S(1)}, f32[256,4]{0,1:T(4,128)}, u32[]{:S(2)}) copy-start(f32[256,4]{0,1:T(4,128)} %param.26) | copy-start | bytes 12292
  139.8 26.7 %all-to-all-start.4 = ((bf16[128,2,1120]{2,1,0:T(2,128)(2,1)}), bf16[128,2,1120]{2,1,0:T(2,128)(2,1)S(1)}, u32[]{:S(2)}, u32[]{:S(2)}) async-start(bf16[128,2,1120]{2,1,0:T(2,128)(2,1)} %copy.100), calls=%async_computation.4 | async-start | bytes 1179648 | tf_op jit(solution)/shard_map/all_to_all | solution.py:205

commit v7 on v6

--- a/solution.py
+++ b/solution.py
@@ -59,29 +59,25 @@
 
     spill_count = spill_cache.shape[0]
     blk = spill_cache.shape[1]
+    earlier = jnp.arange(spill_count)[:, None] > jnp.arange(spill_count)[None, :]
+    own_ids = lax.dynamic_slice_in_dim(spill_owner, attn_here * spill_count, spill_count, 0)
+    own_row = jnp.where(own_ids >= 0, own_ids // req_count, -1)
+    own_rank = jnp.sum((own_row[:, None] == own_row[None, :]) & earlier, axis=1)
+    my_slot = (own_row[None, :] == jnp.arange(n_attn)[:, None]) & (own_rank == rep_here)[None, :]
+    outgoing = jnp.einsum(
+        "ds,sbc->dbc",
+        my_slot.astype(jnp.bfloat16),
+        spill_cache,
+        preferred_element_type=jnp.float32,
+    ).astype(jnp.bfloat16)[:, None]
+    half = lax.all_to_all(outgoing, "attn", split_axis=0, concat_axis=0, tiled=True)
+    other = lax.ppermute(half, "rep", [(i, (i + 1) % n_rep) for i in range(n_rep)])
+    incoming = jnp.concatenate([half, other], axis=1)
     directory = spill_owner.reshape(n_attn, spill_count)
     owner_dev = jnp.where(directory >= 0, directory // req_count, -1)
-    earlier = jnp.arange(spill_count)[:, None] > jnp.arange(spill_count)[None, :]
     same_owner = owner_dev[:, :, None] == owner_dev[:, None, :]
     order_rank = jnp.sum(same_owner & earlier[None, :, :], axis=2)
-    slot_ids = jnp.arange(CAP)
-    own_row = owner_dev[attn_here]
-    own_rank = order_rank[attn_here]
-    pick_slot = (own_row[None, None, :] == jnp.arange(n_attn)[:, None, None]) & (
-        own_rank[None, None, :] == slot_ids[None, :, None]
-    )
-    my_slot = lax.dynamic_slice_in_dim(pick_slot, rep_here, 1, 1)
-    outgoing = jnp.einsum(
-        "dks,sbc->dkbc",
-        my_slot.astype(jnp.bfloat16),
-        spill_cache,
-        preferred_element_type=jnp.float32,
-    ).astype(jnp.bfloat16)
-    half = lax.all_to_all(outgoing, "attn", split_axis=0, concat_axis=0, tiled=True)
-    other = lax.ppermute(half, "rep", [(i, (i + 1) % n_rep) for i in range(n_rep)])
-    first = jnp.where(rep_here == 0, half, other)
-    second = jnp.where(rep_here == 0, other, half)
-    incoming = jnp.concatenate([first, second], axis=1)
+    slot_ids = jnp.stack([rep_here, n_rep - 1 - rep_here])
     mine_slot = (owner_dev[:, None, :] == attn_here) & (
         order_rank[:, None, :] == slot_ids[None, :, None]
     )

time: 169 us -> 167 us (0.988)
  waiting for transfers between devices: 86.9 us -> 83.5 us
    all_to_all x1, waiting for transfers between devices: 19.2 us -> 15.3 us  [per_device(): lax.all_to_all(outgoing, 'attn', split_axis=0, concat_axis=0, tiled=True)]
    unnamed x18 -> x25, local copies, waits for them, and re-layouts: 12.4 us -> 12.5 us
  transfers between devices with their start and end apart: 6 -> 6, of which waited for: 6 -> 6; matrix products, arithmetic and copies ran while one was open for 6% -> 8% of each run, Pallas kernels for 0% -> 0%
where the time goes in v7:
time: 167 us; the launch traced here: 166 us
  waiting for transfers between devices  83.5 us (50%)
  starting transfers between devices  37 us (22%)
  local copies, waits for them, and re-layouts  21.1 us (13%)
  matrix products  17.6 us (11%)
  other arithmetic  6.43 us (4%)
    all_to_all x1, waiting for transfers between devices, per_device(): lax.all_to_all(spread, 'attn', split_axis=0, concat_axis=0, tiled=True)  28 us
    all_to_all x1, waiting for transfers between devices, per_device(): lax.all_to_all(back.reshape((n_dev,) + pack), ('attn', 'expert'), split_a...  19.8 us
    all_to_all x1, waiting for transfers between devices, per_device(): lax.all_to_all(outgoing, 'attn', split_axis=0, concat_axis=0, tiled=True)  15.3 us
    all_to_all x1, waiting for transfers between devices, per_device(): lax.all_to_all(send_rows, ('attn', 'expert'), split_axis=0, concat_axis=0...  15 us
    unnamed x25, local copies, waits for them, and re-layouts  12.5 us
    all_to_all x1, starting transfers between devices, per_device(): lax.all_to_all(outgoing, 'attn', split_axis=0, concat_axis=0, tiled=True)  11.5 us
    all_to_all x1, starting transfers between devices, per_device(): lax.all_to_all(send_rows, ('attn', 'expert'), split_axis=0, concat_axis=0...  9.02 us
    dot_general x1, matrix products, per_device(): jnp.einsum('ku,duc->dkc', activated, down_blocks, preferred_element_type=...  6.95 us
  transfers between devices with their start and end apart: 6, of which 6 were waited for; matrix products, arithmetic and copies ran while one was open for 8% of the time, Pallas kernels for 0%

profile of v7, /device:TPU:2, one launch (start us, length us, event | category | flops | bytes accessed | tf_op | source)
XLA Modules:
  0.0 166.1 jit_solution(181600596459803746)
XLA Ops:
  1.2 1.4 fusion.10
  2.6 1.0 copy.89
  3.6 11.5 %all-to-all-start = ((bf16[32,1,16,576]{3,2,1,0:T(8,128)(2,1)}), bf16[32,1,16,576]{3,2,1,0:T(8,128)(2,1)S(1)}, u32[]{:S(2)}, u32[]{:S(2)}) async-start(bf16[32,1,16,576]{3,2,1,0:T(8,128)(2,1)} %copy.89), calls=%async_computation | async-start | bytes 1310720 | tf_op jit(solution)/shard_map/all_to_all | solution.py:73
  17.2 1.1 reshape.382
  19.1 1.0 fusion.88
  20.0 15.3 %all-to-all-done = bf16[32,1,16,576]{3,2,1,0:T(8,128)(2,1)S(1)} async-done(((bf16[32,1,16,576]{3,2,1,0:T(8,128)(2,1)}), bf16[32,1,16,576]{3,2,1,0:T(8,128)(2,1)S(1)}, u32[]{:S(2)}, u32[]{:S(2)}) %all-to-all-start) | async-done | bytes 589856 | tf_op jit(solution)/shard_map/all_to_all | solution.py:73
  40.1 1.1 broadcast_in_dim.100
  41.2 5.0 %all-to-all-start.1 = ((bf16[32,8,2048]{2,1,0:T(8,128)(2,1)}), bf16[32,8,2048]{2,1,0:T(8,128)(2,1)S(1)}, u32[]{:S(2)}, u32[]{:S(2)}) async-start(bf16[32,8,2048]{2,1,0:T(8,128)(2,1)} %broadcast_in_dim.100), calls=%async_computation.1 | async-start | bytes 2097152 | tf_op jit(solution)/shard_map/all_to_all | solution.py:154
  46.6 28.0 %all-to-all-done.1 = bf16[32,8,2048]{2,1,0:T(8,128)(2,1)S(1)} async-done(((bf16[32,8,2048]{2,1,0:T(8,128)(2,1)}), bf16[32,8,2048]{2,1,0:T(8,128)(2,1)S(1)}, u32[]{:S(2)}, u32[]{:S(2)}) %all-to-all-start.1) | async-done | bytes 1048608 | tf_op jit(solution)/shard_map/all_to_all | solution.py:154
  74.6 1.7 %convolution_convert_fusion.2 = bf16[256,224]{0,1:T(8,128)(2,1)S(1)} fusion(bf16[2048,224]{0,1:T(8,128)(2,1)} %param.22, bf16[32,8,2048]{2,1,0:T(8,128)(2,1)S(1)} %all-to-all-done.1), kind=kOutput, calls=%fused_computation.24 | convolution fusion | flops 234938368 | bytes 2080768 | tf_op jit(solution)/shard_map/dot_general | solution.py:156
  76.9 4.8 %all-to-all-start.2 = ((bf16[8,128,56]{1,2,0:T(8,128)(2,1)}), bf16[8,128,56]{1,2,0:T(8,128)(2,1)S(1)}, u32[]{:S(2)}, u32[]{:S(2)}) async-start(bf16[8,128,56]{1,2,0:T(8,128)(2,1)} %bitcast.25), calls=%async_computation.2 | async-start | bytes 229376 | tf_op jit(solution)/shard_map/all_to_all | solution.py:167
  81.8 4.4 %all-to-all-done.2 = bf16[8,128,56]{1,2,0:T(8,128)(2,1)S(1)} async-done(((bf16[8,128,56]{1,2,0:T(8,128)(2,1)}), bf16[8,128,56]{1,2,0:T(8,128)(2,1)S(1)}, u32[]{:S(2)}, u32[]{:S(2)}) %all-to-all-start.2) | async-done | bytes 114720 | tf_op jit(solution)/shard_map/all_to_all | solution.py:167
  87.4 3.1 %reshape.411 = bf16[128,2,1120]{2,1,0:T(2,128)(2,1)} reshape(bf16[128,40,56]{2,1,0:T(8,128)(2,1)S(1)} %bitcast.130) | data formatting | bytes 1146880
  90.5 9.0 %all-to-all-start.3 = ((bf16[128,2,1120]{2,1,0:T(2,128)(2,1)}), bf16[128,2,1120]{2,1,0:T(2,128)(2,1)}, u32[]{:S(2)}, u32[]{:S(2)}) async-start(bf16[128,2,1120]{2,1,0:T(2,128)(2,1)} %reshape.411), calls=%async_computation.3 | async-start | bytes 1179648 | tf_op jit(solution)/shard_map/all_to_all | solution.py:182
  99.6 5.9 %copy.97 = bf16[256,7168]{0,1:T(8,128)(2,1)} copy(bf16[256,7168]{1,0:T(8,128)(2,1)} %param.29) | data formatting | bytes 7340032 | tf_op args[14]
  105.5 15.0 %all-to-all-done.3 = bf16[128,2,1120]{2,1,0:T(2,128)(2,1)} async-done(((bf16[128,2,1120]{2,1,0:T(2,128)(2,1)}), bf16[128,2,1120]{2,1,0:T(2,128)(2,1)}, u32[]{:S(2)}, u32[]{:S(2)}) %all-to-all-start.3) | async-done | bytes 573472 | tf_op jit(solution)/shard_map/all_to_all | solution.py:182
  120.5 3.3 %reshape.412 = bf16[128,40,56]{2,1,0:T(8,128)(2,1)S(1)} reshape(bf16[128,2,1120]{2,1,0:T(2,128)(2,1)} %all-to-all-done.3) | data formatting | bytes 1146880
  124.4 3.0 %convolution_bitcast_fusion.1 = f32[40,256]{1,0:T(8,128)S(1)} fusion(bf16[128,56,256]{2,1,0:T(8,128)(2,1)} %bitcast.155, bf16[128,40,56]{2,1,0:T(8,128)(2,1)S(1)} %reshape.412, f32[128,56]{1,0:T(8,128)S(1)} %mul.98, f32[40]{0:T(128)S(1)} %add_rsqrt_fusion), kind=kOutput, calls=%fused_computation.28 | convolution fusion | flops 147947520 | bytes 4313248 | tf_op jit(solution)/shard_map/skc,scu->ku/dot_general | solution.py:192
  127.4 7.0 %fusion.11 = bf16[128,40,56]{0,1,2:T(8,128)(2,1)} fusion(bf16[128,256,56]{1,2,0:T(8,128)(2,1)} %bitcast.129, bf16[128,56,256]{2,1,0:T(8,128)(2,1)} %bitcast.131, bf16[128,40,56]{2,1,0:T(8,128)(2,1)S(1)} %reshape.412, f32[128,56]{1,0:T(8,128)S(1)} %mul.98, f32[40]{0:T(128)S(1)} %add_rsqrt_fusion, f32[40,256]{1,0:T(8,128)S(1)} %convolution_bitcast_fusion.1), kind=kOutput, calls=%fused_computation.12 | convolution fusion | flops 295096320 | bytes 8556704 | tf_op jit(solution)/shard_map/ku,duc->dkc/dot_general | solution.py:197
  134.3 1.1 copy.99
  135.5 2.0 %copy.100 = bf16[128,2,1120]{2,1,0:T(2,128)(2,1)} copy(bf16[128,2,1120]{0,2,1:T(8,128)(2,1)S(1)} %bitcast.132) | data formatting | bytes 1146880 | tf_op jit(solution)/shard_map/reshape | solution.py:202
  137.4 6.6 %all-to-all-start.4 = ((bf16[128,2,1120]{2,1,0:T(2,128)(2,1)}), bf16[128,2,1120]{2,1,0:T(2,128)(2,1)S(1)}, u32[]{:S(2)}, u32[]{:S(2)}) async-start(bf16[128,2,1120]{2,1,0:T(2,128)(2,1)} %copy.100), calls=%async_computation.4 | async-start | bytes 1179648 | tf_op jit(solution)/shard_map/all_to_all | solution.py:201
  144.3 19.8 %all-to-all-done.4 = bf16[128,2,1120]{2,1,0:T(2,128)(2,1)S(1)} async-done(((bf16[128,2,1120]{2,1,0:T(2,128)(2,1)}), bf16[128,2,1120]{2,1,0:T(2,128)(2,1)S(1)}, u32[]{:S(2)}, u32[]{:S(2)}) %all-to-all-start.4) | async-done | bytes 573472 | tf_op jit(solution)/shard_map/all_to_all | solution.py:201
  165.0 1.2 fusion.29
  (85 shorter events, 12.3 us)
Async XLA Ops:
  0.0 39.6 %copy-start = (bf16[16,512,128]{2,1,0:T(8,128)(2,1)S(1)}, bf16[16,512,128]{2,1,0:T(8,128)(2,1)}, u32[]{:S(2)}) copy-start(bf16[16,512,128]{2,1,0:T(8,128)(2,1)} %param.21) | copy-start | bytes 6291460
  0.0 15.1 %copy-start.4 = (s32[1024]{0:T(1024)S(1)}, s32[1024]{0:T(1024)}, u32[]{:S(2)}) copy-start(s32[1024]{0:T(1024)} %param.20) | copy-start | bytes 12292
  1.1 17.1 %copy-start.9 = (s32[1,4]{1,0:T(1,128)S(1)}, s32[1,4]{1,0:T(1,128)}, u32[]{:S(2)}) copy-start(s32[1,4]{1,0:T(1,128)} %param.18) | copy-start | bytes 52
  1.1 17.9 %copy-start.3 = (bf16[8,576]{1,0:T(8,128)(2,1)S(1)}, bf16[8,576]{1,0:T(8,128)(2,1)}, u32[]{:S(2)}) copy-start(bf16[8,576]{1,0:T(8,128)(2,1)} %param.16) | copy-start | bytes 27652
  2.6 33.5 %copy-start.1 = (bf16[512,576]{0,1:T(8,128)(2,1)S(1)}, bf16[512,576]{0,1:T(8,128)(2,1)}, u32[]{:S(2)}) copy-start(bf16[512,576]{0,1:T(8,128)(2,1)} %param.17) | copy-start | bytes 1769476
  3.6 31.7 %all-to-all-start = ((bf16[32,1,16,576]{3,2,1,0:T(8,128)(2,1)}), bf16[32,1,16,576]{3,2,1,0:T(8,128)(2,1)S(1)}, u32[]{:S(2)}, u32[]{:S(2)}) async-start(bf16[32,1,16,576]{3,2,1,0:T(8,128)(2,1)} %copy.89), calls=%async_computation | async-start | bytes 1310720 | tf_op jit(solution)/shard_map/all_to_all | solution.py:73
  18.5 0.6 copy-start.8
  35.3 2.1 %collective-permute-start = (bf16[32,1,16,576]{3,2,1,0:T(8,128)(2,1)S(1)}, bf16[32,1,16,576]{3,2,1,0:T(8,128)(2,1)S(1)}, u32[]{:S(2)}, u32[]{:S(2)}) collective-permute-start(bf16[32,1,16,576]{3,2,1,0:T(8,128)(2,1)S(1)} %all-to-all-done), channel_id=1, source_target_pairs={{0,1},{1,0},{2,3},{3,2},{4,5},{5,4},{6,7},{7,6},{8,9},{9,8},{10,11... | collective-permute-start | bytes 1769480 | tf_op jit(solution)/shard_map/ppermute | solution.py:74
  37.5 0.7 copy-start.6
  40.1 6.2 %copy-start.7 = (s32[256,4]{0,1:T(4,128)S(1)}, s32[256,4]{0,1:T(4,128)}, u32[]{:S(2)}) copy-start(s32[256,4]{0,1:T(4,128)} %param.25) | copy-start | bytes 12292
  41.2 33.4 %all-to-all-start.1 = ((bf16[32,8,2048]{2,1,0:T(8,128)(2,1)}), bf16[32,8,2048]{2,1,0:T(8,128)(2,1)S(1)}, u32[]{:S(2)}, u32[]{:S(2)}) async-start(bf16[32,8,2048]{2,1,0:T(8,128)(2,1)} %broadcast_in_dim.100), calls=%async_computation.1 | async-start | bytes 2097152 | tf_op jit(solution)/shard_map/all_to_all | solution.py:154
  76.9 9.3 %all-to-all-start.2 = ((bf16[8,128,56]{1,2,0:T(8,128)(2,1)}), bf16[8,128,56]{1,2,0:T(8,128)(2,1)S(1)}, u32[]{:S(2)}, u32[]{:S(2)}) async-start(bf16[8,128,56]{1,2,0:T(8,128)(2,1)} %bitcast.25), calls=%async_computation.2 | async-start | bytes 229376 | tf_op jit(solution)/shard_map/all_to_all | solution.py:167
  87.2 12.3 %copy-start.2 = (f32[7168]{0:T(1024)S(1)}, f32[7168]{0:T(1024)}, u32[]{:S(2)}) copy-start(f32[7168]{0:T(1024)} %param.24) | copy-start | bytes 86020
  90.5 30.1 %all-to-all-start.3 = ((bf16[128,2,1120]{2,1,0:T(2,128)(2,1)}), bf16[128,2,1120]{2,1,0:T(2,128)(2,1)}, u32[]{:S(2)}, u32[]{:S(2)}) async-start(bf16[128,2,1120]{2,1,0:T(2,128)(2,1)} %reshape.411), calls=%async_computation.3 | async-start | bytes 1179648 | tf_op jit(solution)/shard_map/all_to_all | solution.py:182
  134.3 9.8 %copy-start.5 = (f32[256,4]{0,1:T(4,128)S(1)}, f32[256,4]{0,1:T(4,128)}, u32[]{:S(2)}) copy-start(f32[256,4]{0,1:T(4,128)} %param.26) | copy-start | bytes 12292
  137.4 26.7 %all-to-all-start.4 = ((bf16[128,2,1120]{2,1,0:T(2,128)(2,1)}), bf16[128,2,1120]{2,1,0:T(2,128)(2,1)S(1)}, u32[]{:S(2)}, u32[]{:S(2)}) async-start(bf16[128,2,1120]{2,1,0:T(2,128)(2,1)} %copy.100), calls=%async_computation.4 | async-start | bytes 1179648 | tf_op jit(solution)/shard_map/all_to_all | solution.py:201

commit v8 on v7

--- a/solution.py
+++ b/solution.py
@@ -193,15 +193,22 @@
     up_proj = jnp.einsum("skc,scu->ku", normed, up_blocks, preferred_element_type=jnp.float32)
     activated = (jax.nn.silu(gate_proj) * up_proj).astype(jnp.bfloat16)
     n_dev = n_attn * n_expert
-    down_blocks = w_down.reshape(w_down.shape[0], n_dev, sub_cols).transpose(1, 0, 2)
+    per_attn = shards // n_expert
+    down_blocks = (
+        w_down.reshape(w_down.shape[0], n_attn, n_expert, sub_cols)
+        .transpose(2, 1, 0, 3)
+        .reshape(n_dev, w_down.shape[0], sub_cols)
+    )
     back = jnp.einsum(
         "ku,duc->dkc", activated, down_blocks, preferred_element_type=jnp.float32
     ).astype(jnp.bfloat16)
     pack = (2, capacity * sub_cols // 2)
     returned = lax.all_to_all(
-        back.reshape((n_dev,) + pack), ("attn", "expert"), split_axis=0, concat_axis=0, tiled=True
-    )
-    summed = jnp.sum(returned.astype(jnp.float32).reshape((EXPERTS, shards) + pack), axis=1)
+        back.reshape((n_dev,) + pack), ("expert", "attn"), split_axis=0, concat_axis=0, tiled=True
+    )
+    summed = jnp.sum(
+        returned.astype(jnp.float32).reshape((n_expert, EXPERTS, per_attn) + pack), axis=(0, 2)
+    )
     summed = summed.reshape(EXPERTS, capacity, sub_cols)
     share_part = lax.dynamic_slice_in_dim(route_scores, rep_here * rows_part, rows_part, 0)
     share_part = share_part / jnp.sum(share_part, axis=1, keepdims=True)

time: 167 us -> 166 us (level)
  waiting for transfers between devices: 83.5 us -> 74.5 us
  local copies, waits for them, and re-layouts: 21.1 us -> 25.2 us
  other arithmetic: 6.43 us -> 9.7 us
    all_to_all x1, waiting for transfers between devices: 15 us -> 10.9 us  [per_device(): lax.all_to_all(send_rows, ('attn', 'expert'), split_axis=0, concat_axis=0...]
    transpose x0 -> x1, local copies, waits for them, and re-layouts: none -> 4.08 us  [per_device(): down_blocks = w_down.reshape(w_down.shape[0], n_attn, n_expert, sub_cols)...]
    all_to_all x1, waiting for transfers between devices: 15.3 us -> 12.1 us  [per_device(): lax.all_to_all(outgoing, 'attn', split_axis=0, concat_axis=0, tiled=True)]
    all_to_all x1, waiting for transfers between devices: 19.8 us -> 18.1 us  [per_device(): lax.all_to_all(back.reshape((n_dev,) + pack), ('expert', 'attn'), split_a...]
    unnamed x25 -> x23, local copies, waits for them, and re-layouts: 12.5 us -> 12.5 us
  transfers between devices with their start and end apart: 6 -> 6, of which waited for: 6 -> 6; matrix products, arithmetic and copies ran while one was open for 8% -> 12% of each run, Pallas kernels for 0% -> 0%
where the time goes in v8:
time: 166 us; the launch traced here: 165 us
  waiting for transfers between devices  74.5 us (45%)
  starting transfers between devices  37.2 us (22%)
  local copies, waits for them, and re-layouts  25.2 us (15%)
  matrix products  17.6 us (11%)
  other arithmetic  9.7 us (6%)
    all_to_all x1, waiting for transfers between devices, per_device(): lax.all_to_all(spread, 'attn', split_axis=0, concat_axis=0, tiled=True)  28 us
    all_to_all x1, waiting for transfers between devices, per_device(): lax.all_to_all(back.reshape((n_dev,) + pack), ('expert', 'attn'), split_a...  18.1 us
    unnamed x23, local copies, waits for them, and re-layouts  12.5 us
    all_to_all x1, waiting for transfers between devices, per_device(): lax.all_to_all(outgoing, 'attn', split_axis=0, concat_axis=0, tiled=True)  12.1 us
    all_to_all x1, starting transfers between devices, per_device(): lax.all_to_all(outgoing, 'attn', split_axis=0, concat_axis=0, tiled=True)  11.5 us
    all_to_all x1, waiting for transfers between devices, per_device(): lax.all_to_all(send_rows, ('attn', 'expert'), split_axis=0, concat_axis=0...  10.9 us
    all_to_all x1, starting transfers between devices, per_device(): lax.all_to_all(send_rows, ('attn', 'expert'), split_axis=0, concat_axis=0...  9.02 us
    dot_general x1, matrix products, per_device(): jnp.einsum('ku,duc->dkc', activated, down_blocks, preferred_element_type=...  6.95 us
  transfers between devices with their start and end apart: 6, of which 6 were waited for; matrix products, arithmetic and copies ran while one was open for 12% of the time, Pallas kernels for 0%

profile of v8, /device:TPU:2, one launch (start us, length us, event | category | flops | bytes accessed | tf_op | source)
XLA Modules:
  0.0 164.6 jit_solution(5870240519556073843)
XLA Ops:
  1.1 1.4 fusion.10
  3.6 11.5 %all-to-all-start = ((bf16[32,1,16,576]{3,2,1,0:T(8,128)(2,1)}), bf16[32,1,16,576]{3,2,1,0:T(8,128)(2,1)S(1)}, u32[]{:S(2)}, u32[]{:S(2)}) async-start(bf16[32,1,16,576]{3,2,1,0:T(8,128)(2,1)} %copy.72), calls=%async_computation | async-start | bytes 1310720 | tf_op jit(solution)/shard_map/all_to_all | solution.py:73
  17.5 1.1 reshape.385
  21.0 1.2 bitcast_subtract_fusion
  23.2 12.1 %all-to-all-done = bf16[32,1,16,576]{3,2,1,0:T(8,128)(2,1)S(1)} async-done(((bf16[32,1,16,576]{3,2,1,0:T(8,128)(2,1)}), bf16[32,1,16,576]{3,2,1,0:T(8,128)(2,1)S(1)}, u32[]{:S(2)}, u32[]{:S(2)}) %all-to-all-start) | async-done | bytes 589856 | tf_op jit(solution)/shard_map/all_to_all | solution.py:73
  40.1 1.1 broadcast_in_dim.100
  41.2 5.0 %all-to-all-start.1 = ((bf16[32,8,2048]{2,1,0:T(8,128)(2,1)}), bf16[32,8,2048]{2,1,0:T(8,128)(2,1)S(1)}, u32[]{:S(2)}, u32[]{:S(2)}) async-start(bf16[32,8,2048]{2,1,0:T(8,128)(2,1)} %broadcast_in_dim.100), calls=%async_computation.1 | async-start | bytes 2097152 | tf_op jit(solution)/shard_map/all_to_all | solution.py:154
  46.5 28.0 %all-to-all-done.1 = bf16[32,8,2048]{2,1,0:T(8,128)(2,1)S(1)} async-done(((bf16[32,8,2048]{2,1,0:T(8,128)(2,1)}), bf16[32,8,2048]{2,1,0:T(8,128)(2,1)S(1)}, u32[]{:S(2)}, u32[]{:S(2)}) %all-to-all-start.1) | async-done | bytes 1048608 | tf_op jit(solution)/shard_map/all_to_all | solution.py:154
  74.6 1.7 %convolution_convert_fusion.2 = bf16[256,224]{0,1:T(8,128)(2,1)S(1)} fusion(bf16[2048,224]{0,1:T(8,128)(2,1)} %param.22, bf16[32,8,2048]{2,1,0:T(8,128)(2,1)S(1)} %all-to-all-done.1), kind=kOutput, calls=%fused_computation.24 | convolution fusion | flops 234938368 | bytes 2080768 | tf_op jit(solution)/shard_map/dot_general | solution.py:156
  76.9 4.8 %all-to-all-start.2 = ((bf16[8,128,56]{1,2,0:T(8,128)(2,1)}), bf16[8,128,56]{1,2,0:T(8,128)(2,1)S(1)}, u32[]{:S(2)}, u32[]{:S(2)}) async-start(bf16[8,128,56]{1,2,0:T(8,128)(2,1)} %bitcast.25), calls=%async_computation.2 | async-start | bytes 229376 | tf_op jit(solution)/shard_map/all_to_all | solution.py:167
  81.8 4.4 %all-to-all-done.2 = bf16[8,128,56]{1,2,0:T(8,128)(2,1)S(1)} async-done(((bf16[8,128,56]{1,2,0:T(8,128)(2,1)}), bf16[8,128,56]{1,2,0:T(8,128)(2,1)S(1)}, u32[]{:S(2)}, u32[]{:S(2)}) %all-to-all-start.2) | async-done | bytes 114720 | tf_op jit(solution)/shard_map/all_to_all | solution.py:167
  87.4 3.1 %reshape.415 = bf16[128,2,1120]{2,1,0:T(2,128)(2,1)} reshape(bf16[128,40,56]{2,1,0:T(8,128)(2,1)S(1)} %bitcast.131) | data formatting | bytes 1146880
  90.5 9.0 %all-to-all-start.3 = ((bf16[128,2,1120]{2,1,0:T(2,128)(2,1)}), bf16[128,2,1120]{2,1,0:T(2,128)(2,1)}, u32[]{:S(2)}, u32[]{:S(2)}) async-start(bf16[128,2,1120]{2,1,0:T(2,128)(2,1)} %reshape.415), calls=%async_computation.3 | async-start | bytes 1179648 | tf_op jit(solution)/shard_map/all_to_all | solution.py:182
  99.5 5.9 %copy.80 = bf16[256,7168]{0,1:T(8,128)(2,1)} copy(bf16[256,7168]{1,0:T(8,128)(2,1)} %param.29) | data formatting | bytes 7340032 | tf_op args[14]
  105.5 4.1 %copy.81 = bf16[4,32,256,56]{2,3,1,0:T(8,128)(2,1)} copy(bf16[4,32,256,56]{2,3,0,1:T(8,128)(2,1)} %bitcast.129) | data formatting | bytes 7340032 | tf_op jit(solution)/shard_map/transpose | solution.py:199
  109.6 10.9 %all-to-all-done.3 = bf16[128,2,1120]{2,1,0:T(2,128)(2,1)} async-done(((bf16[128,2,1120]{2,1,0:T(2,128)(2,1)}), bf16[128,2,1120]{2,1,0:T(2,128)(2,1)}, u32[]{:S(2)}, u32[]{:S(2)}) %all-to-all-start.3) | async-done | bytes 573472 | tf_op jit(solution)/shard_map/all_to_all | solution.py:182
  120.6 3.3 %reshape.416 = bf16[128,40,56]{2,1,0:T(8,128)(2,1)S(1)} reshape(bf16[128,2,1120]{2,1,0:T(2,128)(2,1)} %all-to-all-done.3) | data formatting | bytes 1146880
  124.4 3.0 %convolution_bitcast_fusion.1 = f32[40,256]{1,0:T(8,128)S(1)} fusion(bf16[128,56,256]{2,1,0:T(8,128)(2,1)} %bitcast.157, bf16[128,40,56]{2,1,0:T(8,128)(2,1)S(1)} %reshape.416, f32[128,56]{1,0:T(8,128)S(1)} %mul.98, f32[40]{0:T(128)S(1)} %add_rsqrt_fusion), kind=kOutput, calls=%fused_computation.28 | convolution fusion | flops 147947520 | bytes 4313248 | tf_op jit(solution)/shard_map/skc,scu->ku/dot_general | solution.py:192
  127.4 7.0 %fusion.11 = bf16[128,40,56]{0,1,2:T(8,128)(2,1)} fusion(bf16[128,256,56]{1,2,0:T(8,128)(2,1)} %bitcast.130, bf16[128,56,256]{2,1,0:T(8,128)(2,1)} %bitcast.132, bf16[128,40,56]{2,1,0:T(8,128)(2,1)S(1)} %reshape.416, f32[128,56]{1,0:T(8,128)S(1)} %mul.98, f32[40]{0:T(128)S(1)} %add_rsqrt_fusion, f32[40,256]{1,0:T(8,128)S(1)} %convolution_bitcast_fusion.1), kind=kOutput, calls=%fused_computation.12 | convolution fusion | flops 295096320 | bytes 8556704 | tf_op jit(solution)/shard_map/ku,duc->dkc/dot_general | solution.py:202
  134.3 1.1 copy.83
  135.5 2.0 %copy.84 = bf16[128,2,1120]{2,1,0:T(2,128)(2,1)} copy(bf16[128,2,1120]{0,2,1:T(8,128)(2,1)S(1)} %bitcast.134) | data formatting | bytes 1146880 | tf_op jit(solution)/shard_map/reshape | solution.py:207
  137.4 6.8 %all-to-all-start.4 = ((bf16[128,2,1120]{2,1,0:T(2,128)(2,1)}), bf16[128,2,1120]{2,1,0:T(2,128)(2,1)S(1)}, u32[]{:S(2)}, u32[]{:S(2)}) async-start(bf16[128,2,1120]{2,1,0:T(2,128)(2,1)} %copy.84), calls=%async_computation.4 | async-start | bytes 1179648 | tf_op jit(solution)/shard_map/all_to_all | solution.py:206
  144.6 18.1 %all-to-all-done.4 = bf16[128,2,1120]{2,1,0:T(2,128)(2,1)S(1)} async-done(((bf16[128,2,1120]{2,1,0:T(2,128)(2,1)}), bf16[128,2,1120]{2,1,0:T(2,128)(2,1)S(1)}, u32[]{:S(2)}, u32[]{:S(2)}) %all-to-all-start.4) | async-done | bytes 573472 | tf_op jit(solution)/shard_map/all_to_all | solution.py:206
  163.4 1.2 fusion.29
  (83 shorter events, 16.3 us)
Async XLA Ops:
  0.0 39.6 %copy-start = (bf16[16,512,128]{2,1,0:T(8,128)(2,1)S(1)}, bf16[16,512,128]{2,1,0:T(8,128)(2,1)}, u32[]{:S(2)}) copy-start(bf16[16,512,128]{2,1,0:T(8,128)(2,1)} %param.21) | copy-start | bytes 6291460
  0.0 15.1 %copy-start.4 = (s32[1024]{0:T(1024)S(1)}, s32[1024]{0:T(1024)}, u32[]{:S(2)}) copy-start(s32[1024]{0:T(1024)} %param.20) | copy-start | bytes 12292
  1.1 21.1 %copy-start.3 = (bf16[8,576]{1,0:T(8,128)(2,1)S(1)}, bf16[8,576]{1,0:T(8,128)(2,1)}, u32[]{:S(2)}) copy-start(bf16[8,576]{1,0:T(8,128)(2,1)} %param.16) | copy-start | bytes 27652
  2.6 33.5 %copy-start.1 = (bf16[512,576]{0,1:T(8,128)(2,1)S(1)}, bf16[512,576]{0,1:T(8,128)(2,1)}, u32[]{:S(2)}) copy-start(bf16[512,576]{0,1:T(8,128)(2,1)} %param.17) | copy-start | bytes 1769476
  3.6 31.7 %all-to-all-start = ((bf16[32,1,16,576]{3,2,1,0:T(8,128)(2,1)}), bf16[32,1,16,576]{3,2,1,0:T(8,128)(2,1)S(1)}, u32[]{:S(2)}, u32[]{:S(2)}) async-start(bf16[32,1,16,576]{3,2,1,0:T(8,128)(2,1)} %copy.72), calls=%async_computation | async-start | bytes 1310720 | tf_op jit(solution)/shard_map/all_to_all | solution.py:73
  19.6 2.6 %copy-start.8 = (s32[4,1]{0,1:T(1,128)}, s32[4,1]{0,1:T(1,128)S(1)}, u32[]{:S(2)}) copy-start(s32[4,1]{0,1:T(1,128)S(1)} %reduce-window.7) | copy-start | bytes 52
  35.3 2.1 %collective-permute-start = (bf16[32,1,16,576]{3,2,1,0:T(8,128)(2,1)S(1)}, bf16[32,1,16,576]{3,2,1,0:T(8,128)(2,1)S(1)}, u32[]{:S(2)}, u32[]{:S(2)}) collective-permute-start(bf16[32,1,16,576]{3,2,1,0:T(8,128)(2,1)S(1)} %all-to-all-done), channel_id=1, source_target_pairs={{0,1},{1,0},{2,3},{3,2},{4,5},{5,4},{6,7},{7,6},{8,9},{9,8},{10,11... | collective-permute-start | bytes 1769480 | tf_op jit(solution)/shard_map/ppermute | solution.py:74
  37.5 0.7 copy-start.6
  40.0 6.2 %copy-start.7 = (s32[256,4]{0,1:T(4,128)S(1)}, s32[256,4]{0,1:T(4,128)}, u32[]{:S(2)}) copy-start(s32[256,4]{0,1:T(4,128)} %param.25) | copy-start | bytes 12292
  41.2 33.4 %all-to-all-start.1 = ((bf16[32,8,2048]{2,1,0:T(8,128)(2,1)}), bf16[32,8,2048]{2,1,0:T(8,128)(2,1)S(1)}, u32[]{:S(2)}, u32[]{:S(2)}) async-start(bf16[32,8,2048]{2,1,0:T(8,128)(2,1)} %broadcast_in_dim.100), calls=%async_computation.1 | async-start | bytes 2097152 | tf_op jit(solution)/shard_map/all_to_all | solution.py:154
  76.9 9.3 %all-to-all-start.2 = ((bf16[8,128,56]{1,2,0:T(8,128)(2,1)}), bf16[8,128,56]{1,2,0:T(8,128)(2,1)S(1)}, u32[]{:S(2)}, u32[]{:S(2)}) async-start(bf16[8,128,56]{1,2,0:T(8,128)(2,1)} %bitcast.25), calls=%async_computation.2 | async-start | bytes 229376 | tf_op jit(solution)/shard_map/all_to_all | solution.py:167
  90.5 30.1 %all-to-all-start.3 = ((bf16[128,2,1120]{2,1,0:T(2,128)(2,1)}), bf16[128,2,1120]{2,1,0:T(2,128)(2,1)}, u32[]{:S(2)}, u32[]{:S(2)}) async-start(bf16[128,2,1120]{2,1,0:T(2,128)(2,1)} %reshape.415), calls=%async_computation.3 | async-start | bytes 1179648 | tf_op jit(solution)/shard_map/all_to_all | solution.py:182
  105.5 4.1 %copy-start.2 = (f32[7168]{0:T(1024)S(1)}, f32[7168]{0:T(1024)}, u32[]{:S(2)}) copy-start(f32[7168]{0:T(1024)} %param.24) | copy-start | bytes 86020
  134.3 10.0 %copy-start.5 = (f32[256,4]{0,1:T(4,128)S(1)}, f32[256,4]{0,1:T(4,128)}, u32[]{:S(2)}) copy-start(f32[256,4]{0,1:T(4,128)} %param.26) | copy-start | bytes 12292
  137.4 25.2 %all-to-all-start.4 = ((bf16[128,2,1120]{2,1,0:T(2,128)(2,1)}), bf16[128,2,1120]{2,1,0:T(2,128)(2,1)S(1)}, u32[]{:S(2)}, u32[]{:S(2)}) async-start(bf16[128,2,1120]{2,1,0:T(2,128)(2,1)} %copy.84), calls=%async_computation.4 | async-start | bytes 1179648 | tf_op jit(solution)/shard_map/all_to_all | solution.py:206

commit v9 on v8

--- a/solution.py
+++ b/solution.py
@@ -178,22 +178,23 @@
     rows_e = jnp.einsum(
         "jsr,rc->jsc", pick.astype(jnp.bfloat16), hidden_own, preferred_element_type=jnp.float32
     ).astype(jnp.bfloat16)
-    send_rows = jnp.repeat(rows_e, shards, axis=0)
-    recv_rows = lax.all_to_all(send_rows, ("attn", "expert"), split_axis=0, concat_axis=0, tiled=True)
+    per_attn = shards // n_expert
+    send_rows = jnp.broadcast_to(
+        rows_e[None, :, None], (n_expert, EXPERTS, per_attn) + rows_e.shape[1:]
+    ).reshape((-1,) + rows_e.shape[1:])
+    recv_rows = lax.all_to_all(send_rows, ("expert", "attn"), split_axis=0, concat_axis=0, tiled=True)
     n_src = recv_rows.shape[0]
-    widened = recv_rows.astype(jnp.float32)
-    mean_sq = jnp.sum(widened * widened, axis=(0, 2)) / (n_src * sub_cols)
+    widened = recv_rows.astype(jnp.float32).reshape(n_expert, n_attn, capacity, sub_cols)
+    mean_sq = jnp.sum(widened * widened, axis=(0, 1, 3)) / (n_src * sub_cols)
     inv = lax.rsqrt(mean_sq + 1e-06)
-    normed = (
-        widened * inv[None, :, None] * norm_gain.reshape(n_src, 1, sub_cols)
-    ).astype(jnp.bfloat16)
-    gate_blocks = w_gate.reshape(n_src, sub_cols, w_gate.shape[1])
-    up_blocks = w_up.reshape(n_src, sub_cols, w_up.shape[1])
-    gate_proj = jnp.einsum("skc,scu->ku", normed, gate_blocks, preferred_element_type=jnp.float32)
-    up_proj = jnp.einsum("skc,scu->ku", normed, up_blocks, preferred_element_type=jnp.float32)
+    gain = norm_gain.reshape(n_attn, n_expert, sub_cols).swapaxes(0, 1)[:, :, None, :]
+    normed = (widened * inv[None, None, :, None] * gain).astype(jnp.bfloat16)
+    gate_blocks = w_gate.reshape(n_attn, n_expert, sub_cols, w_gate.shape[1])
+    up_blocks = w_up.reshape(n_attn, n_expert, sub_cols, w_up.shape[1])
+    gate_proj = jnp.einsum("eakc,aecu->ku", normed, gate_blocks, preferred_element_type=jnp.float32)
+    up_proj = jnp.einsum("eakc,aecu->ku", normed, up_blocks, preferred_element_type=jnp.float32)
     activated = (jax.nn.silu(gate_proj) * up_proj).astype(jnp.bfloat16)
     n_dev = n_attn * n_expert
-    per_attn = shards // n_expert
     down_blocks = (
         w_down.reshape(w_down.shape[0], n_attn, n_expert, sub_cols)
         .transpose(2, 1, 0, 3)

time: 166 us -> 165 us (level)
  waiting for transfers between devices: 74.5 us -> 72.6 us
    all_to_all x1, waiting for transfers between devices: 10.9 us -> 8.9 us  [per_device(): lax.all_to_all(send_rows, ('expert', 'attn'), split_axis=0, concat_axis=0...]
where the time goes in v9:
time: 165 us; the launch traced here: 164 us
  waiting for transfers between devices  72.6 us (44%)
  starting transfers between devices  38.5 us (23%)
  local copies, waits for them, and re-layouts  25.2 us (15%)
  matrix products  17.8 us (11%)
  other arithmetic  9.7 us (6%)
    all_to_all x1, waiting for transfers between devices, per_device(): lax.all_to_all(spread, 'attn', split_axis=0, concat_axis=0, tiled=True)  28 us
    all_to_all x1, waiting for transfers between devices, per_device(): lax.all_to_all(back.reshape((n_dev,) + pack), ('expert', 'attn'), split_a...  18.2 us
    unnamed x23, local copies, waits for them, and re-layouts  12.5 us
    all_to_all x1, waiting for transfers between devices, per_device(): lax.all_to_all(outgoing, 'attn', split_axis=0, concat_axis=0, tiled=True)  12.1 us
    all_to_all x1, starting transfers between devices, per_device(): lax.all_to_all(outgoing, 'attn', split_axis=0, concat_axis=0, tiled=True)  11.5 us
    all_to_all x1, starting transfers between devices, per_device(): lax.all_to_all(send_rows, ('expert', 'attn'), split_axis=0, concat_axis=0...  9.12 us
    all_to_all x1, waiting for transfers between devices, per_device(): lax.all_to_all(send_rows, ('expert', 'attn'), split_axis=0, concat_axis=0...  8.9 us
    all_to_all x1, starting transfers between devices, per_device(): lax.all_to_all(back.reshape((n_dev,) + pack), ('expert', 'attn'), split_a...  8.11 us
  transfers between devices with their start and end apart: 6, of which 6 were waited for; matrix products, arithmetic and copies ran while one was open for 12% of the time, Pallas kernels for 0%

profile of v9, /device:TPU:2, one launch (start us, length us, event | category | flops | bytes accessed | tf_op | source)
XLA Modules:
  0.0 164.3 jit_solution(3697407639209357868)
XLA Ops:
  1.1 1.4 fusion.7
  3.6 11.5 %all-to-all-start = ((bf16[32,1,16,576]{3,2,1,0:T(8,128)(2,1)}), bf16[32,1,16,576]{3,2,1,0:T(8,128)(2,1)S(1)}, u32[]{:S(2)}, u32[]{:S(2)}) async-start(bf16[32,1,16,576]{3,2,1,0:T(8,128)(2,1)} %copy.75), calls=%async_computation | async-start | bytes 1310720 | tf_op jit(solution)/shard_map/all_to_all | solution.py:73
  17.5 1.1 reshape.391
  21.0 1.2 bitcast_subtract_fusion
  23.2 12.1 %all-to-all-done = bf16[32,1,16,576]{3,2,1,0:T(8,128)(2,1)S(1)} async-done(((bf16[32,1,16,576]{3,2,1,0:T(8,128)(2,1)}), bf16[32,1,16,576]{3,2,1,0:T(8,128)(2,1)S(1)}, u32[]{:S(2)}, u32[]{:S(2)}) %all-to-all-start) | async-done | bytes 589856 | tf_op jit(solution)/shard_map/all_to_all | solution.py:73
  40.1 1.1 broadcast_in_dim.96
  41.2 5.0 %all-to-all-start.1 = ((bf16[32,8,2048]{2,1,0:T(8,128)(2,1)}), bf16[32,8,2048]{2,1,0:T(8,128)(2,1)S(1)}, u32[]{:S(2)}, u32[]{:S(2)}) async-start(bf16[32,8,2048]{2,1,0:T(8,128)(2,1)} %broadcast_in_dim.96), calls=%async_computation.1 | async-start | bytes 2097152 | tf_op jit(solution)/shard_map/all_to_all | solution.py:154
  46.5 28.0 %all-to-all-done.1 = bf16[32,8,2048]{2,1,0:T(8,128)(2,1)S(1)} async-done(((bf16[32,8,2048]{2,1,0:T(8,128)(2,1)}), bf16[32,8,2048]{2,1,0:T(8,128)(2,1)S(1)}, u32[]{:S(2)}, u32[]{:S(2)}) %all-to-all-start.1) | async-done | bytes 1048608 | tf_op jit(solution)/shard_map/all_to_all | solution.py:154
  74.6 1.7 %convolution_convert_fusion.2 = bf16[256,224]{0,1:T(8,128)(2,1)S(1)} fusion(bf16[2048,224]{0,1:T(8,128)(2,1)} %param.22, bf16[32,8,2048]{2,1,0:T(8,128)(2,1)S(1)} %all-to-all-done.1), kind=kOutput, calls=%fused_computation.25 | convolution fusion | flops 234938368 | bytes 2080768 | tf_op jit(solution)/shard_map/dot_general | solution.py:156
  76.9 4.8 %all-to-all-start.2 = ((bf16[8,128,56]{1,2,0:T(8,128)(2,1)}), bf16[8,128,56]{1,2,0:T(8,128)(2,1)S(1)}, u32[]{:S(2)}, u32[]{:S(2)}) async-start(bf16[8,128,56]{1,2,0:T(8,128)(2,1)} %bitcast.25), calls=%async_computation.2 | async-start | bytes 229376 | tf_op jit(solution)/shard_map/all_to_all | solution.py:167
  81.8 4.4 %all-to-all-done.2 = bf16[8,128,56]{1,2,0:T(8,128)(2,1)S(1)} async-done(((bf16[8,128,56]{1,2,0:T(8,128)(2,1)}), bf16[8,128,56]{1,2,0:T(8,128)(2,1)S(1)}, u32[]{:S(2)}, u32[]{:S(2)}) %all-to-all-start.2) | async-done | bytes 114720 | tf_op jit(solution)/shard_map/all_to_all | solution.py:167
  87.4 3.1 %reshape.423 = bf16[128,2,1120]{2,1,0:T(2,128)(2,1)} reshape(bf16[128,40,56]{2,1,0:T(8,128)(2,1)S(1)} %bitcast.139) | data formatting | bytes 1146880
  90.5 9.1 %all-to-all-start.3 = ((bf16[128,2,1120]{2,1,0:T(2,128)(2,1)}), bf16[128,2,1120]{2,1,0:T(2,128)(2,1)}, u32[]{:S(2)}, u32[]{:S(2)}) async-start(bf16[128,2,1120]{2,1,0:T(2,128)(2,1)} %reshape.423), calls=%async_computation.3 | async-start | bytes 1179648 | tf_op jit(solution)/shard_map/all_to_all | solution.py:185
  99.6 5.9 %copy.86 = bf16[256,7168]{0,1:T(8,128)(2,1)} copy(bf16[256,7168]{1,0:T(8,128)(2,1)} %param.29) | data formatting | bytes 7340032 | tf_op args[14]
  105.6 4.1 %copy.87 = bf16[4,32,256,56]{2,3,1,0:T(8,128)(2,1)} copy(bf16[4,32,256,56]{2,3,0,1:T(8,128)(2,1)} %bitcast.136) | data formatting | bytes 7340032 | tf_op jit(solution)/shard_map/transpose | solution.py:200
  109.8 8.9 %all-to-all-done.3 = bf16[128,2,1120]{2,1,0:T(2,128)(2,1)} async-done(((bf16[128,2,1120]{2,1,0:T(2,128)(2,1)}), bf16[128,2,1120]{2,1,0:T(2,128)(2,1)}, u32[]{:S(2)}, u32[]{:S(2)}) %all-to-all-start.3) | async-done | bytes 573472 | tf_op jit(solution)/shard_map/all_to_all | solution.py:185
  118.7 3.3 %reshape.424 = bf16[128,40,56]{2,1,0:T(8,128)(2,1)S(1)} reshape(bf16[128,2,1120]{2,1,0:T(2,128)(2,1)} %all-to-all-done.3) | data formatting | bytes 1146880
  122.6 3.1 %fusion.23 = f32[40,256]{1,0:T(8,128)S(1)} fusion(bf16[32,4,56,256]{3,2,1,0:T(8,128)(2,1)} %bitcast.166, f32[4,32,56]{2,1,0:T(8,128)S(1)} %copy.83, f32[40]{0:T(128)S(1)} %add_rsqrt_fusion, bf16[4,32,40,56]{3,2,1,0:T(8,128)(2,1)S(1)} %bitcast.137), kind=kOutput, calls=%fused_computation.27 | convolution fusion | flops 147947520 | bytes 4313248 | tf_op jit(solution)/shard_map/eakc,aecu->ku/dot_general | solution.py:194
  125.7 7.0 %fusion.8 = bf16[128,40,56]{0,1,2:T(8,128)(2,1)} fusion(bf16[128,256,56]{1,2,0:T(8,128)(2,1)} %bitcast.140, bf16[32,4,56,256]{3,2,1,0:T(8,128)(2,1)} %bitcast.167, f32[40,256]{1,0:T(8,128)S(1)} %fusion.23, f32[4,32,56]{2,1,0:T(8,128)S(1)} %copy.83, f32[40]{0:T(128)S(1)} %add_rsqrt_fusion, bf16[4,32,40,56]{3,2,1,0:T(8,128)(2,1)S(1)} %bitcast.138), kind=kOutput, calls=%fused_computation.9 | convolution fusion | flops 295096320 | bytes 8556704 | tf_op jit(solution)/shard_map/ku,duc->dkc/dot_general | solution.py:203
  132.6 1.1 copy.89
  133.8 2.0 %copy.90 = bf16[128,2,1120]{2,1,0:T(2,128)(2,1)} copy(bf16[128,2,1120]{0,2,1:T(8,128)(2,1)S(1)} %bitcast.142) | data formatting | bytes 1146880 | tf_op jit(solution)/shard_map/reshape | solution.py:208
  135.8 8.1 %all-to-all-start.4 = ((bf16[128,2,1120]{2,1,0:T(2,128)(2,1)}), bf16[128,2,1120]{2,1,0:T(2,128)(2,1)S(1)}, u32[]{:S(2)}, u32[]{:S(2)}) async-start(bf16[128,2,1120]{2,1,0:T(2,128)(2,1)} %copy.90), calls=%async_computation.4 | async-start | bytes 1179648 | tf_op jit(solution)/shard_map/all_to_all | solution.py:207
  144.1 18.2 %all-to-all-done.4 = bf16[128,2,1120]{2,1,0:T(2,128)(2,1)S(1)} async-done(((bf16[128,2,1120]{2,1,0:T(2,128)(2,1)}), bf16[128,2,1120]{2,1,0:T(2,128)(2,1)S(1)}, u32[]{:S(2)}, u32[]{:S(2)}) %all-to-all-start.4) | async-done | bytes 573472 | tf_op jit(solution)/shard_map/all_to_all | solution.py:207
  163.1 1.2 fusion.40
  (84 shorter events, 16.3 us)
Async XLA Ops:
  0.0 39.6 %copy-start = (bf16[16,512,128]{2,1,0:T(8,128)(2,1)S(1)}, bf16[16,512,128]{2,1,0:T(8,128)(2,1)}, u32[]{:S(2)}) copy-start(bf16[16,512,128]{2,1,0:T(8,128)(2,1)} %param.21) | copy-start | bytes 6291460
  0.0 15.1 %copy-start.4 = (s32[1024]{0:T(1024)S(1)}, s32[1024]{0:T(1024)}, u32[]{:S(2)}) copy-start(s32[1024]{0:T(1024)} %param.20) | copy-start | bytes 12292
  1.1 21.1 %copy-start.3 = (bf16[8,576]{1,0:T(8,128)(2,1)S(1)}, bf16[8,576]{1,0:T(8,128)(2,1)}, u32[]{:S(2)}) copy-start(bf16[8,576]{1,0:T(8,128)(2,1)} %param.16) | copy-start | bytes 27652
  2.6 33.5 %copy-start.1 = (bf16[512,576]{0,1:T(8,128)(2,1)S(1)}, bf16[512,576]{0,1:T(8,128)(2,1)}, u32[]{:S(2)}) copy-start(bf16[512,576]{0,1:T(8,128)(2,1)} %param.17) | copy-start | bytes 1769476
  3.6 31.7 %all-to-all-start = ((bf16[32,1,16,576]{3,2,1,0:T(8,128)(2,1)}), bf16[32,1,16,576]{3,2,1,0:T(8,128)(2,1)S(1)}, u32[]{:S(2)}, u32[]{:S(2)}) async-start(bf16[32,1,16,576]{3,2,1,0:T(8,128)(2,1)} %copy.75), calls=%async_computation | async-start | bytes 1310720 | tf_op jit(solution)/shard_map/all_to_all | solution.py:73
  19.6 2.6 %copy-start.8 = (s32[4,1]{0,1:T(1,128)}, s32[4,1]{0,1:T(1,128)S(1)}, u32[]{:S(2)}) copy-start(s32[4,1]{0,1:T(1,128)S(1)} %reduce-window.7) | copy-start | bytes 52
  35.3 2.1 %collective-permute-start = (bf16[32,1,16,576]{3,2,1,0:T(8,128)(2,1)S(1)}, bf16[32,1,16,576]{3,2,1,0:T(8,128)(2,1)S(1)}, u32[]{:S(2)}, u32[]{:S(2)}) collective-permute-start(bf16[32,1,16,576]{3,2,1,0:T(8,128)(2,1)S(1)} %all-to-all-done), channel_id=1, source_target_pairs={{0,1},{1,0},{2,3},{3,2},{4,5},{5,4},{6,7},{7,6},{8,9},{9,8},{10,11... | collective-permute-start | bytes 1769480 | tf_op jit(solution)/shard_map/ppermute | solution.py:74
  37.5 0.7 copy-start.6
  40.0 6.2 %copy-start.7 = (s32[256,4]{0,1:T(4,128)S(1)}, s32[256,4]{0,1:T(4,128)}, u32[]{:S(2)}) copy-start(s32[256,4]{0,1:T(4,128)} %param.25) | copy-start | bytes 12292
  41.2 33.4 %all-to-all-start.1 = ((bf16[32,8,2048]{2,1,0:T(8,128)(2,1)}), bf16[32,8,2048]{2,1,0:T(8,128)(2,1)S(1)}, u32[]{:S(2)}, u32[]{:S(2)}) async-start(bf16[32,8,2048]{2,1,0:T(8,128)(2,1)} %broadcast_in_dim.96), calls=%async_computation.1 | async-start | bytes 2097152 | tf_op jit(solution)/shard_map/all_to_all | solution.py:154
  76.9 9.3 %all-to-all-start.2 = ((bf16[8,128,56]{1,2,0:T(8,128)(2,1)}), bf16[8,128,56]{1,2,0:T(8,128)(2,1)S(1)}, u32[]{:S(2)}, u32[]{:S(2)}) async-start(bf16[8,128,56]{1,2,0:T(8,128)(2,1)} %bitcast.25), calls=%async_computation.2 | async-start | bytes 229376 | tf_op jit(solution)/shard_map/all_to_all | solution.py:167
  90.5 28.2 %all-to-all-start.3 = ((bf16[128,2,1120]{2,1,0:T(2,128)(2,1)}), bf16[128,2,1120]{2,1,0:T(2,128)(2,1)}, u32[]{:S(2)}, u32[]{:S(2)}) async-start(bf16[128,2,1120]{2,1,0:T(2,128)(2,1)} %reshape.423), calls=%async_computation.3 | async-start | bytes 1179648 | tf_op jit(solution)/shard_map/all_to_all | solution.py:185
  105.6 4.1 %copy-start.2 = (f32[7168]{0:T(1024)S(1)}, f32[7168]{0:T(1024)}, u32[]{:S(2)}) copy-start(f32[7168]{0:T(1024)} %param.24) | copy-start | bytes 86020
  132.6 11.2 %copy-start.5 = (f32[256,4]{0,1:T(4,128)S(1)}, f32[256,4]{0,1:T(4,128)}, u32[]{:S(2)}) copy-start(f32[256,4]{0,1:T(4,128)} %param.26) | copy-start | bytes 12292
  135.8 26.5 %all-to-all-start.4 = ((bf16[128,2,1120]{2,1,0:T(2,128)(2,1)}), bf16[128,2,1120]{2,1,0:T(2,128)(2,1)S(1)}, u32[]{:S(2)}, u32[]{:S(2)}) async-start(bf16[128,2,1120]{2,1,0:T(2,128)(2,1)} %copy.90), calls=%async_computation.4 | async-start | bytes 1179648 | tf_op jit(solution)/shard_map/all_to_all | solution.py:207
